TPU v7x, 512 devices: a whole 4x8x8 slice. The times are simulated.
512 devices in a mesh: shot: 32 (over z, y_hi), dom: 16 (over x, y_lo, core).
Axes of the slice: x: 4, y: 8 (y_hi: 4, y_lo: 2; y = y_hi * 2 + y_lo), z: 8, core: 2. Of those that a mesh axis runs over, the one named last changes fastest.
Arguments:
- coefficient: float32 [512, 16, 384], P('dom'), may hold values from 0.02 to 0.18
- fwd_older: float32 [32, 512, 16, 384], P('shot', 'dom'), may hold values from -6 to 6
- fwd_recent: float32 [32, 512, 16, 384], P('shot', 'dom'), may hold values from -6 to 6
- adj_later: float32 [32, 512, 16, 384], P('shot', 'dom'), may hold values from -6 to 6
- adj_recent: float32 [32, 512, 16, 384], P('shot', 'dom'), may hold values from -6 to 6
- source_xcell: int32 [32], P('shot'), may hold values from 0 to 511
- source_ycell: int32 [32], P('shot'), may hold values from 0 to 15
- source_zcell: int32 [32], P('shot'), may hold values from 0 to 383
- amplitude: float32 [32, 2], P('shot'), may hold values from 3547.24 to 7094.48
- receiver_xcell: int32 [32, 1024], P('shot'), may hold values from 0 to 511
- receiver_ycell: int32 [32, 1024], P('shot'), may hold values from 0 to 15
- receiver_zcell: int32 [32, 1024], P('shot'), may hold values from 0 to 383
- observed: float32 [32, 2, 1024], P('shot'), may hold values from -6 to 6
Outputs:
- fwd_latest: float32 [32, 512, 16, 384], P('shot', 'dom')
- adj_latest: float32 [32, 512, 16, 384], P('shot', 'dom')
- model_gradient: float32 [512, 16, 384], P('dom')
All inputs are finite; a program needn't handle non-finite values.
Results may differ from a plain program's by a relative error of at most 0.0003.
Values sent between devices are 32-bit elements; how exact they have to be, the bound alone decides.
No kernel may reach another device: no remote copies, remote signals or barrier semaphores. Data moves between devices by JAX's collectives and lax.ppermute only.
A program may use at most 64 MiB of HBM per device.

v0:
```python
import jax
import jax.numpy as jnp
from jax import lax
from jax.sharding import PartitionSpec as P

R = 4


stencil_weights = (-205.0 / 72.0, 8.0 / 5.0, -1.0 / 5.0, 8.0 / 315.0, -1.0 / 560.0)


def with_halo(block, sides, width):
    for axis, dim in sides:
        count = lax.axis_size(axis)
        forward = [(i, i + 1) for i in range(count - 1)]
        backward = [(target, source) for source, target in forward]
        low = lax.ppermute(
            lax.slice_in_dim(block, block.shape[dim] - width, None, axis=dim), axis, forward
        )
        high = lax.ppermute(lax.slice_in_dim(block, 0, width, axis=dim), axis, backward)
        block = jnp.concatenate([low, block, high], axis=dim)
    return block


def laplace_core(extended):
    count = extended.shape[0] - 2 * R
    center = extended[R : R + count]
    width_y = center.shape[1]
    width_z = center.shape[2]
    total = 3.0 * stencil_weights[0] * center
    padded = jnp.pad(center, ((0, 0), (R, R), (R, R)))
    for offset in range(1, R + 1):
        weight = stencil_weights[offset]
        total = total + weight * (
            extended[R + offset : R + offset + count] + extended[R - offset : R - offset + count]
        )
        total = total + weight * (
            padded[:, R + offset : R + offset + width_y, R : R + width_z]
            + padded[:, R - offset : R - offset + width_y, R : R + width_z]
        )
        total = total + weight * (
            padded[:, R : R + width_y, R + offset : R + offset + width_z]
            + padded[:, R : R + width_y, R - offset : R - offset + width_z]
        )
    return total


def point_grid(shape, xcells, ycells, zcells, values, start):
    count = shape[0]
    inside = (xcells >= start) & (xcells < start + count)
    local = jnp.clip(xcells - start, 0, count - 1)
    kept = jnp.where(inside, values, jnp.zeros_like(values))
    return jnp.zeros(shape, values.dtype).at[local, ycells, zcells].add(kept)


def sample(field, xcells, ycells, zcells, start):
    count = field.shape[0]
    inside = (xcells >= start) & (xcells < start + count)
    local = jnp.clip(xcells - start, 0, count - 1)
    picked = field[local, ycells, zcells]
    return jnp.where(inside, picked, jnp.zeros_like(picked))


def shards(
    coefficient,
    fwd_older,
    fwd_recent,
    adj_later,
    adj_recent,
    source_xcell,
    source_ycell,
    source_zcell,
    amplitude,
    receiver_xcell,
    receiver_ycell,
    receiver_zcell,
    observed,
):
    count = coefficient.shape[0]
    shape = coefficient.shape
    base = lax.axis_index("dom") * count
    older = fwd_older[0]
    recent = fwd_recent[0]
    later = adj_later[0]
    adj_now = adj_recent[0]
    rxc = receiver_xcell[0]
    ryc = receiver_ycell[0]
    rzc = receiver_zcell[0]

    def advance(current, before, sources):
        extended = with_halo(current, (("dom", 0),), R)
        return 2.0 * current - before + coefficient * (laplace_core(extended) + sources)

    fwd_two = advance(
        recent,
        older,
        point_grid(shape, source_xcell, source_ycell, source_zcell, amplitude[0, 0:1], base),
    )
    fwd_three = advance(
        fwd_two,
        recent,
        point_grid(shape, source_xcell, source_ycell, source_zcell, amplitude[0, 1:2], base),
    )
    samples = jnp.stack(
        [sample(fwd_two, rxc, ryc, rzc, base), sample(fwd_three, rxc, ryc, rzc, base)]
    )
    traces = lax.psum(samples, "dom")
    resid_two = traces[0] - observed[0, 0]
    resid_three = traces[1] - observed[0, 1]
    adj_two = advance(adj_now, later, point_grid(shape, rxc, ryc, rzc, resid_three, base))
    late_term = adj_two * (fwd_three - 2.0 * fwd_two + recent)
    adj_one = advance(adj_two, adj_now, point_grid(shape, rxc, ryc, rzc, resid_two, base))
    early_term = adj_one * (fwd_two - 2.0 * recent + older)
    gradient = lax.psum(early_term + late_term, "shot")
    return (fwd_three[None], adj_one[None], gradient)


def solution(mesh):
    return jax.shard_map(
        shards,
        mesh=mesh,
        in_specs=(
            P("dom", None, None),
            P("shot", "dom", None, None),
            P("shot", "dom", None, None),
            P("shot", "dom", None, None),
            P("shot", "dom", None, None),
            P("shot"),
            P("shot"),
            P("shot"),
            P("shot", None),
            P("shot", None),
            P("shot", None),
            P("shot", None),
            P("shot", None, None),
        ),
        out_specs=(
            P("shot", "dom", None, None),
            P("shot", "dom", None, None),
            P("dom", None, None),
        ),
        check_vma=False,
    )
```

profile of v0, /device:TPU:6, one launch (start us, length us, event | category | flops | bytes accessed | tf_op | source)
XLA Modules:
  0.0 465.7 jit_solution(8528080193020406598)
XLA Ops:
  7.2 0.0 copy-start.14
  7.2 0.0 copy-start.12
  7.2 0.0 copy-start.13
  7.2 0.0 copy-start.1
  7.3 0.0 all-reduce.6.cloned.1.call-start
  7.3 1.7 slice_bitcast_fusion.1
  9.0 3.2 collective-permute-start.4
  12.2 1.9 collective-permute-start.5
  14.1 1.0 slice_bitcast_fusion.3
  15.1 4.5 collective-permute-start
  19.6 1.9 collective-permute-start.1
  23.5 0.6 fusion.178
  25.4 0.7 and_reduce_fusion.1
  27.4 0.6 fusion.176
  28.1 0.1 and_reduce_fusion
  28.2 0.1 multiply_reduce_fusion
  28.3 0.6 fusion.172
  28.9 2.7 fusion.80
  31.7 0.6 add.438
  32.9 0.1 add.441
  33.1 0.0 copy-start.3
  33.1 1.4 fusion.169
  34.5 0.7 fusion.175
  35.2 4.5 collective-permute-start.2
  39.7 1.9 collective-permute-start.3
  41.7 2.7 fusion.32
  44.4 10.6 %gather_fusion = f32[1024]{0:T(1024)S(1)} fusion(f32[32,16,384]{2,1,0:T(8,128)S(1)} %fusion.169, s32[1024]{0:T(1024)S(1)} %bitcast.63), kind=kCustom, calls=%fused_computation | custom fusion | bytes 20480 | tf_op jit(solution)/shard_map/gather | solution.py:60
  55.0 0.1 reshape.178
  55.1 3.5 fusion.56
  58.6 1.3 add.467
  60.5 1.4 add.469
  61.9 1.6 multiply_add_fusion.1
  63.5 10.6 %gather_fusion.1 = f32[1024]{0:T(1024)S(1)} fusion(f32[32,16,384]{2,1,0:T(8,128)S(1)} %multiply_add_fusion.1, s32[1024]{0:T(1024)S(1)} %bitcast.64), kind=kCustom, calls=%fused_computation.1 | custom fusion | bytes 20480 | tf_op jit(solution)/shard_map/gather | solution.py:60
  74.1 25.4 %psum.14 = f32[2,1024]{1,0:T(2,128)S(1)} all-reduce(f32[2,1024]{1,0:T(2,128)S(1)} %pad_maximum_fusion.8), channel_id=1, replica_groups=mesh['shot'=32,'dom'=16] {'dom'}, use_global_device_ids=true, to_apply=%region_1.2 | all-reduce | flops 2048 | bytes 16384 | tf_op jit(solution)/shard_map/psum | solution.py:107
  99.6 6.4 %scatter_fusion = f32[196608]{0:T(1024)S(1)} fusion(f32[196608]{0:T(1024)S(1)} %reshape.178, s32[1024]{0:T(1024)S(1)} %broadcast_select_fusion, f32[1024]{0:T(1024)S(1)} %get-tuple-element.48), kind=kCustom, calls=%fused_computation.2 | custom fusion | flops 1024 | bytes 16384
  105.9 1.1 reshape.180
  107.0 2.0 fusion.168
  109.1 1.9 collective-permute-start.6
  111.0 2.4 collective-permute-start.7
  113.4 4.4 collective-permute-done.7
  117.8 3.5 fusion.8
  121.3 1.2 reshape.182
  122.5 6.4 %scatter_fusion.1 = f32[196608]{0:T(1024)S(1)} fusion(f32[196608]{0:T(1024)S(1)} %reshape.182, s32[1024]{0:T(1024)S(1)} %broadcast_select_fusion, f32[1024]{0:T(1024)S(1)} %get-tuple-element.47), kind=kCustom, calls=%fused_computation.3 | custom fusion | flops 1024 | bytes 16384
  128.8 1.1 reshape.184
  129.9 3.6 fusion.171
  133.5 0.0 all-reduce.6.cloned.1.call-update
  133.5 323.3 %all-reduce.6.cloned.1.call-done = f32[32,16,384]{2,1,0:T(8,128)} async-done(((f32[32,16,384]{2,1,0:T(8,128)}), f32[32,16,384]{2,1,0:T(8,128)}) %all-reduce.6.cloned.1.call-update) | async-done | bytes 786448 | tf_op jit(solution)/shard_map/psum | solution.py:114
  456.8 2.1 copy.24
  (39 shorter events, 0.2 us)
Async XLA Ops:
  7.2 18.2 %copy-start.14 = (s32[3]{0:T(128)S(1)}, s32[3]{0:T(128)}, u32[]{:S(2)}) copy-start(s32[3]{0:T(128)} %constant.78.clone.1) | copy-start | bytes 40
  7.2 20.9 %copy-start.12 = (s32[3]{0:T(128)S(1)}, s32[3]{0:T(128)}, u32[]{:S(2)}) copy-start(s32[3]{0:T(128)} %constant.108) | copy-start | bytes 40
  7.2 21.0 %copy-start.13 = (s32[3]{0:T(128)S(1)}, s32[3]{0:T(128)}, u32[]{:S(2)}) copy-start(s32[3]{0:T(128)} %constant.105) | copy-start | bytes 40
  7.2 21.7 %copy-start.1 = (f32[1,32,16,384]{3,2,1,0:T(8,128)S(1)}, f32[1,32,16,384]{3,2,1,0:T(8,128)}, u32[]{:S(2)}) copy-start(f32[1,32,16,384]{3,2,1,0:T(8,128)} %param.19) | copy-start | bytes 2359300
  7.2 16.3 %copy-start.11 = (f32[1,2]{1,0:T(1,128)S(1)}, f32[1,2]{1,0:T(1,128)}, u32[]{:S(2)}) copy-start(f32[1,2]{1,0:T(1,128)} %param.25) | copy-start | bytes 28
  7.2 20.2 %copy-start.7 = (f32[1,2,1024]{2,1,0:T(2,128)S(1)}, f32[1,2,1024]{2,1,0:T(2,128)}, u32[]{:S(2)}) copy-start(f32[1,2,1024]{2,1,0:T(2,128)} %param.29) | copy-start | bytes 24580
  7.2 20.8 %copy-start.5 = (s32[1,1024]{1,0:T(1,128)S(1)}, s32[1,1024]{1,0:T(1,128)}, u32[]{:S(2)}) copy-start(s32[1,1024]{1,0:T(1,128)} %param.26) | copy-start | bytes 12292
  7.2 20.8 %copy-start.9 = (s32[1,1024]{1,0:T(1,128)S(1)}, s32[1,1024]{1,0:T(1,128)}, u32[]{:S(2)}) copy-start(s32[1,1024]{1,0:T(1,128)} %param.28) | copy-start | bytes 12292
  7.3 20.8 %copy-start.8 = (s32[1,1024]{1,0:T(1,128)S(1)}, s32[1,1024]{1,0:T(1,128)}, u32[]{:S(2)}) copy-start(s32[1,1024]{1,0:T(1,128)} %param.27) | copy-start | bytes 12292
  7.3 449.6 %all-reduce.6.cloned.1.call-start = ((), (), s32[]{:S(2)}) async-start(), calls=%async_computation | async-start | bytes 1572864 | tf_op jit(solution)/shard_map/psum | solution.py:114
  9.0 32.7 %collective-permute-start.4 = (f32[4,16,384]{2,1,0:T(8,128)}, f32[4,16,384]{2,1,0:T(8,128)S(1)}, u32[]{:S(2)}, u32[]{:S(2)}) collective-permute-start(f32[4,16,384]{2,1,0:T(8,128)} %get-tuple-element.33), channel_id=1, source_target_pairs={{1,0},{2,1},{3,2},{4,3},{5,4},{6,5},{7,6},{8,7},{9,8},{10,9},{11,1... | collective-permute-start | bytes 294920 | tf_op jit(solution)/shard_map/ppermute | solution.py:20
  12.2 29.5 %collective-permute-start.5 = (f32[4,16,384]{2,1,0:T(8,128)}, f32[4,16,384]{2,1,0:T(8,128)S(1)}, u32[]{:S(2)}, u32[]{:S(2)}) collective-permute-start(f32[4,16,384]{2,1,0:T(8,128)} %get-tuple-element.34), channel_id=1, source_target_pairs={{0,1},{1,2},{2,3},{3,4},{4,5},{5,6},{6,7},{7,8},{8,9},{9,10},{10,1... | collective-permute-start | bytes 294920 | tf_op jit(solution)/shard_map/ppermute | solution.py:17
  15.1 13.9 %collective-permute-start = (f32[4,16,384]{2,1,0:T(8,128)S(1)}, f32[4,16,384]{2,1,0:T(8,128)S(1)}, u32[]{:S(2)}, u32[]{:S(2)}) collective-permute-start(f32[4,16,384]{2,1,0:T(8,128)S(1)} %get-tuple-element.37), channel_id=1, source_target_pairs={{1,0},{2,1},{3,2},{4,3},{5,4},{6,5},{7,6},{8,7},{9,8},{10,9},{11,1... | collective-permute-start | bytes 294920 | tf_op jit(solution)/shard_map/ppermute | solution.py:20
  19.6 9.3 %collective-permute-start.1 = (f32[4,16,384]{2,1,0:T(8,128)S(1)}, f32[4,16,384]{2,1,0:T(8,128)S(1)}, u32[]{:S(2)}, u32[]{:S(2)}) collective-permute-start(f32[4,16,384]{2,1,0:T(8,128)S(1)} %get-tuple-element.38), channel_id=1, source_target_pairs={{0,1},{1,2},{2,3},{3,4},{4,5},{5,6},{6,7},{7,8},{8,9},{9,10},{10,1... | collective-permute-start | bytes 294920 | tf_op jit(solution)/shard_map/ppermute | solution.py:17
  28.9 4.1 copy-start.2
  33.1 8.6 %copy-start.3 = (f32[1,32,16,384]{3,2,1,0:T(8,128)S(1)}, f32[1,32,16,384]{3,2,1,0:T(8,128)}, u32[]{:S(2)}) copy-start(f32[1,32,16,384]{3,2,1,0:T(8,128)} %param.21) | copy-start | bytes 2359300
  35.2 19.9 %collective-permute-start.2 = (f32[4,16,384]{2,1,0:T(8,128)}, f32[4,16,384]{2,1,0:T(8,128)S(1)}, u32[]{:S(2)}, u32[]{:S(2)}) collective-permute-start(f32[4,16,384]{2,1,0:T(8,128)} %get-tuple-element.35), channel_id=1, source_target_pairs={{1,0},{2,1},{3,2},{4,3},{5,4},{6,5},{7,6},{8,7},{9,8},{10,9},{11,1... | collective-permute-start | bytes 294920 | tf_op jit(solution)/shard_map/ppermute | solution.py:20
  39.7 15.3 %collective-permute-start.3 = (f32[4,16,384]{2,1,0:T(8,128)}, f32[4,16,384]{2,1,0:T(8,128)S(1)}, u32[]{:S(2)}, u32[]{:S(2)}) collective-permute-start(f32[4,16,384]{2,1,0:T(8,128)} %get-tuple-element.36), channel_id=1, source_target_pairs={{0,1},{1,2},{2,3},{3,4},{4,5},{5,6},{6,7},{7,8},{8,9},{9,10},{10,1... | collective-permute-start | bytes 294920 | tf_op jit(solution)/shard_map/ppermute | solution.py:17
  63.4 66.5 %copy-start = (f32[32,16,384]{2,1,0:T(8,128)}, f32[32,16,384]{2,1,0:T(8,128)S(1)}, u32[]{:S(2)}) copy-start(f32[32,16,384]{2,1,0:T(8,128)S(1)} %multiply_add_fusion.1) | copy-start | bytes 2359300
  63.4 36.1 %copy-start.6 = (f32[1,1,1024]{2,1,0:T(1,128)S(1)}, f32[1,1,1024]{2,1,0:T(1,128)}, u32[]{:S(2)}) copy-start(f32[1,1,1024]{2,1,0:T(1,128)} %get-tuple-element.40) | copy-start | bytes 12292
  63.4 36.1 %copy-start.10 = (pred[1024]{0:T(1024)(128)(4,1)S(1)}, pred[1024]{0:T(1024)(128)(4,1)}, u32[]{:S(2)}) copy-start(pred[1024]{0:T(1024)(128)(4,1)} %fusion.172) | copy-start | bytes 3076
  109.0 8.8 %copy-start.4 = (f32[32,16,384]{2,1,0:T(8,128)}, f32[32,16,384]{2,1,0:T(8,128)S(1)}, u32[]{:S(2)}) copy-start(f32[32,16,384]{2,1,0:T(8,128)S(1)} %fusion.168) | copy-start | bytes 2359300
  109.1 4.3 collective-permute-start.6
  111.0 6.8 %collective-permute-start.7 = (f32[4,16,384]{2,1,0:T(8,128)S(1)}, f32[4,16,384]{2,1,0:T(8,128)S(1)}, u32[]{:S(2)}, u32[]{:S(2)}) collective-permute-start(f32[4,16,384]{2,1,0:T(8,128)S(1)} %get-tuple-element.32), channel_id=1, source_target_pairs={{0,1},{1,2},{2,3},{3,4},{4,5},{5,6},{6,7},{7,8},{8,9},{9,10},{10,1... | collective-permute-start | bytes 294920 | tf_op jit(solution)/shard_map/ppermute | solution.py:17
Sparse Core Ops, SparseCore 0:
  133.7 323.1 all-reduce.5
where the time goes:
time: 466 us
  waiting for transfers between devices  328 us (70%)
  other arithmetic  35.3 us (8%)
  local copies, waits for them, and re-layouts  34.5 us (7%)
  blocking collectives  25.4 us (5%)
  starting transfers between devices  22.4 us (5%)
  between operations  20.4 us (4%)
    psum x1, waiting for transfers between devices, shards(): gradient = lax.psum(early_term + late_term, 'shot')  323 us
    psum x1, blocking collectives, shards(): traces = lax.psum(samples, 'dom')  25.4 us
    gather x2, local copies, waits for them, and re-layouts, sample(): picked = field[local, ycells, zcells]  21.1 us
    ppermute x4, starting transfers between devices, with_halo(): lax.ppermute(lax.slice_in_dim(block, 0, width, axis=dim), axis, backward)  14.2 us
    unnamed x5, other arithmetic  12.9 us
    add x4, other arithmetic, laplace_core(): total + weight * (padded[:, R:R + width_y, R + offset:R + offset + width_...  12.4 us
  transfers between devices with their start and end apart: 9, of which 2 were waited for; matrix products, arithmetic and copies ran while one was open for 5% of the time, Pallas kernels for 0%

commit v1 on v0

--- a/solution.py
+++ b/solution.py
@@ -61,6 +61,14 @@
     return jnp.where(inside, picked, jnp.zeros_like(picked))
 
 
+def shot_sum(term):
+    count = lax.axis_size("shot")
+    pieces = term.reshape((count, term.shape[0] // count) + term.shape[1:])
+    mine = jnp.sum(lax.all_to_all(pieces, "shot", 0, 0, tiled=False), axis=0)
+    spread = jnp.broadcast_to(mine[None], (count,) + mine.shape)
+    return lax.all_to_all(spread, "shot", 0, 0, tiled=False).reshape(term.shape)
+
+
 def shards(
     coefficient,
     fwd_older,
@@ -101,17 +109,13 @@
         recent,
         point_grid(shape, source_xcell, source_ycell, source_zcell, amplitude[0, 1:2], base),
     )
-    samples = jnp.stack(
-        [sample(fwd_two, rxc, ryc, rzc, base), sample(fwd_three, rxc, ryc, rzc, base)]
-    )
-    traces = lax.psum(samples, "dom")
-    resid_two = traces[0] - observed[0, 0]
-    resid_three = traces[1] - observed[0, 1]
+    resid_two = sample(fwd_two, rxc, ryc, rzc, base) - observed[0, 0]
+    resid_three = sample(fwd_three, rxc, ryc, rzc, base) - observed[0, 1]
     adj_two = advance(adj_now, later, point_grid(shape, rxc, ryc, rzc, resid_three, base))
     late_term = adj_two * (fwd_three - 2.0 * fwd_two + recent)
     adj_one = advance(adj_two, adj_now, point_grid(shape, rxc, ryc, rzc, resid_two, base))
     early_term = adj_one * (fwd_two - 2.0 * recent + older)
-    gradient = lax.psum(early_term + late_term, "shot")
+    gradient = shot_sum(early_term + late_term)
     return (fwd_three[None], adj_one[None], gradient)
 
 

time: 466 us -> 175 us (0.38)
  the two profiles are of different devices: /device:TPU:6 before, /device:TPU:11 now
where the time goes in v1:
time: 175 us; the launch traced here: 174 us
  blocking collectives  71.6 us (41%)
  other arithmetic  35.1 us (20%)
  local copies, waits for them, and re-layouts  32.8 us (19%)
  starting transfers between devices  25.8 us (15%)
  between operations  6.98 us (4%)
    all_to_all x1, blocking collectives, shot_sum(): mine = jnp.sum(lax.all_to_all(pieces, 'shot', 0, 0, tiled=False), axis=0)  40 us
    all_to_all x1, blocking collectives, shot_sum(): return lax.all_to_all(spread, 'shot', 0, 0, tiled=False).reshape(term.shape)  31.6 us
    gather x2, local copies, waits for them, and re-layouts, sample(): picked = field[local, ycells, zcells]  21.1 us
    ppermute x4, starting transfers between devices, with_halo(): lax.ppermute(lax.slice_in_dim(block, block.shape[dim] - width, None, axis...  17.5 us
    unnamed x5, other arithmetic  12.9 us
    add x4, other arithmetic, laplace_core(): total + weight * (padded[:, R:R + width_y, R + offset:R + offset + width_...  12.4 us
    ppermute x4, starting transfers between devices, with_halo(): lax.ppermute(lax.slice_in_dim(block, 0, width, axis=dim), axis, backward)  8.32 us
    add x3, other arithmetic, advance(): 2.0 * current - before + coefficient * (laplace_core(extended) + sources)  5.03 us
  transfers between devices with their start and end apart: 8, of which 2 were waited for; matrix products, arithmetic and copies ran while one was open for 13% of the time, Pallas kernels for 0%

profile of v1, /device:TPU:11, one launch (start us, length us, event | category | flops | bytes accessed | tf_op | source)
XLA Modules:
  0.0 174.0 jit_solution(17264245207240661347)
XLA Ops:
  0.6 0.0 copy-start.13
  0.6 0.0 copy-start.11
  0.7 0.0 copy-start.12
  0.7 0.0 copy-start.1
  0.7 1.7 slice_bitcast_fusion.1
  2.4 2.6 %collective-permute-start.4 = (f32[4,16,384]{2,1,0:T(8,128)}, f32[4,16,384]{2,1,0:T(8,128)S(1)}, u32[]{:S(2)}, u32[]{:S(2)}) collective-permute-start(f32[4,16,384]{2,1,0:T(8,128)} %get-tuple-element.33), channel_id=1, source_target_pairs={{1,0},{2,1},{3,2},{4,3},{5,4},{6,5},{7,6},{8,7},{9,8},{10,9},{11,1... | collective-permute-start | bytes 294920 | tf_op jit(solution)/shard_map/ppermute | solution.py:20
  5.0 3.9 %collective-permute-start.5 = (f32[4,16,384]{2,1,0:T(8,128)}, f32[4,16,384]{2,1,0:T(8,128)S(1)}, u32[]{:S(2)}, u32[]{:S(2)}) collective-permute-start(f32[4,16,384]{2,1,0:T(8,128)} %get-tuple-element.34), channel_id=1, source_target_pairs={{0,1},{1,2},{2,3},{3,4},{4,5},{5,6},{6,7},{7,8},{8,9},{9,10},{10,1... | collective-permute-start | bytes 294920 | tf_op jit(solution)/shard_map/ppermute | solution.py:17
  8.9 1.0 slice_bitcast_fusion.3
  9.8 1.9 %collective-permute-start = (f32[4,16,384]{2,1,0:T(8,128)S(1)}, f32[4,16,384]{2,1,0:T(8,128)S(1)}, u32[]{:S(2)}, u32[]{:S(2)}) collective-permute-start(f32[4,16,384]{2,1,0:T(8,128)S(1)} %get-tuple-element.37), channel_id=1, source_target_pairs={{1,0},{2,1},{3,2},{4,3},{5,4},{6,5},{7,6},{8,7},{9,8},{10,9},{11,1... | collective-permute-start | bytes 294920 | tf_op jit(solution)/shard_map/ppermute | solution.py:20
  11.8 4.5 %collective-permute-start.1 = (f32[4,16,384]{2,1,0:T(8,128)S(1)}, f32[4,16,384]{2,1,0:T(8,128)S(1)}, u32[]{:S(2)}, u32[]{:S(2)}) collective-permute-start(f32[4,16,384]{2,1,0:T(8,128)S(1)} %get-tuple-element.38), channel_id=1, source_target_pairs={{0,1},{1,2},{2,3},{3,4},{4,5},{5,6},{6,7},{7,8},{8,9},{9,10},{10,1... | collective-permute-start | bytes 294920 | tf_op jit(solution)/shard_map/ppermute | solution.py:17
  18.3 0.6 fusion.177
  20.3 0.7 and_reduce_fusion.2
  22.4 0.1 and_reduce_fusion
  22.5 0.1 multiply_reduce_fusion
  22.6 0.6 and_reduce_fusion.1
  23.2 0.0 copy-start.2
  23.2 2.7 %fusion.80 = f32[32,16,384]{2,1,0:T(8,128)S(1)} fusion(f32[32,16,384]{2,1,0:T(8,128)S(1)} %bitcast.69, f32[4,16,384]{2,1,0:T(8,128)S(1)} %collective-permute-done.1, f32[4,16,384]{2,1,0:T(8,128)S(1)} %collective-permute-done), kind=kLoop, calls=%fused_computation.196 | loop fusion | flops 8847360 | bytes 1769472 | tf_op jit(solution)/shard_map/add | solution.py:41
  25.9 0.6 add.434
  27.2 0.1 add.437
  27.4 1.4 fusion.169
  28.8 0.7 fusion.175
  29.5 1.9 %collective-permute-start.2 = (f32[4,16,384]{2,1,0:T(8,128)}, f32[4,16,384]{2,1,0:T(8,128)S(1)}, u32[]{:S(2)}, u32[]{:S(2)}) collective-permute-start(f32[4,16,384]{2,1,0:T(8,128)} %get-tuple-element.35), channel_id=1, source_target_pairs={{1,0},{2,1},{3,2},{4,3},{5,4},{6,5},{7,6},{8,7},{9,8},{10,9},{11,1... | collective-permute-start | bytes 294920 | tf_op jit(solution)/shard_map/ppermute | solution.py:20
  31.4 4.5 %collective-permute-start.3 = (f32[4,16,384]{2,1,0:T(8,128)}, f32[4,16,384]{2,1,0:T(8,128)S(1)}, u32[]{:S(2)}, u32[]{:S(2)}) collective-permute-start(f32[4,16,384]{2,1,0:T(8,128)} %get-tuple-element.36), channel_id=1, source_target_pairs={{0,1},{1,2},{2,3},{3,4},{4,5},{5,6},{6,7},{7,8},{8,9},{9,10},{10,1... | collective-permute-start | bytes 294920 | tf_op jit(solution)/shard_map/ppermute | solution.py:17
  36.0 2.7 %fusion.32 = f32[32,16,384]{2,1,0:T(8,128)S(1)} fusion(f32[32,16,384]{2,1,0:T(8,128)S(1)} %bitcast.70, f32[4,16,384]{2,1,0:T(8,128)S(1)} %collective-permute-done.5, f32[4,16,384]{2,1,0:T(8,128)S(1)} %collective-permute-done.4), kind=kLoop, calls=%fused_computation.148 | loop fusion | flops 8847360 | bytes 1769472 | tf_op jit(solution)/shard_map/add | solution.py:41
  38.7 10.6 %gather_fusion.1 = f32[1024]{0:T(1024)S(1)} fusion(f32[32,16,384]{2,1,0:T(8,128)S(1)} %fusion.169, s32[1024]{0:T(1024)S(1)} %bitcast.66), kind=kCustom, calls=%fused_computation.1 | custom fusion | bytes 20480 | tf_op jit(solution)/shard_map/gather | solution.py:60
  49.3 0.1 reshape.189
  49.4 3.5 %fusion.56 = f32[32,16,384]{2,1,0:T(8,128)} fusion(f32[32,16,384]{2,1,0:T(8,128)S(1)} %fusion.169, f32[4,16,384]{2,1,0:T(8,128)S(1)} %collective-permute-done.3, f32[4,16,384]{2,1,0:T(8,128)S(1)} %collective-permute-done.2), kind=kLoop, calls=%fused_computation.172 | loop fusion | flops 8847360 | bytes 1769472 | tf_op jit(solution)/shard_map/add | solution.py:41
  52.8 1.3 add.463
  54.8 1.4 add.465
  56.1 1.6 multiply_add_fusion.1
  57.7 10.6 %gather_fusion = f32[1024]{0:T(1024)S(1)} fusion(f32[32,16,384]{2,1,0:T(8,128)S(1)} %multiply_add_fusion.1, s32[1024]{0:T(1024)S(1)} %bitcast.67), kind=kCustom, calls=%fused_computation | custom fusion | bytes 20480 | tf_op jit(solution)/shard_map/gather | solution.py:60
  68.3 6.4 %scatter_fusion = f32[196608]{0:T(1024)S(1)} fusion(f32[196608]{0:T(1024)S(1)} %reshape.189, s32[1024]{0:T(1024)S(1)} %broadcast_select_fusion, f32[1024]{0:T(1024)S(1)} %get-tuple-element.44), kind=kCustom, calls=%fused_computation.2 | custom fusion | flops 1024 | bytes 16384
  74.7 1.1 reshape.191
  75.8 2.0 %fusion.168 = f32[32,16,384]{2,1,0:T(8,128)S(1)} fusion(f32[1,32,16,384]{3,2,1,0:T(8,128)} %param.20, f32[32,16,384]{2,1,0:T(8,128)} %param.17, f32[32,16,384]{2,1,0:T(8,128)} %reshape.191, f32[1,32,16,384]{3,2,1,0:T(8,128)} %param.21), kind=kLoop, calls=%fused_computation.293 | loop fusion | flops 786432 | bytes 3932160 | tf_op jit(solution)/shard_map/add | solution.py:100
  77.8 1.9 %collective-permute-start.6 = (f32[4,16,384]{2,1,0:T(8,128)S(1)}, f32[4,16,384]{2,1,0:T(8,128)S(1)}, u32[]{:S(2)}, u32[]{:S(2)}) collective-permute-start(f32[4,16,384]{2,1,0:T(8,128)S(1)} %get-tuple-element.31), channel_id=1, source_target_pairs={{1,0},{2,1},{3,2},{4,3},{5,4},{6,5},{7,6},{8,7},{9,8},{10,9},{11,1... | collective-permute-start | bytes 294920 | tf_op jit(solution)/shard_map/ppermute | solution.py:20
  79.8 4.5 %collective-permute-start.7 = (f32[4,16,384]{2,1,0:T(8,128)S(1)}, f32[4,16,384]{2,1,0:T(8,128)S(1)}, u32[]{:S(2)}, u32[]{:S(2)}) collective-permute-start(f32[4,16,384]{2,1,0:T(8,128)S(1)} %get-tuple-element.32), channel_id=1, source_target_pairs={{0,1},{1,2},{2,3},{3,4},{4,5},{5,6},{6,7},{7,8},{8,9},{9,10},{10,1... | collective-permute-start | bytes 294920 | tf_op jit(solution)/shard_map/ppermute | solution.py:17
  84.3 0.7 collective-permute-done.6
  85.0 1.0 collective-permute-done.7
  85.9 3.4 %fusion.8 = f32[32,16,384]{2,1,0:T(8,128)} fusion(f32[32,16,384]{2,1,0:T(8,128)S(1)} %fusion.168, f32[4,16,384]{2,1,0:T(8,128)S(1)} %collective-permute-done.7, f32[4,16,384]{2,1,0:T(8,128)S(1)} %collective-permute-done.6), kind=kLoop, calls=%fused_computation.124 | loop fusion | flops 8847360 | bytes 1769472 | tf_op jit(solution)/shard_map/add | solution.py:41
  89.4 1.2 reshape.193
  90.6 6.4 %scatter_fusion.1 = f32[196608]{0:T(1024)S(1)} fusion(f32[196608]{0:T(1024)S(1)} %reshape.193, s32[1024]{0:T(1024)S(1)} %broadcast_select_fusion, f32[1024]{0:T(1024)S(1)} %get-tuple-element.43), kind=kCustom, calls=%fused_computation.3 | custom fusion | flops 1024 | bytes 16384
  96.9 1.1 reshape.195
  98.0 3.4 %fusion.172 = (f32[32,1,16,384]{3,2,1,0:T(8,128)S(1)}, f32[1,32,16,384]{3,2,1,0:T(8,128)}) fusion(f32[1,32,16,384]{3,2,1,0:T(8,128)} %param.18, f32[32,16,384]{2,1,0:T(8,128)} %copy-done.4, f32[32,16,384]{2,1,0:T(8,128)S(1)} %multiply_add_fusion.1, f32[32,16,384]{2,1,0:T(8,128)S(1)} %fusion.169, f32[1,32,16,384]{3,2,1,0:T(8,128)S(1)} %copy-done.1, ...), kind=kLoop, calls=%fused_computation.299 | loop fusion | flops 2555904 | bytes 7864320 | tf_op jit(solution)/shard_map/reshape | solution.py:66
  101.4 40.0 %all_to_all.10 = f32[32,1,16,384]{3,2,1,0:T(8,128)S(1)} all-to-all(f32[32,1,16,384]{3,2,1,0:T(8,128)S(1)} %get-tuple-element.29), channel_id=1, replica_groups=mesh['shot'=32,'dom'=16] {'shot'}, dimensions={0} | all-to-all | bytes 1572864 | tf_op jit(solution)/shard_map/all_to_all | solution.py:67
  141.3 0.1 reduce_sum.9
  141.4 0.1 broadcast_in_dim.8
  141.4 31.6 %all_to_all.11 = f32[32,1,16,384]{3,2,1,0:T(8,128)S(1)} all-to-all(f32[32,1,16,384]{3,2,1,0:T(8,128)S(1)} %broadcast_in_dim.8), channel_id=1, replica_groups=mesh['shot'=32,'dom'=16] {'shot'}, dimensions={0} | all-to-all | bytes 1572864 | tf_op jit(solution)/shard_map/all_to_all | solution.py:69
  173.1 0.9 copy.25
  (34 shorter events, 0.1 us)
Async XLA Ops:
  0.6 19.6 %copy-start.13 = (s32[3]{0:T(128)S(1)}, s32[3]{0:T(128)}, u32[]{:S(2)}) copy-start(s32[3]{0:T(128)} %constant.79.clone.1) | copy-start | bytes 40
  0.6 21.7 %copy-start.11 = (s32[3]{0:T(128)S(1)}, s32[3]{0:T(128)}, u32[]{:S(2)}) copy-start(s32[3]{0:T(128)} %constant.109) | copy-start | bytes 40
  0.7 21.8 %copy-start.12 = (s32[3]{0:T(128)S(1)}, s32[3]{0:T(128)}, u32[]{:S(2)}) copy-start(s32[3]{0:T(128)} %constant.106) | copy-start | bytes 40
  0.7 22.5 %copy-start.1 = (f32[1,32,16,384]{3,2,1,0:T(8,128)S(1)}, f32[1,32,16,384]{3,2,1,0:T(8,128)}, u32[]{:S(2)}) copy-start(f32[1,32,16,384]{3,2,1,0:T(8,128)} %param.19) | copy-start | bytes 2359300
  0.7 17.6 %copy-start.10 = (f32[1,2]{1,0:T(1,128)S(1)}, f32[1,2]{1,0:T(1,128)}, u32[]{:S(2)}) copy-start(f32[1,2]{1,0:T(1,128)} %param.25) | copy-start | bytes 28
  0.7 21.6 %copy-start.6 = (f32[1,2,1024]{2,1,0:T(2,128)S(1)}, f32[1,2,1024]{2,1,0:T(2,128)}, u32[]{:S(2)}) copy-start(f32[1,2,1024]{2,1,0:T(2,128)} %param.29) | copy-start | bytes 24580
  0.7 21.6 %copy-start.5 = (s32[1,1024]{1,0:T(1,128)S(1)}, s32[1,1024]{1,0:T(1,128)}, u32[]{:S(2)}) copy-start(s32[1,1024]{1,0:T(1,128)} %param.26) | copy-start | bytes 12292
  0.7 21.6 %copy-start.8 = (s32[1,1024]{1,0:T(1,128)S(1)}, s32[1,1024]{1,0:T(1,128)}, u32[]{:S(2)}) copy-start(s32[1,1024]{1,0:T(1,128)} %param.28) | copy-start | bytes 12292
  0.7 21.6 %copy-start.7 = (s32[1,1024]{1,0:T(1,128)S(1)}, s32[1,1024]{1,0:T(1,128)}, u32[]{:S(2)}) copy-start(s32[1,1024]{1,0:T(1,128)} %param.27) | copy-start | bytes 12292
  2.4 33.5 %collective-permute-start.4 = (f32[4,16,384]{2,1,0:T(8,128)}, f32[4,16,384]{2,1,0:T(8,128)S(1)}, u32[]{:S(2)}, u32[]{:S(2)}) collective-permute-start(f32[4,16,384]{2,1,0:T(8,128)} %get-tuple-element.33), channel_id=1, source_target_pairs={{1,0},{2,1},{3,2},{4,3},{5,4},{6,5},{7,6},{8,7},{9,8},{10,9},{11,1... | collective-permute-start | bytes 294920 | tf_op jit(solution)/shard_map/ppermute | solution.py:20
  5.0 30.9 %collective-permute-start.5 = (f32[4,16,384]{2,1,0:T(8,128)}, f32[4,16,384]{2,1,0:T(8,128)S(1)}, u32[]{:S(2)}, u32[]{:S(2)}) collective-permute-start(f32[4,16,384]{2,1,0:T(8,128)} %get-tuple-element.34), channel_id=1, source_target_pairs={{0,1},{1,2},{2,3},{3,4},{4,5},{5,6},{6,7},{7,8},{8,9},{9,10},{10,1... | collective-permute-start | bytes 294920 | tf_op jit(solution)/shard_map/ppermute | solution.py:17
  9.8 13.3 %collective-permute-start = (f32[4,16,384]{2,1,0:T(8,128)S(1)}, f32[4,16,384]{2,1,0:T(8,128)S(1)}, u32[]{:S(2)}, u32[]{:S(2)}) collective-permute-start(f32[4,16,384]{2,1,0:T(8,128)S(1)} %get-tuple-element.37), channel_id=1, source_target_pairs={{1,0},{2,1},{3,2},{4,3},{5,4},{6,5},{7,6},{8,7},{9,8},{10,9},{11,1... | collective-permute-start | bytes 294920 | tf_op jit(solution)/shard_map/ppermute | solution.py:20
  11.8 11.4 %collective-permute-start.1 = (f32[4,16,384]{2,1,0:T(8,128)S(1)}, f32[4,16,384]{2,1,0:T(8,128)S(1)}, u32[]{:S(2)}, u32[]{:S(2)}) collective-permute-start(f32[4,16,384]{2,1,0:T(8,128)S(1)} %get-tuple-element.38), channel_id=1, source_target_pairs={{0,1},{1,2},{2,3},{3,4},{4,5},{5,6},{6,7},{7,8},{8,9},{9,10},{10,1... | collective-permute-start | bytes 294920 | tf_op jit(solution)/shard_map/ppermute | solution.py:17
  23.2 4.1 %copy-start.2 = (f32[32,16,384]{2,1,0:T(8,128)S(1)}, f32[32,16,384]{2,1,0:T(8,128)}, u32[]{:S(2)}) copy-start(f32[32,16,384]{2,1,0:T(8,128)} %param.17) | copy-start | bytes 2359300
  27.4 8.6 %copy-start.3 = (f32[1,32,16,384]{3,2,1,0:T(8,128)S(1)}, f32[1,32,16,384]{3,2,1,0:T(8,128)}, u32[]{:S(2)}) copy-start(f32[1,32,16,384]{3,2,1,0:T(8,128)} %param.21) | copy-start | bytes 2359300
  29.5 19.9 %collective-permute-start.2 = (f32[4,16,384]{2,1,0:T(8,128)}, f32[4,16,384]{2,1,0:T(8,128)S(1)}, u32[]{:S(2)}, u32[]{:S(2)}) collective-permute-start(f32[4,16,384]{2,1,0:T(8,128)} %get-tuple-element.35), channel_id=1, source_target_pairs={{1,0},{2,1},{3,2},{4,3},{5,4},{6,5},{7,6},{8,7},{9,8},{10,9},{11,1... | collective-permute-start | bytes 294920 | tf_op jit(solution)/shard_map/ppermute | solution.py:20
  31.4 18.0 %collective-permute-start.3 = (f32[4,16,384]{2,1,0:T(8,128)}, f32[4,16,384]{2,1,0:T(8,128)S(1)}, u32[]{:S(2)}, u32[]{:S(2)}) collective-permute-start(f32[4,16,384]{2,1,0:T(8,128)} %get-tuple-element.36), channel_id=1, source_target_pairs={{0,1},{1,2},{2,3},{3,4},{4,5},{5,6},{6,7},{7,8},{8,9},{9,10},{10,1... | collective-permute-start | bytes 294920 | tf_op jit(solution)/shard_map/ppermute | solution.py:17
  57.7 40.3 %copy-start = (f32[32,16,384]{2,1,0:T(8,128)}, f32[32,16,384]{2,1,0:T(8,128)S(1)}, u32[]{:S(2)}) copy-start(f32[32,16,384]{2,1,0:T(8,128)S(1)} %multiply_add_fusion.1) | copy-start | bytes 2359300
  57.7 10.6 %copy-start.9 = (pred[1024]{0:T(1024)(128)(4,1)S(1)}, pred[1024]{0:T(1024)(128)(4,1)}, u32[]{:S(2)}) copy-start(pred[1024]{0:T(1024)(128)(4,1)} %and_reduce_fusion.1) | copy-start | bytes 3076
  77.8 8.1 %copy-start.4 = (f32[32,16,384]{2,1,0:T(8,128)}, f32[32,16,384]{2,1,0:T(8,128)S(1)}, u32[]{:S(2)}) copy-start(f32[32,16,384]{2,1,0:T(8,128)S(1)} %fusion.168) | copy-start | bytes 2359300
  77.8 7.1 %collective-permute-start.6 = (f32[4,16,384]{2,1,0:T(8,128)S(1)}, f32[4,16,384]{2,1,0:T(8,128)S(1)}, u32[]{:S(2)}, u32[]{:S(2)}) collective-permute-start(f32[4,16,384]{2,1,0:T(8,128)S(1)} %get-tuple-element.31), channel_id=1, source_target_pairs={{1,0},{2,1},{3,2},{4,3},{5,4},{6,5},{7,6},{8,7},{9,8},{10,9},{11,1... | collective-permute-start | bytes 294920 | tf_op jit(solution)/shard_map/ppermute | solution.py:20
  79.8 6.2 %collective-permute-start.7 = (f32[4,16,384]{2,1,0:T(8,128)S(1)}, f32[4,16,384]{2,1,0:T(8,128)S(1)}, u32[]{:S(2)}, u32[]{:S(2)}) collective-permute-start(f32[4,16,384]{2,1,0:T(8,128)S(1)} %get-tuple-element.32), channel_id=1, source_target_pairs={{0,1},{1,2},{2,3},{3,4},{4,5},{5,6},{6,7},{7,8},{8,9},{9,10},{10,1... | collective-permute-start | bytes 294920 | tf_op jit(solution)/shard_map/ppermute | solution.py:17

commit v2 on v1

--- a/solution.py
+++ b/solution.py
@@ -53,12 +53,27 @@
     return jnp.zeros(shape, values.dtype).at[local, ycells, zcells].add(kept)
 
 
-def sample(field, xcells, ycells, zcells, start):
-    count = field.shape[0]
-    inside = (xcells >= start) & (xcells < start + count)
-    local = jnp.clip(xcells - start, 0, count - 1)
-    picked = field[local, ycells, zcells]
-    return jnp.where(inside, picked, jnp.zeros_like(picked))
+def selectors(shape, xcells, ycells, zcells, start):
+    width_x, width_y, width_z = shape
+    inside = (xcells >= start) & (xcells < start + width_x)
+    row = jnp.where(inside, (xcells - start) * width_y + ycells, -1)
+    count = xcells.shape[0]
+    rows = (row[:, None] == lax.broadcasted_iota(jnp.int32, (count, width_x * width_y), 1)).astype(jnp.float32)
+    cols = (zcells[:, None] == lax.broadcasted_iota(jnp.int32, (count, width_z), 1)).astype(jnp.float32)
+    return rows, cols
+
+
+def sample(field, rows, cols):
+    width_x, width_y, width_z = field.shape
+    picked = jnp.dot(rows, field.reshape(width_x * width_y, width_z), precision=lax.Precision.HIGHEST)
+    return jnp.sum(picked * cols, axis=1)
+
+
+def receiver_grid(shape, rows, cols, values):
+    placed = lax.dot_general(
+        rows * values[:, None], cols, (((0,), (0,)), ((), ())), precision=lax.Precision.HIGHEST
+    )
+    return placed.reshape(shape)
 
 
 def shot_sum(term):
@@ -109,11 +124,12 @@
         recent,
         point_grid(shape, source_xcell, source_ycell, source_zcell, amplitude[0, 1:2], base),
     )
-    resid_two = sample(fwd_two, rxc, ryc, rzc, base) - observed[0, 0]
-    resid_three = sample(fwd_three, rxc, ryc, rzc, base) - observed[0, 1]
-    adj_two = advance(adj_now, later, point_grid(shape, rxc, ryc, rzc, resid_three, base))
+    rows, cols = selectors(shape, rxc, ryc, rzc, base)
+    resid_two = sample(fwd_two, rows, cols) - observed[0, 0]
+    resid_three = sample(fwd_three, rows, cols) - observed[0, 1]
+    adj_two = advance(adj_now, later, receiver_grid(shape, rows, cols, resid_three))
     late_term = adj_two * (fwd_three - 2.0 * fwd_two + recent)
-    adj_one = advance(adj_two, adj_now, point_grid(shape, rxc, ryc, rzc, resid_two, base))
+    adj_one = advance(adj_two, adj_now, receiver_grid(shape, rows, cols, resid_two))
     early_term = adj_one * (fwd_two - 2.0 * recent + older)
     gradient = shot_sum(early_term + late_term)
     return (fwd_three[None], adj_one[None], gradient)

time: 175 us -> 136 us (0.78)
  the two profiles are of different devices: /device:TPU:11 before, /device:TPU:1 now
where the time goes in v2:
time: 136 us; the launch traced here: 134 us
  blocking collectives  67.3 us (49%)
  starting transfers between devices  28.2 us (21%)
  other arithmetic  14.5 us (11%)
  matrix products  11.1 us (8%)
  between operations  6.97 us (5%)
  local copies, waits for them, and re-layouts  5.73 us (4%)
    all_to_all x1, blocking collectives, shot_sum(): mine = jnp.sum(lax.all_to_all(pieces, 'shot', 0, 0, tiled=False), axis=0)  34.8 us
    all_to_all x1, blocking collectives, shot_sum(): return lax.all_to_all(spread, 'shot', 0, 0, tiled=False).reshape(term.shape)  32.5 us
    ppermute x4, starting transfers between devices, with_halo(): lax.ppermute(lax.slice_in_dim(block, 0, width, axis=dim), axis, backward)  15 us
    ppermute x4, starting transfers between devices, with_halo(): lax.ppermute(lax.slice_in_dim(block, block.shape[dim] - width, None, axis...  13.1 us
    dot_general x2, matrix products, receiver_grid(): lax.dot_general(rows * values[:, None], cols, (((0,), (0,)), ((), ())), p...  7.58 us
    add x2, other arithmetic, laplace_core(): total + weight * (padded[:, R:R + width_y, R + offset:R + offset + width_...  5.45 us
    add x3, other arithmetic, advance(): 2.0 * current - before + coefficient * (laplace_core(extended) + sources)  4.33 us
    reshape x1, other arithmetic, shot_sum(): pieces = term.reshape((count, term.shape[0] // count) + term.shape[1:])  3.9 us
  transfers between devices with their start and end apart: 8, of which 0 were waited for; matrix products, arithmetic and copies ran while one was open for 17% of the time, Pallas kernels for 0%

profile of v2, /device:TPU:1, one launch (start us, length us, event | category | flops | bytes accessed | tf_op | source)
XLA Modules:
  0.0 133.8 jit_solution(1265154456625778702)
XLA Ops:
  0.6 0.0 copy-start.10
  0.6 0.0 copy-start
  0.7 1.0 slice_bitcast_fusion.1
  1.7 8.8 %collective-permute-start.4 = (f32[4,16,384]{2,1,0:T(8,128)S(1)}, f32[4,16,384]{2,1,0:T(8,128)S(1)}, u32[]{:S(2)}, u32[]{:S(2)}) collective-permute-start(f32[4,16,384]{2,1,0:T(8,128)S(1)} %get-tuple-element.31), channel_id=1, source_target_pairs={{1,0},{2,1},{3,2},{4,3},{5,4},{6,5},{7,6},{8,7},{9,8},{10,9},{11,1... | collective-permute-start | bytes 294920 | tf_op jit(solution)/shard_map/ppermute | solution.py:20
  10.5 1.9 %collective-permute-start.5 = (f32[4,16,384]{2,1,0:T(8,128)S(1)}, f32[4,16,384]{2,1,0:T(8,128)S(1)}, u32[]{:S(2)}, u32[]{:S(2)}) collective-permute-start(f32[4,16,384]{2,1,0:T(8,128)S(1)} %get-tuple-element.32), channel_id=1, source_target_pairs={{0,1},{1,2},{2,3},{3,4},{4,5},{5,6},{6,7},{7,8},{8,9},{9,10},{10,1... | collective-permute-start | bytes 294920 | tf_op jit(solution)/shard_map/ppermute | solution.py:17
  12.4 1.0 slice_bitcast_fusion.3
  13.4 2.4 %collective-permute-start = (f32[4,16,384]{2,1,0:T(8,128)S(1)}, f32[4,16,384]{2,1,0:T(8,128)S(1)}, u32[]{:S(2)}, u32[]{:S(2)}) collective-permute-start(f32[4,16,384]{2,1,0:T(8,128)S(1)} %get-tuple-element.35), channel_id=1, source_target_pairs={{1,0},{2,1},{3,2},{4,3},{5,4},{6,5},{7,6},{8,7},{9,8},{10,9},{11,1... | collective-permute-start | bytes 294920 | tf_op jit(solution)/shard_map/ppermute | solution.py:20
  15.8 3.2 %collective-permute-start.1 = (f32[4,16,384]{2,1,0:T(8,128)S(1)}, f32[4,16,384]{2,1,0:T(8,128)S(1)}, u32[]{:S(2)}, u32[]{:S(2)}) collective-permute-start(f32[4,16,384]{2,1,0:T(8,128)S(1)} %get-tuple-element.36), channel_id=1, source_target_pairs={{0,1},{1,2},{2,3},{3,4},{4,5},{5,6},{6,7},{7,8},{8,9},{9,10},{10,1... | collective-permute-start | bytes 294920 | tf_op jit(solution)/shard_map/ppermute | solution.py:17
  21.0 0.6 fusion.200
  22.9 0.7 and_reduce_fusion
  25.0 0.0 collective-permute-done
  25.0 0.0 collective-permute-done.1
  25.0 0.0 copy-start.1
  25.0 2.7 %fusion.100 = f32[32,16,384]{2,1,0:T(8,128)S(1)} fusion(f32[32,16,384]{2,1,0:T(8,128)S(1)} %bitcast.55, f32[4,16,384]{2,1,0:T(8,128)S(1)} %collective-permute-done.1, f32[4,16,384]{2,1,0:T(8,128)S(1)} %collective-permute-done), kind=kLoop, calls=%fused_computation.216 | loop fusion | flops 8847360 | bytes 1769472 | tf_op jit(solution)/shard_map/add | solution.py:41
  27.7 0.6 add.398
  29.0 0.1 add.401
  29.1 0.0 copy-start.11
  29.1 1.3 fusion.188
  30.5 1.9 %collective-permute-start.2 = (f32[4,16,384]{2,1,0:T(8,128)S(1)}, f32[4,16,384]{2,1,0:T(8,128)S(1)}, u32[]{:S(2)}, u32[]{:S(2)}) collective-permute-start(f32[4,16,384]{2,1,0:T(8,128)S(1)} %get-tuple-element.33), channel_id=1, source_target_pairs={{1,0},{2,1},{3,2},{4,3},{5,4},{6,5},{7,6},{8,7},{9,8},{10,9},{11,1... | collective-permute-start | bytes 294920 | tf_op jit(solution)/shard_map/ppermute | solution.py:20
  32.4 3.6 %collective-permute-start.3 = (f32[4,16,384]{2,1,0:T(8,128)S(1)}, f32[4,16,384]{2,1,0:T(8,128)S(1)}, u32[]{:S(2)}, u32[]{:S(2)}) collective-permute-start(f32[4,16,384]{2,1,0:T(8,128)S(1)} %get-tuple-element.34), channel_id=1, source_target_pairs={{0,1},{1,2},{2,3},{3,4},{4,5},{5,6},{6,7},{7,8},{8,9},{9,10},{10,1... | collective-permute-start | bytes 294920 | tf_op jit(solution)/shard_map/ppermute | solution.py:17
  36.1 1.8 %select_reduce_fusion = f32[1024]{0:T(1024)S(1)} fusion(f32[512,384]{1,0:T(8,128)S(1)} %bitcast.56, s32[1024]{0:T(1024)S(1)} %bitcast.66, s32[1024]{0:T(1024)S(1)} %bitcast.70), kind=kOutput, calls=%fused_computation.71 | convolution fusion | flops 2417622016 | bytes 798720 | tf_op jit(solution)/shard_map/dot_general | solution.py:68
  37.9 0.0 collective-permute-done.2
  37.9 0.0 collective-permute-done.3
  37.9 2.7 %fusion.76 = f32[32,16,384]{2,1,0:T(8,128)S(1)} fusion(f32[32,16,384]{2,1,0:T(8,128)S(1)} %fusion.188, f32[4,16,384]{2,1,0:T(8,128)S(1)} %collective-permute-done.3, f32[4,16,384]{2,1,0:T(8,128)S(1)} %collective-permute-done.2), kind=kLoop, calls=%fused_computation.192 | loop fusion | flops 8847360 | bytes 1769472 | tf_op jit(solution)/shard_map/add | solution.py:41
  40.6 0.6 add.427
  41.9 0.3 add.429
  42.2 0.0 copy-start.12
  42.2 0.2 multiply_add_fusion
  42.4 0.0 copy-start.4
  42.5 0.5 copy-done.12
  42.9 1.8 %select_reduce_fusion.1 = f32[1024]{0:T(1024)S(1)} fusion(f32[512,384]{1,0:T(8,128)S(1)} %bitcast.59, s32[1024]{0:T(1024)S(1)} %bitcast.67, s32[1024]{0:T(1024)S(1)} %bitcast.71), kind=kOutput, calls=%fused_computation.72 | convolution fusion | flops 2417622016 | bytes 798720 | tf_op jit(solution)/shard_map/dot_general | solution.py:68
  44.7 0.0 copy-start.2
  44.7 0.0 copy-start.5
  44.7 3.8 %fusion.2 = f32[512,384]{1,0:T(8,128)S(1)} fusion(f32[1024]{0:T(1024)S(1)} %sub.55, s32[1024]{0:T(1024)S(1)} %bitcast.68, s32[1024]{0:T(1024)S(1)} %bitcast.72), kind=kOutput, calls=%fused_computation.66 | convolution fusion | flops 2417360896 | bytes 798720 | tf_op jit(solution)/shard_map/dot_general | solution.py:73
  48.5 0.0 collective-permute-done.4
  48.5 0.0 collective-permute-done.5
  48.6 2.8 %fusion.52 = f32[32,16,384]{2,1,0:T(8,128)S(1)} fusion(f32[32,16,384]{2,1,0:T(8,128)S(1)} %copy-done.1, f32[32,16,384]{2,1,0:T(8,128)S(1)} %bitcast.61, f32[32,16,384]{2,1,0:T(8,128)S(1)} %bitcast.57, f32[4,16,384]{2,1,0:T(8,128)S(1)} %collective-permute-done.5, f32[4,16,384]{2,1,0:T(8,128)S(1)} %collective-permute-done.4, f32[1,32,16,384]{3,2,1,0:T(8,128)S(1)} %copy-done.5), kind=kLoop, calls=%fused_computation.168 | loop fusion | flops 9830400 | bytes 4128768 | tf_op jit(solution)/shard_map/add | solution.py:115
  51.4 1.9 %collective-permute-start.6 = (f32[4,16,384]{2,1,0:T(8,128)S(1)}, f32[4,16,384]{2,1,0:T(8,128)S(1)}, u32[]{:S(2)}, u32[]{:S(2)}) collective-permute-start(f32[4,16,384]{2,1,0:T(8,128)S(1)} %get-tuple-element.29), channel_id=1, source_target_pairs={{1,0},{2,1},{3,2},{4,3},{5,4},{6,5},{7,6},{8,7},{9,8},{10,9},{11,1... | collective-permute-start | bytes 294920 | tf_op jit(solution)/shard_map/ppermute | solution.py:20
  53.3 0.0 copy-start.3
  53.3 4.4 %collective-permute-start.7 = (f32[4,16,384]{2,1,0:T(8,128)S(1)}, f32[4,16,384]{2,1,0:T(8,128)S(1)}, u32[]{:S(2)}, u32[]{:S(2)}) collective-permute-start(f32[4,16,384]{2,1,0:T(8,128)S(1)} %get-tuple-element.30), channel_id=1, source_target_pairs={{0,1},{1,2},{2,3},{3,4},{4,5},{5,6},{6,7},{7,8},{8,9},{9,10},{10,1... | collective-permute-start | bytes 294920 | tf_op jit(solution)/shard_map/ppermute | solution.py:17
  57.8 3.8 %fusion = f32[512,384]{1,0:T(8,128)S(1)} fusion(f32[1024]{0:T(1024)S(1)} %sub.57, s32[1024]{0:T(1024)S(1)} %bitcast.69, s32[1024]{0:T(1024)S(1)} %bitcast.73), kind=kOutput, calls=%fused_computation.64 | convolution fusion | flops 2417360896 | bytes 798720 | tf_op jit(solution)/shard_map/dot_general | solution.py:73
  61.6 0.0 collective-permute-done.6
  61.6 3.9 %fusion.191 = (f32[32,1,16,384]{3,2,1,0:T(8,128)S(1)}, f32[32,16,384]{2,1,0:T(8,128)}) fusion(f32[1,32,16,384]{3,2,1,0:T(8,128)S(1)} %copy-done.3, f32[32,16,384]{2,1,0:T(8,128)S(1)} %fusion.52, f32[32,16,384]{2,1,0:T(8,128)S(1)} %multiply_add_fusion, f32[32,16,384]{2,1,0:T(8,128)S(1)} %fusion.188, f32[1,32,16,384]{3,2,1,0:T(8,128)S(1)} %copy-done, ...), kind=kLoop, calls=%fused_computation.318 | loop fusion | flops 11599872 | bytes 8060928 | tf_op jit(solution)/shard_map/reshape | solution.py:81
  65.5 34.8 %all_to_all.10 = f32[32,1,16,384]{3,2,1,0:T(8,128)S(1)} all-to-all(f32[32,1,16,384]{3,2,1,0:T(8,128)S(1)} %get-tuple-element.27), channel_id=1, replica_groups=mesh['shot'=32,'dom'=16] {'shot'}, dimensions={0} | all-to-all | bytes 1572864 | tf_op jit(solution)/shard_map/all_to_all | solution.py:82
  100.3 0.1 reduce_sum.29
  100.4 0.1 broadcast_in_dim.13
  100.4 32.5 %all_to_all.11 = f32[32,1,16,384]{3,2,1,0:T(8,128)S(1)} all-to-all(f32[32,1,16,384]{3,2,1,0:T(8,128)S(1)} %broadcast_in_dim.13), channel_id=1, replica_groups=mesh['shot'=32,'dom'=16] {'shot'}, dimensions={0} | all-to-all | bytes 1572864 | tf_op jit(solution)/shard_map/all_to_all | solution.py:84
  132.9 0.9 copy.26
  (23 shorter events, 0.1 us)
Async XLA Ops:
  0.6 22.3 %copy-start.10 = (s32[3]{0:T(128)S(1)}, s32[3]{0:T(128)}, u32[]{:S(2)}) copy-start(s32[3]{0:T(128)} %constant.80.clone.1) | copy-start | bytes 40
  0.6 24.3 %copy-start = (f32[1,32,16,384]{3,2,1,0:T(8,128)S(1)}, f32[1,32,16,384]{3,2,1,0:T(8,128)}, u32[]{:S(2)}) copy-start(f32[1,32,16,384]{3,2,1,0:T(8,128)} %param.19) | copy-start | bytes 2359300
  0.7 20.3 %copy-start.9 = (f32[1,2]{1,0:T(1,128)S(1)}, f32[1,2]{1,0:T(1,128)}, u32[]{:S(2)}) copy-start(f32[1,2]{1,0:T(1,128)} %param.25) | copy-start | bytes 28
  0.7 22.2 %copy-start.6 = (f32[1,2,1024]{2,1,0:T(2,128)S(1)}, f32[1,2,1024]{2,1,0:T(2,128)}, u32[]{:S(2)}) copy-start(f32[1,2,1024]{2,1,0:T(2,128)} %param.29) | copy-start | bytes 24580
  0.7 22.2 %copy-start.8 = (s32[1,1024]{1,0:T(1,128)S(1)}, s32[1,1024]{1,0:T(1,128)}, u32[]{:S(2)}) copy-start(s32[1,1024]{1,0:T(1,128)} %param.27) | copy-start | bytes 12292
  0.7 22.2 %copy-start.7 = (s32[1,1024]{1,0:T(1,128)S(1)}, s32[1,1024]{1,0:T(1,128)}, u32[]{:S(2)}) copy-start(s32[1,1024]{1,0:T(1,128)} %param.26) | copy-start | bytes 12292
  1.7 46.8 %collective-permute-start.4 = (f32[4,16,384]{2,1,0:T(8,128)S(1)}, f32[4,16,384]{2,1,0:T(8,128)S(1)}, u32[]{:S(2)}, u32[]{:S(2)}) collective-permute-start(f32[4,16,384]{2,1,0:T(8,128)S(1)} %get-tuple-element.31), channel_id=1, source_target_pairs={{1,0},{2,1},{3,2},{4,3},{5,4},{6,5},{7,6},{8,7},{9,8},{10,9},{11,1... | collective-permute-start | bytes 294920 | tf_op jit(solution)/shard_map/ppermute | solution.py:20
  10.5 38.0 %collective-permute-start.5 = (f32[4,16,384]{2,1,0:T(8,128)S(1)}, f32[4,16,384]{2,1,0:T(8,128)S(1)}, u32[]{:S(2)}, u32[]{:S(2)}) collective-permute-start(f32[4,16,384]{2,1,0:T(8,128)S(1)} %get-tuple-element.32), channel_id=1, source_target_pairs={{0,1},{1,2},{2,3},{3,4},{4,5},{5,6},{6,7},{7,8},{8,9},{9,10},{10,1... | collective-permute-start | bytes 294920 | tf_op jit(solution)/shard_map/ppermute | solution.py:17
  13.4 11.6 %collective-permute-start = (f32[4,16,384]{2,1,0:T(8,128)S(1)}, f32[4,16,384]{2,1,0:T(8,128)S(1)}, u32[]{:S(2)}, u32[]{:S(2)}) collective-permute-start(f32[4,16,384]{2,1,0:T(8,128)S(1)} %get-tuple-element.35), channel_id=1, source_target_pairs={{1,0},{2,1},{3,2},{4,3},{5,4},{6,5},{7,6},{8,7},{9,8},{10,9},{11,1... | collective-permute-start | bytes 294920 | tf_op jit(solution)/shard_map/ppermute | solution.py:20
  15.8 9.1 %collective-permute-start.1 = (f32[4,16,384]{2,1,0:T(8,128)S(1)}, f32[4,16,384]{2,1,0:T(8,128)S(1)}, u32[]{:S(2)}, u32[]{:S(2)}) collective-permute-start(f32[4,16,384]{2,1,0:T(8,128)S(1)} %get-tuple-element.36), channel_id=1, source_target_pairs={{0,1},{1,2},{2,3},{3,4},{4,5},{5,6},{6,7},{7,8},{8,9},{9,10},{10,1... | collective-permute-start | bytes 294920 | tf_op jit(solution)/shard_map/ppermute | solution.py:17
  25.0 4.1 %copy-start.1 = (f32[32,16,384]{2,1,0:T(8,128)S(1)}, f32[32,16,384]{2,1,0:T(8,128)}, u32[]{:S(2)}) copy-start(f32[32,16,384]{2,1,0:T(8,128)} %param.17) | copy-start | bytes 2359300
  29.1 7.0 %copy-start.11 = (s32[1,1024]{1,0:T(1,128)S(1)}, s32[1,1024]{1,0:T(1,128)}, u32[]{:S(2)}) copy-start(s32[1,1024]{1,0:T(1,128)} %param.28) | copy-start | bytes 12292
  30.5 7.4 %collective-permute-start.2 = (f32[4,16,384]{2,1,0:T(8,128)S(1)}, f32[4,16,384]{2,1,0:T(8,128)S(1)}, u32[]{:S(2)}, u32[]{:S(2)}) collective-permute-start(f32[4,16,384]{2,1,0:T(8,128)S(1)} %get-tuple-element.33), channel_id=1, source_target_pairs={{1,0},{2,1},{3,2},{4,3},{5,4},{6,5},{7,6},{8,7},{9,8},{10,9},{11,1... | collective-permute-start | bytes 294920 | tf_op jit(solution)/shard_map/ppermute | solution.py:20
  32.4 5.5 %collective-permute-start.3 = (f32[4,16,384]{2,1,0:T(8,128)S(1)}, f32[4,16,384]{2,1,0:T(8,128)S(1)}, u32[]{:S(2)}, u32[]{:S(2)}) collective-permute-start(f32[4,16,384]{2,1,0:T(8,128)S(1)} %get-tuple-element.34), channel_id=1, source_target_pairs={{0,1},{1,2},{2,3},{3,4},{4,5},{5,6},{6,7},{7,8},{8,9},{9,10},{10,1... | collective-permute-start | bytes 294920 | tf_op jit(solution)/shard_map/ppermute | solution.py:17
  42.2 0.7 copy-start.12
  42.4 19.2 %copy-start.4 = (f32[32,16,384]{2,1,0:T(8,128)}, f32[32,16,384]{2,1,0:T(8,128)S(1)}, u32[]{:S(2)}) copy-start(f32[32,16,384]{2,1,0:T(8,128)S(1)} %multiply_add_fusion) | copy-start | bytes 2359300
  44.7 3.8 %copy-start.2 = (f32[1,32,16,384]{3,2,1,0:T(8,128)S(1)}, f32[1,32,16,384]{3,2,1,0:T(8,128)}, u32[]{:S(2)}) copy-start(f32[1,32,16,384]{3,2,1,0:T(8,128)} %param.21) | copy-start | bytes 2359300
  44.7 3.8 %copy-start.5 = (f32[1,32,16,384]{3,2,1,0:T(8,128)S(1)}, f32[1,32,16,384]{3,2,1,0:T(8,128)}, u32[]{:S(2)}) copy-start(f32[1,32,16,384]{3,2,1,0:T(8,128)} %param.20) | copy-start | bytes 2359300
  51.4 10.2 %collective-permute-start.6 = (f32[4,16,384]{2,1,0:T(8,128)S(1)}, f32[4,16,384]{2,1,0:T(8,128)S(1)}, u32[]{:S(2)}, u32[]{:S(2)}) collective-permute-start(f32[4,16,384]{2,1,0:T(8,128)S(1)} %get-tuple-element.29), channel_id=1, source_target_pairs={{1,0},{2,1},{3,2},{4,3},{5,4},{6,5},{7,6},{8,7},{9,8},{10,9},{11,1... | collective-permute-start | bytes 294920 | tf_op jit(solution)/shard_map/ppermute | solution.py:20
  53.3 8.3 %copy-start.3 = (f32[1,32,16,384]{3,2,1,0:T(8,128)S(1)}, f32[1,32,16,384]{3,2,1,0:T(8,128)}, u32[]{:S(2)}) copy-start(f32[1,32,16,384]{3,2,1,0:T(8,128)} %param.18) | copy-start | bytes 2359300
  53.3 8.2 %collective-permute-start.7 = (f32[4,16,384]{2,1,0:T(8,128)S(1)}, f32[4,16,384]{2,1,0:T(8,128)S(1)}, u32[]{:S(2)}, u32[]{:S(2)}) collective-permute-start(f32[4,16,384]{2,1,0:T(8,128)S(1)} %get-tuple-element.30), channel_id=1, source_target_pairs={{0,1},{1,2},{2,3},{3,4},{4,5},{5,6},{6,7},{7,8},{8,9},{9,10},{10,1... | collective-permute-start | bytes 294920 | tf_op jit(solution)/shard_map/ppermute | solution.py:17

commit v3 on v2

--- a/solution.py
+++ b/solution.py
@@ -20,6 +20,21 @@
         high = lax.ppermute(lax.slice_in_dim(block, 0, width, axis=dim), axis, backward)
         block = jnp.concatenate([low, block, high], axis=dim)
     return block
+
+
+def wide_halo(fields, widths):
+    count = lax.axis_size("dom")
+    forward = [(i, i + 1) for i in range(count - 1)]
+    backward = [(target, source) for source, target in forward]
+    tails = jnp.concatenate([f[f.shape[0] - w :] for f, w in zip(fields, widths)])
+    heads = jnp.concatenate([f[:w] for f, w in zip(fields, widths)])
+    lows = lax.ppermute(tails, "dom", forward)
+    highs = lax.ppermute(heads, "dom", backward)
+    out, at = [], 0
+    for f, w in zip(fields, widths):
+        out.append(jnp.concatenate([lows[at : at + w], f, highs[at : at + w]]))
+        at += w
+    return out
 
 
 def laplace_core(extended):
@@ -110,27 +125,40 @@
     ryc = receiver_ycell[0]
     rzc = receiver_zcell[0]
 
-    def advance(current, before, sources):
-        extended = with_halo(current, (("dom", 0),), R)
-        return 2.0 * current - before + coefficient * (laplace_core(extended) + sources)
+    widths = (3 * R, 2 * R, 2 * R, 2 * R, R)
+    fields = (recent, older, coefficient, adj_now, later)
+    recent_x, older_x, coef_x, adj_now_x, later_x = wide_halo(fields, widths)
 
-    fwd_two = advance(
-        recent,
-        older,
-        point_grid(shape, source_xcell, source_ycell, source_zcell, amplitude[0, 0:1], base),
+    def advance(current, before, coef, sources):
+        return 2.0 * current[R:-R] - before + coef * (laplace_core(current) + sources)
+
+    def region(margin):
+        return (count + 2 * margin,) + shape[1:]
+
+    def source_grid(margin, step):
+        return point_grid(
+            region(margin), source_xcell, source_ycell, source_zcell,
+            amplitude[0, step : step + 1], base - margin,
+        )
+
+    fwd_two_x = advance(recent_x, older_x, coef_x, source_grid(2 * R, 0))
+    fwd_three_x = advance(fwd_two_x, recent_x[2 * R : -2 * R], coef_x[R:-R], source_grid(R, 1))
+    rows_x, cols = selectors(region(R), rxc, ryc, rzc, base - R)
+    rows = rows_x[:, R * shape[1] : (R + count) * shape[1]]
+    fwd_two = fwd_two_x[2 * R : -2 * R]
+    fwd_three = fwd_three_x[R:-R]
+    resid_two = sample(fwd_two, rows, cols) - observed[0, 0]
+    resid_three = sample(fwd_three_x, rows_x, cols) - observed[0, 1]
+    adj_two_x = advance(
+        adj_now_x, later_x, coef_x[R:-R], receiver_grid(region(R), rows_x, cols, resid_three)
     )
-    fwd_three = advance(
-        fwd_two,
-        recent,
-        point_grid(shape, source_xcell, source_ycell, source_zcell, amplitude[0, 1:2], base),
+    adj_one = advance(
+        adj_two_x, adj_now_x[2 * R : -2 * R], coefficient, receiver_grid(shape, rows, cols, resid_two)
     )
-    rows, cols = selectors(shape, rxc, ryc, rzc, base)
-    resid_two = sample(fwd_two, rows, cols) - observed[0, 0]
-    resid_three = sample(fwd_three, rows, cols) - observed[0, 1]
-    adj_two = advance(adj_now, later, receiver_grid(shape, rows, cols, resid_three))
-    late_term = adj_two * (fwd_three - 2.0 * fwd_two + recent)
-    adj_one = advance(adj_two, adj_now, receiver_grid(shape, rows, cols, resid_two))
-    early_term = adj_one * (fwd_two - 2.0 * recent + older)
+    adj_two = adj_two_x[R:-R]
+    recent_own = recent_x[3 * R : -3 * R]
+    late_term = adj_two * (fwd_three - 2.0 * fwd_two + recent_own)
+    early_term = adj_one * (fwd_two - 2.0 * recent_own + older)
     gradient = shot_sum(early_term + late_term)
     return (fwd_three[None], adj_one[None], gradient)
 

time: 136 us -> 152 us (1.12)
  the two profiles are of different devices: /device:TPU:1 before, /device:TPU:4 now
where the time goes in v3:
time: 152 us; the launch traced here: 151 us
  blocking collectives  75 us (49%)
  local copies, waits for them, and re-layouts  19.6 us (13%)
  other arithmetic  19.1 us (13%)
  matrix products  13.3 us (9%)
  waiting for transfers between devices  10.9 us (7%)
  between operations  6.95 us (5%)
  starting transfers between devices  6.45 us (4%)
    all_to_all x1, blocking collectives, shot_sum(): mine = jnp.sum(lax.all_to_all(pieces, 'shot', 0, 0, tiled=False), axis=0)  42.3 us
    all_to_all x1, blocking collectives, shot_sum(): return lax.all_to_all(spread, 'shot', 0, 0, tiled=False).reshape(term.shape)  32.7 us
    ppermute x1, waiting for transfers between devices, wide_halo(): lows = lax.ppermute(tails, 'dom', forward)  9.69 us
    dot_general x2, matrix products, receiver_grid(): lax.dot_general(rows * values[:, None], cols, (((0,), (0,)), ((), ())), p...  8.87 us
    unnamed x61, local copies, waits for them, and re-layouts  8.43 us
    add x2, other arithmetic, laplace_core(): total + weight * (padded[:, R:R + width_y, R + offset:R + offset + width_...  5.1 us
    add x2, other arithmetic, advance(): 2.0 * current[R:-R] - before + coef * (laplace_core(current) + sources)  4.86 us
    slice x7, local copies, waits for them, and re-layouts, wide_halo(): out.append(jnp.concatenate([lows[at:at + w], f, highs[at:at + w]]))  4.8 us
  transfers between devices with their start and end apart: 2, of which 2 were waited for; matrix products, arithmetic and copies ran while one was open for 2% of the time, Pallas kernels for 0%

profile of v3, /device:TPU:4, one launch (start us, length us, event | category | flops | bytes accessed | tf_op | source)
XLA Modules:
  0.0 151.3 jit_solution(8355702350223988014)
XLA Ops:
  0.6 0.0 copy-start.7
  0.7 2.1 %bitcast_dynamic-update-slice_fusion.1 = (f32[40,16,384]{2,1,0:T(8,128)}, f32[40,16,384]{2,1,0:T(8,128)}) fusion(f32[1,32,16,384]{3,2,1,0:T(8,128)} %param.19), kind=kLoop, calls=%fused_computation.244 | loop fusion | bytes 1179648
  2.7 0.8 bitcast_dynamic-update-slice_fusion.5
  3.5 0.8 slice_dynamic-update-slice_fusion.1
  4.3 0.8 bitcast_dynamic-update-slice_fusion.4
  5.1 1.7 %bitcast_dynamic-update-slice_fusion.7 = (f32[40,16,384]{2,1,0:T(8,128)}, f32[40,16,384]{2,1,0:T(8,128)}) fusion(f32[40,16,384]{2,1,0:T(8,128)} %get-tuple-element.40, f32[1,32,16,384]{3,2,1,0:T(8,128)} %param.20, f32[40,16,384]{2,1,0:T(8,128)} %get-tuple-element.41), kind=kLoop, calls=%fused_computation.252 | loop fusion | bytes 393216 | tf_op jit(solution)/shard_map/concatenate | solution.py:29
  6.8 1.9 %collective-permute-start = (f32[40,16,384]{2,1,0:T(8,128)}, f32[40,16,384]{2,1,0:T(8,128)S(1)}, u32[]{:S(2)}, u32[]{:S(2)}) collective-permute-start(f32[40,16,384]{2,1,0:T(8,128)} %get-tuple-element.38), channel_id=1, source_target_pairs={{0,1},{1,2},{2,3},{3,4},{4,5},{5,6},{6,7},{7,8},{8,9},{9,10},{10,1... | collective-permute-start | bytes 2949128 | tf_op jit(solution)/shard_map/ppermute | solution.py:31
  8.7 4.5 %collective-permute-start.1 = (f32[40,16,384]{2,1,0:T(8,128)}, f32[40,16,384]{2,1,0:T(8,128)}, u32[]{:S(2)}, u32[]{:S(2)}) collective-permute-start(f32[40,16,384]{2,1,0:T(8,128)} %get-tuple-element.39), channel_id=1, source_target_pairs={{1,0},{2,1},{3,2},{4,3},{5,4},{6,5},{7,6},{8,7},{9,8},{10,9},{11,1... | collective-permute-start | bytes 2949128 | tf_op jit(solution)/shard_map/ppermute | solution.py:32
  15.3 0.6 fusion.159
  17.2 0.7 and_reduce_fusion.1
  18.5 0.7 and_reduce_fusion
  20.0 1.3 iota_compare_fusion
  21.3 9.7 %collective-permute-done = f32[40,16,384]{2,1,0:T(8,128)S(1)} collective-permute-done((f32[40,16,384]{2,1,0:T(8,128)}, f32[40,16,384]{2,1,0:T(8,128)S(1)}, u32[]{:S(2)}, u32[]{:S(2)}) %collective-permute-start) | collective-permute-done | bytes 983072 | tf_op jit(solution)/shard_map/ppermute | solution.py:31
  31.0 1.2 collective-permute-done.1
  32.2 1.0 slice.600
  33.2 0.1 pad_maximum_fusion
  33.3 0.1 slice.601
  33.4 2.8 %fusion.25 = f32[48,16,384]{2,1,0:T(8,128)S(1)} fusion(f32[48,16,384]{2,1,0:T(8,128)S(1)} %slice.601, f32[56,16,384]{2,1,0:T(8,128)S(1)} %pad_maximum_fusion), kind=kLoop, calls=%fused_computation.92 | loop fusion | flops 10911744 | bytes 11796480 | tf_op jit(solution)/shard_map/add | solution.py:56
  36.2 0.6 add.406
  37.4 0.1 add.409
  37.6 1.6 %fusion.156 = (f32[8,16,384]{2,1,0:T(8,128)S(1)}, f32[8,16,384]{2,1,0:T(8,128)S(1)}, f32[8,16,384]{2,1,0:T(8,128)S(1)}) fusion(f32[40,16,384]{2,1,0:T(8,128)} %copy-done.18), kind=kLoop, calls=%fused_computation.258 | loop fusion | bytes 1179648 | tf_op jit(solution)/shard_map/slice | solution.py:35
  39.2 1.2 fusion.157
  40.4 3.1 %pad_maximum_fusion.1 = (f32[48,16,384]{2,1,0:T(8,128)}, f32[48,16,384]{2,1,0:T(8,128)S(1)}, f32[48,16,384]{2,1,0:T(8,128)}) fusion(f32[8,16,384]{2,1,0:T(8,128)S(1)} %get-tuple-element.36, f32[32,16,384]{2,1,0:T(8,128)S(1)} %copy-done.11, f32[8,16,384]{2,1,0:T(8,128)S(1)} %get-tuple-element.33, f32[48,16,384]{2,1,0:T(8,128)} %copy-done.13, ...), kind=kLoop, calls=%fused_computation.118 | loop fusion | flops 2949120 | bytes 9437184 | tf_op jit(solution)/shard_map/concatenate | solution.py:35
  43.6 0.1 slice.614
  43.6 0.9 slice.647
  44.6 2.3 %fusion.60 = f32[40,16,384]{2,1,0:T(8,128)S(1)} fusion(f32[40,16,384]{2,1,0:T(8,128)S(1)} %slice.614, f32[48,16,384]{2,1,0:T(8,128)S(1)} %get-tuple-element.30), kind=kLoop, calls=%fused_computation.134 | loop fusion | flops 9093120 | bytes 9830400 | tf_op jit(solution)/shard_map/add | solution.py:56
  46.9 0.9 copy-done.14
  47.8 0.6 add.435
  49.0 1.5 add.438
  50.5 1.8 %fusion.114 = f32[40,16,384]{2,1,0:T(8,128)S(1)} fusion(f32[56,16,384]{2,1,0:T(8,128)S(1)} %pad_maximum_fusion, f32[40,16,384]{2,1,0:T(8,128)} %add.438, f32[48,16,384]{2,1,0:T(8,128)} %get-tuple-element.29, f32[48,16,384]{2,1,0:T(8,128)S(1)} %get-tuple-element.30), kind=kLoop, calls=%fused_computation.196 | loop fusion | flops 983040 | bytes 4915200 | tf_op jit(solution)/shard_map/add | solution.py:133
  52.2 2.4 %select_reduce_fusion.1 = f32[1024]{0:T(1024)S(1)} fusion(f32[640,384]{1,0:T(8,128)S(1)} %bitcast.58, s32[1024]{0:T(1024)S(1)} %bitcast.66, s32[1024]{0:T(1024)S(1)} %bitcast.70), kind=kOutput, calls=%fused_computation.73 | convolution fusion | flops 3021732864 | bytes 995328 | tf_op jit(solution)/shard_map/dot_general | solution.py:83
  54.7 4.7 %fusion = f32[640,384]{1,0:T(8,128)S(1)} fusion(f32[1024]{0:T(1024)S(1)} %sub.70, s32[1024]{0:T(1024)S(1)} %bitcast.67, s32[1024]{0:T(1024)S(1)} %bitcast.71), kind=kOutput, calls=%fused_computation.64 | convolution fusion | flops 3021602816 | bytes 995328 | tf_op jit(solution)/shard_map/dot_general | solution.py:88
  59.4 0.1 slice.628
  59.5 1.0 slice.630
  60.5 0.2 copy-done.4
  60.7 0.0 copy-done.16
  60.7 0.3 copy-done.17
  60.9 3.1 %fusion.90 = f32[40,16,384]{2,1,0:T(8,128)S(1)} fusion(f32[40,16,384]{2,1,0:T(8,128)S(1)} %bitcast.61, f32[40,16,384]{2,1,0:T(8,128)S(1)} %slice.628, f32[48,16,384]{2,1,0:T(8,128)S(1)} %copy-done.2, f32[4,16,384]{2,1,0:T(8,128)S(1)} %slice.630, f32[32,16,384]{2,1,0:T(8,128)S(1)} %bitcast.60, f32[4,16,384]{2,1,0:T(8,128)S(1)} %slice-done.1, ...), kind=kLoop, calls=%fused_computation.164 | loop fusion | flops 11304960 | bytes 11993088 | tf_op jit(solution)/shard_map/add | solution.py:133
  64.1 1.5 copy-done.19
  65.6 0.2 copy-done.20
  65.8 2.1 %select_reduce_fusion = f32[1024]{0:T(1024)S(1)} fusion(f32[512,384]{1,0:T(8,128)S(1)} %bitcast.62, pred[1024,640]{1,0:T(32,128)(4,1)S(1)} %copy-done.20, s32[1024]{0:T(1024)S(1)} %bitcast.72), kind=kOutput, calls=%fused_computation.72 | convolution fusion | flops 2417097728 | bytes 1318912 | tf_op jit(solution)/shard_map/dot_general | solution.py:83
  67.9 4.2 %fusion.2 = f32[512,384]{1,0:T(8,128)S(1)} fusion(pred[1024,640]{1,0:T(32,128)(4,1)S(1)} %copy-done.20, f32[1024]{0:T(1024)S(1)} %sub.72, s32[1024]{0:T(1024)S(1)} %bitcast.73), kind=kOutput, calls=%fused_computation.67 | convolution fusion | flops 2416836608 | bytes 1318912 | tf_op jit(solution)/shard_map/dot_general | solution.py:88
  72.2 3.1 %add_bitcast_fusion = (f32[32,1,16,384]{3,2,1,0:T(8,128)S(1)}, f32[32,16,384]{2,1,0:T(8,128)}, f32[1,32,16,384]{3,2,1,0:T(8,128)}) fusion(f32[40,16,384]{2,1,0:T(8,128)S(1)} %fusion.114, f32[1,32,16,384]{3,2,1,0:T(8,128)S(1)} %copy-done.9, f32[1,32,16,384]{3,2,1,0:T(8,128)S(1)} %copy-done.6, f32[48,16,384]{2,1,0:T(8,128)S(1)} %get-tuple-element.30, ...), kind=kLoop, calls=%fused_computation.239 | loop fusion | flops 10027008 | bytes 15728640 | tf_op jit(solution)/shard_map/reshape | solution.py:96
  75.3 42.3 %all_to_all.10 = f32[32,1,16,384]{3,2,1,0:T(8,128)S(1)} all-to-all(f32[32,1,16,384]{3,2,1,0:T(8,128)S(1)} %get-tuple-element.27), channel_id=1, replica_groups=mesh['shot'=32,'dom'=16] {'shot'}, dimensions={0} | all-to-all | bytes 1572864 | tf_op jit(solution)/shard_map/all_to_all | solution.py:97
  117.6 0.1 reduce_sum.29
  117.7 0.1 broadcast_in_dim.13
  117.7 32.7 %all_to_all.11 = f32[32,1,16,384]{3,2,1,0:T(8,128)S(1)} all-to-all(f32[32,1,16,384]{3,2,1,0:T(8,128)S(1)} %broadcast_in_dim.13), channel_id=1, replica_groups=mesh['shot'=32,'dom'=16] {'shot'}, dimensions={0} | all-to-all | bytes 1572864 | tf_op jit(solution)/shard_map/all_to_all | solution.py:99
  150.4 0.9 copy.35
  (58 shorter events, 0.2 us)
Async XLA Ops:
  0.6 2.1 %copy-start.7 = (f32[1,32,16,384]{3,2,1,0:T(8,128)S(1)}, f32[1,32,16,384]{3,2,1,0:T(8,128)}, u32[]{:S(2)}) copy-start(f32[1,32,16,384]{3,2,1,0:T(8,128)} %param.18) | copy-start | bytes 2359300
  0.6 2.9 %copy-start.10 = (f32[32,16,384]{2,1,0:T(8,128)S(1)}, f32[32,16,384]{2,1,0:T(8,128)}, u32[]{:S(2)}) copy-start(f32[32,16,384]{2,1,0:T(8,128)} %param.17) | copy-start | bytes 2359300
  0.7 3.7 %copy-start.3 = (f32[1,32,16,384]{3,2,1,0:T(8,128)S(1)}, f32[1,32,16,384]{3,2,1,0:T(8,128)}, u32[]{:S(2)}) copy-start(f32[1,32,16,384]{3,2,1,0:T(8,128)} %param.21) | copy-start | bytes 2359300
  3.5 11.8 %copy-start.24 = (f32[1,2]{1,0:T(1,128)S(1)}, f32[1,2]{1,0:T(1,128)}, u32[]{:S(2)}) copy-start(f32[1,2]{1,0:T(1,128)} %param.25) | copy-start | bytes 28
  3.5 13.7 %copy-start.26 = (s32[3]{0:T(128)S(1)}, s32[3]{0:T(128)}, u32[]{:S(2)}) copy-start(s32[3]{0:T(128)} %constant.107.clone.1) | copy-start | bytes 40
  3.5 15.0 %copy-start.25 = (s32[3]{0:T(128)S(1)}, s32[3]{0:T(128)}, u32[]{:S(2)}) copy-start(s32[3]{0:T(128)} %constant.114.clone.1) | copy-start | bytes 40
  3.5 16.4 %copy-start.22 = (s32[1,1024]{1,0:T(1,128)S(1)}, s32[1,1024]{1,0:T(1,128)}, u32[]{:S(2)}) copy-start(s32[1,1024]{1,0:T(1,128)} %param.26) | copy-start | bytes 12292
  3.5 16.4 %copy-start.23 = (s32[1,1024]{1,0:T(1,128)S(1)}, s32[1,1024]{1,0:T(1,128)}, u32[]{:S(2)}) copy-start(s32[1,1024]{1,0:T(1,128)} %param.27) | copy-start | bytes 12292
  3.5 16.4 %copy-start.21 = (f32[1,2,1024]{2,1,0:T(2,128)S(1)}, f32[1,2,1024]{2,1,0:T(2,128)}, u32[]{:S(2)}) copy-start(f32[1,2,1024]{2,1,0:T(2,128)} %param.29) | copy-start | bytes 24580
  5.1 28.1 %copy-start.5 = (f32[1,32,16,384]{3,2,1,0:T(8,128)S(1)}, f32[1,32,16,384]{3,2,1,0:T(8,128)}, u32[]{:S(2)}) copy-start(f32[1,32,16,384]{3,2,1,0:T(8,128)} %param.19) | copy-start | bytes 2359300
  6.8 24.1 %collective-permute-start = (f32[40,16,384]{2,1,0:T(8,128)}, f32[40,16,384]{2,1,0:T(8,128)S(1)}, u32[]{:S(2)}, u32[]{:S(2)}) collective-permute-start(f32[40,16,384]{2,1,0:T(8,128)} %get-tuple-element.38), channel_id=1, source_target_pairs={{0,1},{1,2},{2,3},{3,4},{4,5},{5,6},{6,7},{7,8},{8,9},{9,10},{10,1... | collective-permute-start | bytes 2949128 | tf_op jit(solution)/shard_map/ppermute | solution.py:31
  8.7 23.4 %collective-permute-start.1 = (f32[40,16,384]{2,1,0:T(8,128)}, f32[40,16,384]{2,1,0:T(8,128)}, u32[]{:S(2)}, u32[]{:S(2)}) collective-permute-start(f32[40,16,384]{2,1,0:T(8,128)} %get-tuple-element.39), channel_id=1, source_target_pairs={{1,0},{2,1},{3,2},{4,3},{5,4},{6,5},{7,6},{8,7},{9,8},{10,9},{11,1... | collective-permute-start | bytes 2949128 | tf_op jit(solution)/shard_map/ppermute | solution.py:32
  30.9 2.2 %copy-start.18 = (f32[40,16,384]{2,1,0:T(8,128)}, f32[40,16,384]{2,1,0:T(8,128)S(1)}, u32[]{:S(2)}) copy-start(f32[40,16,384]{2,1,0:T(8,128)S(1)} %collective-permute-done) | copy-start | bytes 2949124
  37.6 2.8 %copy-start.13 = (f32[48,16,384]{2,1,0:T(8,128)}, f32[48,16,384]{2,1,0:T(8,128)S(1)}, u32[]{:S(2)}) copy-start(f32[48,16,384]{2,1,0:T(8,128)S(1)} %add.409) | copy-start | bytes 3538948
  37.6 2.8 %copy-start.8 = (f32[1,32,16,384]{3,2,1,0:T(8,128)S(1)}, f32[1,32,16,384]{3,2,1,0:T(8,128)}, u32[]{:S(2)}) copy-start(f32[1,32,16,384]{3,2,1,0:T(8,128)} %param.18) | copy-start | bytes 2359300
  37.6 2.8 %copy-start.11 = (f32[32,16,384]{2,1,0:T(8,128)S(1)}, f32[32,16,384]{2,1,0:T(8,128)}, u32[]{:S(2)}) copy-start(f32[32,16,384]{2,1,0:T(8,128)} %param.17) | copy-start | bytes 2359300
  40.4 3.2 %copy-start.15 = (f32[8,16,384]{2,1,0:T(8,128)}, f32[8,16,384]{2,1,0:T(8,128)S(1)}, u32[]{:S(2)}) copy-start(f32[8,16,384]{2,1,0:T(8,128)S(1)} %get-tuple-element.35) | copy-start | bytes 589828
  46.9 1.0 copy-start.14
  50.5 1.8 %copy-start.27 = (s32[1,1024]{1,0:T(1,128)S(1)}, s32[1,1024]{1,0:T(1,128)}, u32[]{:S(2)}) copy-start(s32[1,1024]{1,0:T(1,128)} %param.28) | copy-start | bytes 12292
  54.7 4.7 %copy-start.2 = (f32[48,16,384]{2,1,0:T(8,128)S(1)}, f32[48,16,384]{2,1,0:T(8,128)}, u32[]{:S(2)}) copy-start(f32[48,16,384]{2,1,0:T(8,128)} %get-tuple-element.52) | copy-start | bytes 3538948
  59.4 1.3 copy-start.4
  59.4 1.3 copy-start.16
  59.4 1.6 %copy-start.17 = (f32[1,32,16,384]{3,2,1,0:T(8,128)S(1)}, f32[1,32,16,384]{3,2,1,0:T(8,128)}, u32[]{:S(2)}) copy-start(f32[1,32,16,384]{3,2,1,0:T(8,128)} %param.20) | copy-start | bytes 2359300
  59.4 1.6 %slice-start.1 = ((f32[40,16,384]{2,1,0:T(8,128)}), f32[4,16,384]{2,1,0:T(8,128)S(1)}, s32[]{:S(2)}) async-start(f32[40,16,384]{2,1,0:T(8,128)} %copy-done.18), calls=%async_computation.3 | async-start | bytes 196608 | tf_op jit(solution)/shard_map/slice | solution.py:35
  64.1 3.8 %copy-start = (f32[40,16,384]{2,1,0:T(8,128)}, f32[40,16,384]{2,1,0:T(8,128)S(1)}, u32[]{:S(2)}) copy-start(f32[40,16,384]{2,1,0:T(8,128)S(1)} %fusion.90) | copy-start | bytes 2949124
  64.1 1.5 copy-start.19
  64.1 1.7 %copy-start.20 = (pred[1024,640]{1,0:T(32,128)(4,1)S(1)}, pred[1024,640]{1,0:T(32,128)(4,1)}, u32[]{:S(2)}) copy-start(pred[1024,640]{1,0:T(32,128)(4,1)} %iota_compare_fusion) | copy-start | bytes 1966084
  67.8 4.3 %copy-start.1 = (f32[40,16,384]{2,1,0:T(8,128)S(1)}, f32[40,16,384]{2,1,0:T(8,128)}, u32[]{:S(2)}) copy-start(f32[40,16,384]{2,1,0:T(8,128)} %copy-done) | copy-start | bytes 2949124
  67.9 4.3 %slice-start = ((f32[40,16,384]{2,1,0:T(8,128)}), f32[32,16,384]{2,1,0:T(8,128)S(1)}, s32[]{:S(2)}) async-start(f32[40,16,384]{2,1,0:T(8,128)} %copy-done), calls=%async_computation.2 | async-start | bytes 1572864 | tf_op jit(solution)/shard_map/slice | solution.py:133
  67.9 4.3 %copy-start.6 = (f32[1,32,16,384]{3,2,1,0:T(8,128)S(1)}, f32[1,32,16,384]{3,2,1,0:T(8,128)}, u32[]{:S(2)}) copy-start(f32[1,32,16,384]{3,2,1,0:T(8,128)} %param.19) | copy-start | bytes 2359300
  67.9 4.3 %copy-start.9 = (f32[1,32,16,384]{3,2,1,0:T(8,128)S(1)}, f32[1,32,16,384]{3,2,1,0:T(8,128)}, u32[]{:S(2)}) copy-start(f32[1,32,16,384]{3,2,1,0:T(8,128)} %param.18) | copy-start | bytes 2359300
  67.9 4.3 %copy-start.12 = (f32[32,16,384]{2,1,0:T(8,128)S(1)}, f32[32,16,384]{2,1,0:T(8,128)}, u32[]{:S(2)}) copy-start(f32[32,16,384]{2,1,0:T(8,128)} %param.17) | copy-start | bytes 2359300

commit v4 on v3

--- a/solution.py
+++ b/solution.py
@@ -125,38 +125,31 @@
     ryc = receiver_ycell[0]
     rzc = receiver_zcell[0]
 
-    widths = (3 * R, 2 * R, 2 * R, 2 * R, R)
-    fields = (recent, older, coefficient, adj_now, later)
-    recent_x, older_x, coef_x, adj_now_x, later_x = wide_halo(fields, widths)
+    widths = (2 * R, R, R, R)
+    fields = (recent, older, coefficient, adj_now)
+    recent_x, older_x, coef_x, adj_now_x = wide_halo(fields, widths)
 
     def advance(current, before, coef, sources):
         return 2.0 * current[R:-R] - before + coef * (laplace_core(current) + sources)
 
-    def region(margin):
-        return (count + 2 * margin,) + shape[1:]
-
     def source_grid(margin, step):
         return point_grid(
-            region(margin), source_xcell, source_ycell, source_zcell,
+            (count + 2 * margin,) + shape[1:], source_xcell, source_ycell, source_zcell,
             amplitude[0, step : step + 1], base - margin,
         )
 
-    fwd_two_x = advance(recent_x, older_x, coef_x, source_grid(2 * R, 0))
-    fwd_three_x = advance(fwd_two_x, recent_x[2 * R : -2 * R], coef_x[R:-R], source_grid(R, 1))
-    rows_x, cols = selectors(region(R), rxc, ryc, rzc, base - R)
-    rows = rows_x[:, R * shape[1] : (R + count) * shape[1]]
-    fwd_two = fwd_two_x[2 * R : -2 * R]
-    fwd_three = fwd_three_x[R:-R]
+    fwd_two_x = advance(recent_x, older_x, coef_x, source_grid(R, 0))
+    fwd_two = fwd_two_x[R:-R]
+    recent_own = recent_x[2 * R : -2 * R]
+    fwd_three = advance(fwd_two_x, recent_own, coefficient, source_grid(0, 1))
+    rows, cols = selectors(shape, rxc, ryc, rzc, base)
     resid_two = sample(fwd_two, rows, cols) - observed[0, 0]
-    resid_three = sample(fwd_three_x, rows_x, cols) - observed[0, 1]
-    adj_two_x = advance(
-        adj_now_x, later_x, coef_x[R:-R], receiver_grid(region(R), rows_x, cols, resid_three)
+    resid_three = sample(fwd_three, rows, cols) - observed[0, 1]
+    adj_two = advance(adj_now_x, later, coefficient, receiver_grid(shape, rows, cols, resid_three))
+    adj_one = advance(
+        with_halo(adj_two, (("dom", 0),), R), adj_now, coefficient,
+        receiver_grid(shape, rows, cols, resid_two),
     )
-    adj_one = advance(
-        adj_two_x, adj_now_x[2 * R : -2 * R], coefficient, receiver_grid(shape, rows, cols, resid_two)
-    )
-    adj_two = adj_two_x[R:-R]
-    recent_own = recent_x[3 * R : -3 * R]
     late_term = adj_two * (fwd_three - 2.0 * fwd_two + recent_own)
     early_term = adj_one * (fwd_two - 2.0 * recent_own + older)
     gradient = shot_sum(early_term + late_term)

time: 152 us -> 132 us (0.87)
  the two profiles are of different devices: /device:TPU:4 before, /device:TPU:10 now
where the time goes in v4:
time: 132 us
  blocking collectives  75.5 us (57%)
  other arithmetic  14.5 us (11%)
  matrix products  11.2 us (8%)
  local copies, waits for them, and re-layouts  9.52 us (7%)
  starting transfers between devices  9.01 us (7%)
  between operations  6.8 us (5%)
  waiting for transfers between devices  5.1 us (4%)
    all_to_all x1, blocking collectives, shot_sum(): mine = jnp.sum(lax.all_to_all(pieces, 'shot', 0, 0, tiled=False), axis=0)  42 us
    all_to_all x1, blocking collectives, shot_sum(): return lax.all_to_all(spread, 'shot', 0, 0, tiled=False).reshape(term.shape)  33.4 us
    dot_general x2, matrix products, receiver_grid(): lax.dot_general(rows * values[:, None], cols, (((0,), (0,)), ((), ())), p...  7.58 us
    ppermute x1, waiting for transfers between devices, wide_halo(): lows = lax.ppermute(tails, 'dom', forward)  5.09 us
    add x3, other arithmetic, advance(): 2.0 * current[R:-R] - before + coef * (laplace_core(current) + sources)  4.92 us
    add x2, other arithmetic, laplace_core(): total + weight * (padded[:, R:R + width_y, R + offset:R + offset + width_...  4.69 us
    reshape x1, other arithmetic, shot_sum(): pieces = term.reshape((count, term.shape[0] // count) + term.shape[1:])  3.9 us
    dot_general x2, matrix products, sample(): jnp.dot(rows, field.reshape(width_x * width_y, width_z), precision=lax.Pr...  3.58 us
  transfers between devices with their start and end apart: 4, of which 1 were waited for; matrix products, arithmetic and copies ran while one was open for 4% of the time, Pallas kernels for 0%

profile of v4, /device:TPU:10, one launch (start us, length us, event | category | flops | bytes accessed | tf_op | source)
XLA Modules:
  0.0 131.5 jit_solution(16706894346350517480)
XLA Ops:
  0.6 1.0 fusion.175
  1.6 1.1 slice_bitcast_fusion.1
  2.6 1.1 slice_bitcast_fusion.4
  3.7 0.0 copy-start.14
  3.7 0.0 copy-start.15
  3.7 0.0 copy-start.13
  3.8 0.0 copy-start.11
  3.8 0.0 copy-start.12
  3.8 0.0 copy-start.10
  3.8 0.0 copy-start
  3.8 2.1 %collective-permute-start.1 = (f32[20,16,384]{2,1,0:T(8,128)S(1)}, f32[20,16,384]{2,1,0:T(8,128)S(1)}, u32[]{:S(2)}, u32[]{:S(2)}) collective-permute-start(f32[20,16,384]{2,1,0:T(8,128)S(1)} %pad_maximum_fusion.6), channel_id=1, source_target_pairs={{1,0},{2,1},{3,2},{4,3},{5,4},{6,5},{7,6},{8,7},{9,8},{10,9},{11,1... | collective-permute-start | bytes 1474568 | tf_op jit(solution)/shard_map/ppermute | solution.py:32
  5.9 2.4 %collective-permute-start = (f32[20,16,384]{2,1,0:T(8,128)S(1)}, f32[20,16,384]{2,1,0:T(8,128)S(1)}, u32[]{:S(2)}, u32[]{:S(2)}) collective-permute-start(f32[20,16,384]{2,1,0:T(8,128)S(1)} %pad_maximum_fusion.5), channel_id=1, source_target_pairs={{0,1},{1,2},{2,3},{3,4},{4,5},{5,6},{6,7},{7,8},{8,9},{9,10},{10,1... | collective-permute-start | bytes 1474568 | tf_op jit(solution)/shard_map/ppermute | solution.py:31
  10.3 0.7 and_reduce_fusion
  11.1 0.7 fusion.179
  14.3 5.1 %collective-permute-done = f32[20,16,384]{2,1,0:T(8,128)S(1)} collective-permute-done((f32[20,16,384]{2,1,0:T(8,128)S(1)}, f32[20,16,384]{2,1,0:T(8,128)S(1)}, u32[]{:S(2)}, u32[]{:S(2)}) %collective-permute-start) | collective-permute-done | bytes 491552 | tf_op jit(solution)/shard_map/ppermute | solution.py:31
  19.4 0.1 pad_maximum_fusion
  19.5 0.7 copy-done.9
  20.2 0.1 slice.569
  20.2 2.8 %fusion.26 = f32[40,16,384]{2,1,0:T(8,128)S(1)} fusion(f32[40,16,384]{2,1,0:T(8,128)S(1)} %slice.569, f32[48,16,384]{2,1,0:T(8,128)S(1)} %pad_maximum_fusion, f32[8,16,384]{2,1,0:T(8,128)S(1)} %slice.568, f32[32,16,384]{2,1,0:T(8,128)S(1)} %bitcast.54, f32[8,16,384]{2,1,0:T(8,128)S(1)} %slice.567), kind=kLoop, calls=%fused_computation.107 | loop fusion | flops 9584640 | bytes 9043968 | tf_op jit(solution)/shard_map/add | solution.py:56
  23.0 0.6 add.403
  24.3 0.1 add.406
  24.5 1.3 %fusion.177 = (f32[4,16,384]{2,1,0:T(8,128)S(1)}, f32[4,16,384]{2,1,0:T(8,128)S(1)}, f32[4,16,384]{2,1,0:T(8,128)S(1)}) fusion(f32[20,16,384]{2,1,0:T(8,128)} %copy-done.9), kind=kLoop, calls=%fused_computation.297 | loop fusion | bytes 589824 | tf_op jit(solution)/shard_map/slice | solution.py:35
  25.8 1.9 %fusion.45 = f32[40,16,384]{2,1,0:T(8,128)S(1)} fusion(f32[4,16,384]{2,1,0:T(8,128)S(1)} %get-tuple-element.41, f32[32,16,384]{2,1,0:T(8,128)} %bitcast.55, f32[4,16,384]{2,1,0:T(8,128)S(1)} %get-tuple-element.44, f32[40,16,384]{2,1,0:T(8,128)} %copy-done.4, f32[4,16,384]{2,1,0:T(8,128)S(1)} %get-tuple-element.40, f32[32,16,384]{2,1,0:T(8,128)} %param.17, ...), kind=kLoop, calls=%fused_computation.130 | loop fusion | flops 1966080 | bytes 4915200 | tf_op jit(solution)/shard_map/add | solution.py:133
  27.7 0.1 slice.580
  27.8 0.0 copy-start.5
  27.8 0.0 copy-start.1
  27.8 1.9 %fusion.113 = f32[32,16,384]{2,1,0:T(8,128)S(1)} fusion(f32[32,16,384]{2,1,0:T(8,128)S(1)} %slice.580, f32[40,16,384]{2,1,0:T(8,128)S(1)} %fusion.45), kind=kLoop, calls=%fused_computation.212 | loop fusion | flops 7274496 | bytes 7864320 | tf_op jit(solution)/shard_map/add | solution.py:56
  29.7 0.6 add.432
  31.0 0.3 add.435
  31.3 0.0 copy-start.6
  31.3 0.0 copy-start.16
  31.4 0.2 multiply_add_fusion
  31.6 0.0 copy-start.7
  31.6 0.9 copy-done.6
  32.5 1.8 %select_reduce_fusion = f32[1024]{0:T(1024)S(1)} fusion(f32[512,384]{1,0:T(8,128)S(1)} %bitcast.58, s32[1024]{0:T(1024)S(1)} %bitcast.66, s32[1024]{0:T(1024)S(1)} %bitcast.70), kind=kOutput, calls=%fused_computation.71 | convolution fusion | flops 2417622016 | bytes 798720 | tf_op jit(solution)/shard_map/dot_general | solution.py:83
  34.3 1.8 %select_reduce_fusion.1 = f32[1024]{0:T(1024)S(1)} fusion(f32[512,384]{1,0:T(8,128)S(1)} %bitcast.59, s32[1024]{0:T(1024)S(1)} %bitcast.67, s32[1024]{0:T(1024)S(1)} %bitcast.71), kind=kOutput, calls=%fused_computation.72 | convolution fusion | flops 2417622016 | bytes 798720 | tf_op jit(solution)/shard_map/dot_general | solution.py:83
  36.1 0.0 copy-start.8
  36.1 3.8 %fusion.2 = f32[512,384]{1,0:T(8,128)S(1)} fusion(f32[1024]{0:T(1024)S(1)} %sub.65, s32[1024]{0:T(1024)S(1)} %bitcast.68, s32[1024]{0:T(1024)S(1)} %bitcast.72), kind=kOutput, calls=%fused_computation.66 | convolution fusion | flops 2417360896 | bytes 798720 | tf_op jit(solution)/shard_map/dot_general | solution.py:88
  39.9 2.8 %fusion.85 = f32[32,16,384]{2,1,0:T(8,128)S(1)} fusion(f32[32,16,384]{2,1,0:T(8,128)S(1)} %copy-done.1, f32[32,16,384]{2,1,0:T(8,128)S(1)} %bitcast.61, f32[32,16,384]{2,1,0:T(8,128)S(1)} %bitcast.56, f32[4,16,384]{2,1,0:T(8,128)S(1)} %get-tuple-element.42, f32[4,16,384]{2,1,0:T(8,128)S(1)} %get-tuple-element.39, f32[1,32,16,384]{3,2,1,0:T(8,128)S(1)} %copy-done.8), kind=kLoop, calls=%fused_computation.184 | loop fusion | flops 9830400 | bytes 4128768 | tf_op jit(solution)/shard_map/add | solution.py:133
  42.7 1.9 %collective-permute-start.2 = (f32[4,16,384]{2,1,0:T(8,128)S(1)}, f32[4,16,384]{2,1,0:T(8,128)S(1)}, u32[]{:S(2)}, u32[]{:S(2)}) collective-permute-start(f32[4,16,384]{2,1,0:T(8,128)S(1)} %get-tuple-element.29), channel_id=1, source_target_pairs={{1,0},{2,1},{3,2},{4,3},{5,4},{6,5},{7,6},{8,7},{9,8},{10,9},{11,1... | collective-permute-start | bytes 294920 | tf_op jit(solution)/shard_map/ppermute | solution.py:20
  44.7 2.6 %collective-permute-start.3 = (f32[4,16,384]{2,1,0:T(8,128)S(1)}, f32[4,16,384]{2,1,0:T(8,128)S(1)}, u32[]{:S(2)}, u32[]{:S(2)}) collective-permute-start(f32[4,16,384]{2,1,0:T(8,128)S(1)} %get-tuple-element.30), channel_id=1, source_target_pairs={{0,1},{1,2},{2,3},{3,4},{4,5},{5,6},{6,7},{7,8},{8,9},{9,10},{10,1... | collective-permute-start | bytes 294920 | tf_op jit(solution)/shard_map/ppermute | solution.py:17
  47.3 3.8 %fusion = f32[512,384]{1,0:T(8,128)S(1)} fusion(f32[1024]{0:T(1024)S(1)} %sub.67, s32[1024]{0:T(1024)S(1)} %bitcast.69, s32[1024]{0:T(1024)S(1)} %bitcast.73), kind=kOutput, calls=%fused_computation.64 | convolution fusion | flops 2417360896 | bytes 798720 | tf_op jit(solution)/shard_map/dot_general | solution.py:88
  51.2 3.9 %add_bitcast_fusion = (f32[32,1,16,384]{3,2,1,0:T(8,128)S(1)}, f32[32,16,384]{2,1,0:T(8,128)}) fusion(f32[32,16,384]{2,1,0:T(8,128)S(1)} %fusion.85, f32[32,16,384]{2,1,0:T(8,128)S(1)} %multiply_add_fusion, f32[1,32,16,384]{3,2,1,0:T(8,128)S(1)} %copy-done.2, f32[1,32,16,384]{3,2,1,0:T(8,128)S(1)} %copy-done, f32[40,16,384]{2,1,0:T(8,128)S(1)} %fusion.45, ...), kind=kLoop, calls=%fused_computation.277 | loop fusion | flops 11599872 | bytes 8060928 | tf_op jit(solution)/shard_map/reshape | solution.py:96
  55.1 42.0 %all_to_all.10 = f32[32,1,16,384]{3,2,1,0:T(8,128)S(1)} all-to-all(f32[32,1,16,384]{3,2,1,0:T(8,128)S(1)} %get-tuple-element.27), channel_id=1, replica_groups=mesh['shot'=32,'dom'=16] {'shot'}, dimensions={0} | all-to-all | bytes 1572864 | tf_op jit(solution)/shard_map/all_to_all | solution.py:97
  97.1 0.1 reduce_sum.29
  97.2 0.1 broadcast_in_dim.13
  97.2 33.4 %all_to_all.11 = f32[32,1,16,384]{3,2,1,0:T(8,128)S(1)} all-to-all(f32[32,1,16,384]{3,2,1,0:T(8,128)S(1)} %broadcast_in_dim.13), channel_id=1, replica_groups=mesh['shot'=32,'dom'=16] {'shot'}, dimensions={0} | all-to-all | bytes 1572864 | tf_op jit(solution)/shard_map/all_to_all | solution.py:99
  130.6 0.9 copy.26
  (32 shorter events, 0.2 us)
Async XLA Ops:
  3.7 6.6 %copy-start.14 = (s32[3]{0:T(128)S(1)}, s32[3]{0:T(128)}, u32[]{:S(2)}) copy-start(s32[3]{0:T(128)} %constant.103.clone.1) | copy-start | bytes 40
  3.7 6.6 %copy-start.15 = (s32[3]{0:T(128)S(1)}, s32[3]{0:T(128)}, u32[]{:S(2)}) copy-start(s32[3]{0:T(128)} %constant.97.clone.1) | copy-start | bytes 40
  3.7 7.3 %copy-start.13 = (f32[1,2]{1,0:T(1,128)S(1)}, f32[1,2]{1,0:T(1,128)}, u32[]{:S(2)}) copy-start(f32[1,2]{1,0:T(1,128)} %param.25) | copy-start | bytes 28
  3.8 10.4 %copy-start.11 = (s32[1,1024]{1,0:T(1,128)S(1)}, s32[1,1024]{1,0:T(1,128)}, u32[]{:S(2)}) copy-start(s32[1,1024]{1,0:T(1,128)} %param.26) | copy-start | bytes 12292
  3.8 10.4 %copy-start.12 = (s32[1,1024]{1,0:T(1,128)S(1)}, s32[1,1024]{1,0:T(1,128)}, u32[]{:S(2)}) copy-start(s32[1,1024]{1,0:T(1,128)} %param.27) | copy-start | bytes 12292
  3.8 10.4 %copy-start.10 = (f32[1,2,1024]{2,1,0:T(2,128)S(1)}, f32[1,2,1024]{2,1,0:T(2,128)}, u32[]{:S(2)}) copy-start(f32[1,2,1024]{2,1,0:T(2,128)} %param.29) | copy-start | bytes 24580
  3.8 15.6 %copy-start = (f32[1,32,16,384]{3,2,1,0:T(8,128)S(1)}, f32[1,32,16,384]{3,2,1,0:T(8,128)}, u32[]{:S(2)}) copy-start(f32[1,32,16,384]{3,2,1,0:T(8,128)} %param.19) | copy-start | bytes 2359300
  3.8 10.4 %collective-permute-start.1 = (f32[20,16,384]{2,1,0:T(8,128)S(1)}, f32[20,16,384]{2,1,0:T(8,128)S(1)}, u32[]{:S(2)}, u32[]{:S(2)}) collective-permute-start(f32[20,16,384]{2,1,0:T(8,128)S(1)} %pad_maximum_fusion.6), channel_id=1, source_target_pairs={{1,0},{2,1},{3,2},{4,3},{5,4},{6,5},{7,6},{8,7},{9,8},{10,9},{11,1... | collective-permute-start | bytes 1474568 | tf_op jit(solution)/shard_map/ppermute | solution.py:32
  5.9 13.4 %collective-permute-start = (f32[20,16,384]{2,1,0:T(8,128)S(1)}, f32[20,16,384]{2,1,0:T(8,128)S(1)}, u32[]{:S(2)}, u32[]{:S(2)}) collective-permute-start(f32[20,16,384]{2,1,0:T(8,128)S(1)} %pad_maximum_fusion.5), channel_id=1, source_target_pairs={{0,1},{1,2},{2,3},{3,4},{4,5},{5,6},{6,7},{7,8},{8,9},{9,10},{10,1... | collective-permute-start | bytes 1474568 | tf_op jit(solution)/shard_map/ppermute | solution.py:31
  19.4 0.8 copy-start.9
  24.4 1.4 %copy-start.4 = (f32[40,16,384]{2,1,0:T(8,128)}, f32[40,16,384]{2,1,0:T(8,128)S(1)}, u32[]{:S(2)}) copy-start(f32[40,16,384]{2,1,0:T(8,128)S(1)} %add.406) | copy-start | bytes 2949124
  27.8 1.9 %copy-start.5 = (f32[32,16,384]{2,1,0:T(8,128)}, f32[32,16,384]{2,1,0:T(8,128)S(1)}, u32[]{:S(2)}) copy-start(f32[32,16,384]{2,1,0:T(8,128)S(1)} %slice.580) | copy-start | bytes 2359300
  27.8 3.5 %copy-start.1 = (f32[32,16,384]{2,1,0:T(8,128)S(1)}, f32[32,16,384]{2,1,0:T(8,128)}, u32[]{:S(2)}) copy-start(f32[32,16,384]{2,1,0:T(8,128)} %param.17) | copy-start | bytes 2359300
  31.3 1.1 copy-start.6
  31.3 1.1 copy-start.16
  31.6 19.6 %copy-start.7 = (f32[32,16,384]{2,1,0:T(8,128)}, f32[32,16,384]{2,1,0:T(8,128)S(1)}, u32[]{:S(2)}) copy-start(f32[32,16,384]{2,1,0:T(8,128)S(1)} %multiply_add_fusion) | copy-start | bytes 2359300
  36.1 3.8 %copy-start.3 = (f32[1,32,16,384]{3,2,1,0:T(8,128)S(1)}, f32[1,32,16,384]{3,2,1,0:T(8,128)}, u32[]{:S(2)}) copy-start(f32[1,32,16,384]{3,2,1,0:T(8,128)} %param.21) | copy-start | bytes 2359300
  36.1 3.8 %copy-start.8 = (f32[1,32,16,384]{3,2,1,0:T(8,128)S(1)}, f32[1,32,16,384]{3,2,1,0:T(8,128)}, u32[]{:S(2)}) copy-start(f32[1,32,16,384]{3,2,1,0:T(8,128)} %param.20) | copy-start | bytes 2359300
  42.7 8.4 %collective-permute-start.2 = (f32[4,16,384]{2,1,0:T(8,128)S(1)}, f32[4,16,384]{2,1,0:T(8,128)S(1)}, u32[]{:S(2)}, u32[]{:S(2)}) collective-permute-start(f32[4,16,384]{2,1,0:T(8,128)S(1)} %get-tuple-element.29), channel_id=1, source_target_pairs={{1,0},{2,1},{3,2},{4,3},{5,4},{6,5},{7,6},{8,7},{9,8},{10,9},{11,1... | collective-permute-start | bytes 294920 | tf_op jit(solution)/shard_map/ppermute | solution.py:20
  44.7 6.5 %collective-permute-start.3 = (f32[4,16,384]{2,1,0:T(8,128)S(1)}, f32[4,16,384]{2,1,0:T(8,128)S(1)}, u32[]{:S(2)}, u32[]{:S(2)}) collective-permute-start(f32[4,16,384]{2,1,0:T(8,128)S(1)} %get-tuple-element.30), channel_id=1, source_target_pairs={{0,1},{1,2},{2,3},{3,4},{4,5},{5,6},{6,7},{7,8},{8,9},{9,10},{10,1... | collective-permute-start | bytes 294920 | tf_op jit(solution)/shard_map/ppermute | solution.py:17
  47.3 3.8 %copy-start.2 = (f32[1,32,16,384]{3,2,1,0:T(8,128)S(1)}, f32[1,32,16,384]{3,2,1,0:T(8,128)}, u32[]{:S(2)}) copy-start(f32[1,32,16,384]{3,2,1,0:T(8,128)} %param.18) | copy-start | bytes 2359300

commit v5 on v4

--- a/solution.py
+++ b/solution.py
@@ -20,6 +20,28 @@
         high = lax.ppermute(lax.slice_in_dim(block, 0, width, axis=dim), axis, backward)
         block = jnp.concatenate([low, block, high], axis=dim)
     return block
+
+
+def window(field, start, stop):
+    low, own, high = field
+    count = own.shape[0]
+    parts = []
+    if start < 0:
+        parts.append(low[low.shape[0] + start : low.shape[0] + min(stop, 0)])
+    if stop > 0 and start < count:
+        parts.append(own[max(start, 0) : min(stop, count)])
+    if stop > count:
+        parts.append(high[max(start - count, 0) : stop - count])
+    return parts[0] if len(parts) == 1 else jnp.concatenate(parts)
+
+
+def with_halo_parts(block, width):
+    count = lax.axis_size("dom")
+    forward = [(i, i + 1) for i in range(count - 1)]
+    backward = [(target, source) for source, target in forward]
+    low = lax.ppermute(block[block.shape[0] - width :], "dom", forward)
+    high = lax.ppermute(block[:width], "dom", backward)
+    return low, high
 
 
 def wide_halo(fields, widths):
@@ -31,8 +53,8 @@
     lows = lax.ppermute(tails, "dom", forward)
     highs = lax.ppermute(heads, "dom", backward)
     out, at = [], 0
-    for f, w in zip(fields, widths):
-        out.append(jnp.concatenate([lows[at : at + w], f, highs[at : at + w]]))
+    for w in widths:
+        out.append((lows[at : at + w], highs[at : at + w]))
         at += w
     return out
 
@@ -127,32 +149,66 @@
 
     widths = (2 * R, R, R, R)
     fields = (recent, older, coefficient, adj_now)
-    recent_x, older_x, coef_x, adj_now_x = wide_halo(fields, widths)
-
-    def advance(current, before, coef, sources):
-        return 2.0 * current[R:-R] - before + coef * (laplace_core(current) + sources)
-
-    def source_grid(margin, step):
-        return point_grid(
+    halos = wide_halo(fields, widths)
+    recent_t, older_t, coef_t, adj_now_t = [(lo, f, hi) for f, (lo, hi) in zip(fields, halos)]
+    later_t = (None, later, None)
+    inner = [(-R, R), (R, count - R), (count - R, count + R)]
+    split = [(0, R), (R, count - R), (count - R, count)]
+
+    def source_grid(step, margin):
+        grid = point_grid(
             (count + 2 * margin,) + shape[1:], source_xcell, source_ycell, source_zcell,
             amplitude[0, step : step + 1], base - margin,
         )
-
-    fwd_two_x = advance(recent_x, older_x, coef_x, source_grid(R, 0))
-    fwd_two = fwd_two_x[R:-R]
-    recent_own = recent_x[2 * R : -2 * R]
-    fwd_three = advance(fwd_two_x, recent_own, coefficient, source_grid(0, 1))
+        return lambda a, b: grid[a + margin : b + margin]
+
+    def laplace_parts(current, pieces):
+        return [laplace_core(window(current, a - R, b + R)) for a, b in pieces]
+
+    def advance(current, before, laplace, sources, pieces):
+        return [
+            2.0 * window(current, a, b) - window(before, a, b)
+            + window(coef_t, a, b) * (lap + sources(a, b))
+            for lap, (a, b) in zip(laplace, pieces)
+        ]
+
+    fwd_two_p = advance(
+        recent_t, older_t, laplace_parts(recent_t, inner), source_grid(0, R), inner
+    )
+    fwd_two_t = (
+        fwd_two_p[0][:R],
+        jnp.concatenate([fwd_two_p[0][R:], fwd_two_p[1], fwd_two_p[2][:R]]),
+        fwd_two_p[2][R:],
+    )
+    fwd_two = fwd_two_t[1]
+    (fwd_three,) = advance(
+        fwd_two_t, recent_t, laplace_parts(fwd_two_t, [(0, count)]), source_grid(1, 0), [(0, count)]
+    )
     rows, cols = selectors(shape, rxc, ryc, rzc, base)
     resid_two = sample(fwd_two, rows, cols) - observed[0, 0]
     resid_three = sample(fwd_three, rows, cols) - observed[0, 1]
-    adj_two = advance(adj_now_x, later, coefficient, receiver_grid(shape, rows, cols, resid_three))
-    adj_one = advance(
-        with_halo(adj_two, (("dom", 0),), R), adj_now, coefficient,
-        receiver_grid(shape, rows, cols, resid_two),
-    )
-    late_term = adj_two * (fwd_three - 2.0 * fwd_two + recent_own)
-    early_term = adj_one * (fwd_two - 2.0 * recent_own + older)
-    gradient = shot_sum(early_term + late_term)
+    adj_lap = lax.optimization_barrier(laplace_parts(adj_now_t, split))
+    adj_sources = receiver_grid(shape, rows, cols, resid_three)
+    adj_two_p = advance(
+        adj_now_t, later_t, adj_lap, lambda a, b: adj_sources[a:b], split
+    )
+    adj_two = jnp.concatenate(adj_two_p)
+    adj_two_low, adj_two_high = with_halo_parts(adj_two, R)
+    adj_two_t = (adj_two_low, adj_two, adj_two_high)
+    adj_sources_two = receiver_grid(shape, rows, cols, resid_two)
+    adj_one_p = advance(
+        adj_two_t, adj_now_t, laplace_parts(adj_two_t, split),
+        lambda a, b: adj_sources_two[a:b], split,
+    )
+    adj_one = jnp.concatenate(adj_one_p)
+    terms = []
+    for one, (a, b) in zip(adj_one_p, split):
+        recent_ab = recent[a:b]
+        terms.append(
+            one * (fwd_two[a:b] - 2.0 * recent_ab + older[a:b])
+            + adj_two[a:b] * (fwd_three[a:b] - 2.0 * fwd_two[a:b] + recent_ab)
+        )
+    gradient = shot_sum(jnp.concatenate(terms))
     return (fwd_three[None], adj_one[None], gradient)
 
 

time: 132 us -> 152 us (1.15)
  the two profiles are of different devices: /device:TPU:10 before, /device:TPU:9 now
where the time goes in v5:
time: 152 us; the launch traced here: 151 us
  blocking collectives  39.8 us (26%)
  waiting for transfers between devices  27 us (18%)
  other arithmetic  25.5 us (17%)
  local copies, waits for them, and re-layouts  22.7 us (15%)
  starting transfers between devices  18.4 us (12%)
  matrix products  11.2 us (7%)
  between operations  6.67 us (4%)
    all_to_all x1, blocking collectives, shot_sum(): mine = jnp.sum(lax.all_to_all(pieces, 'shot', 0, 0, tiled=False), axis=0)  39.8 us
    all_to_all x1, waiting for transfers between devices, shot_sum(): return lax.all_to_all(spread, 'shot', 0, 0, tiled=False).reshape(term.shape)  27 us
    add x6, other arithmetic, advance(): 2.0 * window(current, a, b) - window(before, a, b)  13.1 us
    dot_general x2, matrix products, receiver_grid(): lax.dot_general(rows * values[:, None], cols, (((0,), (0,)), ((), ())), p...  7.58 us
    slice x4, local copies, waits for them, and re-layouts, wide_halo(): out.append((lows[at:at + w], highs[at:at + w]))  5.46 us
    unnamed x81, local copies, waits for them, and re-layouts  5.44 us
    all_to_all x1, starting transfers between devices, shot_sum(): return lax.all_to_all(spread, 'shot', 0, 0, tiled=False).reshape(term.shape)  5.26 us
    add x4, other arithmetic, laplace_core(): total + weight * (padded[:, R:R + width_y, R + offset:R + offset + width_...  5.03 us
  transfers between devices with their start and end apart: 5, of which 1 were waited for; matrix products, arithmetic and copies ran while one was open for 18% of the time, Pallas kernels for 0%

profile of v5, /device:TPU:9, one launch (start us, length us, event | category | flops | bytes accessed | tf_op | source)
XLA Modules:
  0.0 151.3 jit_solution(18055950313639683003)
XLA Ops:
  0.6 1.1 slice_bitcast_fusion.4
  1.8 1.0 fusion.421
  2.8 1.0 slice_bitcast_fusion.10
  3.9 0.8 pad_maximum_fusion.4
  4.7 2.6 %collective-permute-start.1 = (f32[20,16,384]{2,1,0:T(8,128)}, f32[20,16,384]{2,1,0:T(8,128)}, u32[]{:S(2)}, u32[]{:S(2)}) collective-permute-start(f32[20,16,384]{2,1,0:T(8,128)} %pad_maximum_fusion.4), channel_id=1, source_target_pairs={{1,0},{2,1},{3,2},{4,3},{5,4},{6,5},{7,6},{8,7},{9,8},{10,9},{11,1... | collective-permute-start | bytes 1474568 | tf_op jit(solution)/shard_map/ppermute | solution.py:54
  7.2 0.8 pad_maximum_fusion.3
  8.1 3.9 %collective-permute-start = (f32[20,16,384]{2,1,0:T(8,128)}, f32[20,16,384]{2,1,0:T(8,128)}, u32[]{:S(2)}, u32[]{:S(2)}) collective-permute-start(f32[20,16,384]{2,1,0:T(8,128)} %pad_maximum_fusion.3), channel_id=1, source_target_pairs={{0,1},{1,2},{2,3},{3,4},{4,5},{5,6},{6,7},{7,8},{8,9},{9,10},{10,1... | collective-permute-start | bytes 1474568 | tf_op jit(solution)/shard_map/ppermute | solution.py:53
  12.6 0.7 slice_bitcast_fusion.9
  13.3 0.9 slice_bitcast_fusion.1
  14.2 0.8 slice_bitcast_fusion.2
  16.4 0.6 fusion.425
  17.0 2.2 %fusion.121 = f32[24,16,384]{2,1,0:T(8,128)} fusion(f32[24,16,384]{2,1,0:T(8,128)S(1)} %slice_bitcast_fusion, f32[1,32,16,384]{3,2,1,0:T(8,128)S(1)} %copy-done), kind=kLoop, calls=%fused_computation.346 | loop fusion | flops 5455872 | bytes 5898240 | tf_op jit(solution)/shard_map/add | solution.py:78
  20.7 0.8 and_reduce_fusion
  22.8 1.1 broadcast_in_dim.12
  23.8 1.4 scatter-add.6
  25.2 8.7 %fusion.94 = f32[24,16,384]{2,1,0:T(8,128)S(1)} fusion(f32[24,16,384]{2,1,0:T(8,128)} %slice_bitcast_fusion.1, f32[40,16,384]{2,1,0:T(8,128)} %scatter-add.6, f32[1,32,16,384]{3,2,1,0:T(8,128)S(1)} %copy-done.1, f32[1,32,16,384]{3,2,1,0:T(8,128)} %param.18, f32[32,16,384]{2,1,0:T(8,128)S(1)} %copy-done.2), kind=kLoop, calls=%fused_computation.319 | loop fusion | flops 6193152 | bytes 7667712 | tf_op jit(solution)/shard_map/add | solution.py:170
  33.9 1.0 slice.1403
  35.0 1.7 %fusion.422 = (f32[4,16,384]{2,1,0:T(8,128)}, f32[4,16,384]{2,1,0:T(8,128)S(1)}, f32[4,16,384]{2,1,0:T(8,128)S(1)}, f32[4,16,384]{2,1,0:T(8,128)S(1)}) fusion(f32[20,16,384]{2,1,0:T(8,128)} %collective-permute-done.1), kind=kLoop, calls=%fused_computation.701 | loop fusion | bytes 786432 | tf_op jit(solution)/shard_map/slice | solution.py:57
  36.7 1.4 fusion.170
  38.2 1.1 slice.1384
  39.2 1.7 %fusion.423 = (f32[4,16,384]{2,1,0:T(8,128)}, f32[4,16,384]{2,1,0:T(8,128)S(1)}, f32[4,16,384]{2,1,0:T(8,128)S(1)}, f32[4,16,384]{2,1,0:T(8,128)S(1)}) fusion(f32[20,16,384]{2,1,0:T(8,128)} %collective-permute-done), kind=kLoop, calls=%fused_computation.702 | loop fusion | bytes 786432 | tf_op jit(solution)/shard_map/slice | solution.py:57
  41.0 1.4 fusion.197
  42.6 2.3 %fusion.26 = f32[32,16,384]{2,1,0:T(8,128)S(1)} fusion(f32[32,16,384]{2,1,0:T(8,128)S(1)} %pad_maximum_fusion.1, f32[40,16,384]{2,1,0:T(8,128)S(1)} %pad_maximum_fusion, f32[8,16,384]{2,1,0:T(8,128)S(1)} %fusion.170, f32[24,16,384]{2,1,0:T(8,128)S(1)} %fusion.94, f32[8,16,384]{2,1,0:T(8,128)S(1)} %fusion.197), kind=kLoop, calls=%fused_computation.141 | loop fusion | flops 7667712 | bytes 7274496 | tf_op jit(solution)/shard_map/add | solution.py:78
  44.8 0.9 copy-done.3
  45.7 0.6 add.986
  46.9 1.5 add.989
  48.4 1.3 fusion.46
  49.8 1.8 %select_reduce_fusion.1 = f32[1024]{0:T(1024)S(1)} fusion(f32[512,384]{1,0:T(8,128)S(1)} %bitcast.154, s32[1024]{0:T(1024)S(1)} %bitcast.164, s32[1024]{0:T(1024)S(1)} %bitcast.168), kind=kOutput, calls=%fused_computation.86 | convolution fusion | flops 2417622016 | bytes 798720 | tf_op jit(solution)/shard_map/dot_general | solution.py:105
  51.6 3.8 %fusion.2 = f32[512,384]{1,0:T(8,128)S(1)} fusion(f32[1024]{0:T(1024)S(1)} %sub.97, s32[1024]{0:T(1024)S(1)} %bitcast.165, s32[1024]{0:T(1024)S(1)} %bitcast.169), kind=kOutput, calls=%fused_computation.80 | convolution fusion | flops 2417360896 | bytes 798720 | tf_op jit(solution)/shard_map/dot_general | solution.py:110
  55.5 1.4 copy-done.5
  56.9 1.8 %select_reduce_fusion = f32[1024]{0:T(1024)S(1)} fusion(f32[512,384]{1,0:T(8,128)S(1)} %bitcast.152, s32[1024]{0:T(1024)S(1)} %bitcast.166, s32[1024]{0:T(1024)S(1)} %bitcast.170), kind=kOutput, calls=%fused_computation.85 | convolution fusion | flops 2417622016 | bytes 798720 | tf_op jit(solution)/shard_map/dot_general | solution.py:105
  58.7 3.8 %fusion = f32[512,384]{1,0:T(8,128)S(1)} fusion(f32[1024]{0:T(1024)S(1)} %sub.101, s32[1024]{0:T(1024)S(1)} %bitcast.167, s32[1024]{0:T(1024)S(1)} %bitcast.171), kind=kOutput, calls=%fused_computation.78 | convolution fusion | flops 2417360896 | bytes 798720 | tf_op jit(solution)/shard_map/dot_general | solution.py:110
  62.6 0.9 copy-done.15
  63.5 0.3 copy-done.28
  63.8 0.3 fusion.318
  64.2 0.3 fusion.300
  64.5 1.9 %collective-permute-start.3 = (f32[4,16,384]{2,1,0:T(8,128)S(1)}, f32[4,16,384]{2,1,0:T(8,128)S(1)}, u32[]{:S(2)}, u32[]{:S(2)}) collective-permute-start(f32[4,16,384]{2,1,0:T(8,128)S(1)} %get-tuple-element.39), channel_id=1, source_target_pairs={{1,0},{2,1},{3,2},{4,3},{5,4},{6,5},{7,6},{8,7},{9,8},{10,9},{11,1... | collective-permute-start | bytes 294920 | tf_op jit(solution)/shard_map/ppermute | solution.py:43
  66.4 4.8 %collective-permute-start.2 = (f32[4,16,384]{2,1,0:T(8,128)S(1)}, f32[4,16,384]{2,1,0:T(8,128)S(1)}, u32[]{:S(2)}, u32[]{:S(2)}) collective-permute-start(f32[4,16,384]{2,1,0:T(8,128)S(1)} %get-tuple-element.40), channel_id=1, source_target_pairs={{0,1},{1,2},{2,3},{3,4},{4,5},{5,6},{6,7},{7,8},{8,9},{9,10},{10,1... | collective-permute-start | bytes 294920 | tf_op jit(solution)/shard_map/ppermute | solution.py:42
  71.5 0.9 copy-done.7
  72.5 3.1 %fusion.154 = (f32[24,16,384]{2,1,0:T(8,128)S(1)}, f32[24,16,384]{2,1,0:T(8,128)}) fusion(f32[24,16,384]{2,1,0:T(8,128)S(1)} %fusion.155, f32[32,16,384]{2,1,0:T(8,128)S(1)} %fusion.46, f32[24,16,384]{2,1,0:T(8,128)S(1)} %fusion.94, f32[1,32,16,384]{3,2,1,0:T(8,128)S(1)} %copy-done.7, f32[1,32,16,384]{3,2,1,0:T(8,128)S(1)} %copy-done.1, ...), kind=kLoop, calls=%fused_computation.380 | loop fusion | flops 8699904 | bytes 6094848 | tf_op jit(solution)/shard_map/add | solution.py:208
  75.7 0.3 fusion.398
  76.0 0.3 fusion.401
  76.4 39.8 %all_to_all.10 = f32[32,1,16,384]{3,2,1,0:T(8,128)S(1)} all-to-all(f32[32,1,16,384]{3,2,1,0:T(8,128)S(1)} %maximum_bitcast_fusion.1), channel_id=1, replica_groups=mesh['shot'=32,'dom'=16] {'shot'}, dimensions={0} | all-to-all | bytes 1572864 | tf_op jit(solution)/shard_map/all_to_all | solution.py:119
  116.3 0.9 broadcast_in_dim.16
  117.2 5.3 %all-to-all-start.1 = ((f32[32,1,16,384]{3,2,1,0:T(8,128)}), f32[32,1,16,384]{3,2,1,0:T(8,128)S(1)}, u32[]{:S(2)}, u32[]{:S(2)}) async-start(f32[32,1,16,384]{3,2,1,0:T(8,128)} %broadcast_in_dim.16), calls=%async_computation.1 | async-start | bytes 1572864 | tf_op jit(solution)/shard_map/all_to_all | solution.py:121
  122.5 0.9 maximum_bitcast_fusion
  123.4 27.0 %all-to-all-done.1 = f32[32,1,16,384]{3,2,1,0:T(8,128)S(1)} async-done(((f32[32,1,16,384]{3,2,1,0:T(8,128)}), f32[32,1,16,384]{3,2,1,0:T(8,128)S(1)}, u32[]{:S(2)}, u32[]{:S(2)}) %all-to-all-start.1) | async-done | bytes 786464 | tf_op jit(solution)/shard_map/all_to_all | solution.py:121
  150.4 0.9 copy.26
  (101 shorter events, 1.1 us)
Async XLA Ops:
  0.6 2.1 %copy-start = (f32[1,32,16,384]{3,2,1,0:T(8,128)S(1)}, f32[1,32,16,384]{3,2,1,0:T(8,128)}, u32[]{:S(2)}) copy-start(f32[1,32,16,384]{3,2,1,0:T(8,128)} %param.21) | copy-start | bytes 2359300
  2.7 5.3 %copy-start.20 = (f32[4,16,384]{2,1,0:T(8,128)}, f32[4,16,384]{2,1,0:T(8,128)S(1)}, u32[]{:S(2)}) copy-start(f32[4,16,384]{2,1,0:T(8,128)S(1)} %get-tuple-element.52) | copy-start | bytes 294916
  2.7 5.3 %copy-start.22 = (f32[4,16,384]{2,1,0:T(8,128)}, f32[4,16,384]{2,1,0:T(8,128)S(1)}, u32[]{:S(2)}) copy-start(f32[4,16,384]{2,1,0:T(8,128)S(1)} %get-tuple-element.51) | copy-start | bytes 294916
  3.8 4.3 %copy-start.12 = (f32[4,16,384]{2,1,0:T(8,128)}, f32[4,16,384]{2,1,0:T(8,128)S(1)}, u32[]{:S(2)}) copy-start(f32[4,16,384]{2,1,0:T(8,128)S(1)} %get-tuple-element.49) | copy-start | bytes 294916
  3.8 4.3 %copy-start.14 = (f32[4,16,384]{2,1,0:T(8,128)}, f32[4,16,384]{2,1,0:T(8,128)S(1)}, u32[]{:S(2)}) copy-start(f32[4,16,384]{2,1,0:T(8,128)S(1)} %get-tuple-element.50) | copy-start | bytes 294916
  3.8 4.3 %copy-start.16 = (f32[4,16,384]{2,1,0:T(8,128)}, f32[4,16,384]{2,1,0:T(8,128)S(1)}, u32[]{:S(2)}) copy-start(f32[4,16,384]{2,1,0:T(8,128)S(1)} %get-tuple-element.71) | copy-start | bytes 294916
  3.8 4.3 %copy-start.18 = (f32[4,16,384]{2,1,0:T(8,128)}, f32[4,16,384]{2,1,0:T(8,128)S(1)}, u32[]{:S(2)}) copy-start(f32[4,16,384]{2,1,0:T(8,128)S(1)} %get-tuple-element.72) | copy-start | bytes 294916
  3.8 8.8 %copy-start.1 = (f32[1,32,16,384]{3,2,1,0:T(8,128)S(1)}, f32[1,32,16,384]{3,2,1,0:T(8,128)}, u32[]{:S(2)}) copy-start(f32[1,32,16,384]{3,2,1,0:T(8,128)} %param.19) | copy-start | bytes 2359300
  4.7 29.3 %collective-permute-start.1 = (f32[20,16,384]{2,1,0:T(8,128)}, f32[20,16,384]{2,1,0:T(8,128)}, u32[]{:S(2)}, u32[]{:S(2)}) collective-permute-start(f32[20,16,384]{2,1,0:T(8,128)} %pad_maximum_fusion.4), channel_id=1, source_target_pairs={{1,0},{2,1},{3,2},{4,3},{5,4},{6,5},{7,6},{8,7},{9,8},{10,9},{11,1... | collective-permute-start | bytes 1474568 | tf_op jit(solution)/shard_map/ppermute | solution.py:54
  8.1 30.1 %collective-permute-start = (f32[20,16,384]{2,1,0:T(8,128)}, f32[20,16,384]{2,1,0:T(8,128)}, u32[]{:S(2)}, u32[]{:S(2)}) collective-permute-start(f32[20,16,384]{2,1,0:T(8,128)} %pad_maximum_fusion.3), channel_id=1, source_target_pairs={{0,1},{1,2},{2,3},{3,4},{4,5},{5,6},{6,7},{7,8},{8,9},{9,10},{10,1... | collective-permute-start | bytes 1474568 | tf_op jit(solution)/shard_map/ppermute | solution.py:53
  14.2 2.2 %copy-start.36 = (f32[1,2]{1,0:T(1,128)S(1)}, f32[1,2]{1,0:T(1,128)}, u32[]{:S(2)}) copy-start(f32[1,2]{1,0:T(1,128)} %param.25) | copy-start | bytes 28
  17.0 2.3 %copy-start.33 = (f32[1,2,1024]{2,1,0:T(2,128)S(1)}, f32[1,2,1024]{2,1,0:T(2,128)}, u32[]{:S(2)}) copy-start(f32[1,2,1024]{2,1,0:T(2,128)} %param.29) | copy-start | bytes 24580
  17.0 3.6 %copy-start.34 = (s32[1,1024]{1,0:T(1,128)S(1)}, s32[1,1024]{1,0:T(1,128)}, u32[]{:S(2)}) copy-start(s32[1,1024]{1,0:T(1,128)} %param.26) | copy-start | bytes 12292
  17.0 3.6 %copy-start.35 = (s32[1,1024]{1,0:T(1,128)S(1)}, s32[1,1024]{1,0:T(1,128)}, u32[]{:S(2)}) copy-start(s32[1,1024]{1,0:T(1,128)} %param.27) | copy-start | bytes 12292
  17.0 3.7 %copy-start.37 = (s32[3]{0:T(128)S(1)}, s32[3]{0:T(128)}, u32[]{:S(2)}) copy-start(s32[3]{0:T(128)} %constant.115.clone.1) | copy-start | bytes 40
  17.0 3.7 %copy-start.38 = (s32[3]{0:T(128)S(1)}, s32[3]{0:T(128)}, u32[]{:S(2)}) copy-start(s32[3]{0:T(128)} %constant.109.clone.1) | copy-start | bytes 40
  19.3 6.0 %copy-start.2 = (f32[32,16,384]{2,1,0:T(8,128)S(1)}, f32[32,16,384]{2,1,0:T(8,128)}, u32[]{:S(2)}) copy-start(f32[32,16,384]{2,1,0:T(8,128)} %param.17) | copy-start | bytes 2359300
  33.9 2.8 %copy-start.19 = (f32[4,16,384]{2,1,0:T(8,128)S(1)}, f32[4,16,384]{2,1,0:T(8,128)}, u32[]{:S(2)}) copy-start(f32[4,16,384]{2,1,0:T(8,128)} %copy-done.18) | copy-start | bytes 294916
  33.9 2.8 %copy-start.23 = (f32[4,16,384]{2,1,0:T(8,128)S(1)}, f32[4,16,384]{2,1,0:T(8,128)}, u32[]{:S(2)}) copy-start(f32[4,16,384]{2,1,0:T(8,128)} %copy-done.22) | copy-start | bytes 294916
  33.9 2.8 %copy-start.32 = (f32[4,16,384]{2,1,0:T(8,128)S(1)}, f32[4,16,384]{2,1,0:T(8,128)}, u32[]{:S(2)}) copy-start(f32[4,16,384]{2,1,0:T(8,128)} %get-tuple-element.48) | copy-start | bytes 294916
  38.1 2.9 %copy-start.17 = (f32[4,16,384]{2,1,0:T(8,128)S(1)}, f32[4,16,384]{2,1,0:T(8,128)}, u32[]{:S(2)}) copy-start(f32[4,16,384]{2,1,0:T(8,128)} %copy-done.16) | copy-start | bytes 294916
  38.1 2.8 %copy-start.21 = (f32[4,16,384]{2,1,0:T(8,128)S(1)}, f32[4,16,384]{2,1,0:T(8,128)}, u32[]{:S(2)}) copy-start(f32[4,16,384]{2,1,0:T(8,128)} %copy-done.20) | copy-start | bytes 294916
  38.1 2.8 %copy-start.31 = (f32[4,16,384]{2,1,0:T(8,128)S(1)}, f32[4,16,384]{2,1,0:T(8,128)}, u32[]{:S(2)}) copy-start(f32[4,16,384]{2,1,0:T(8,128)} %get-tuple-element.47) | copy-start | bytes 294916
  38.1 4.3 %copy-start.24 = (f32[4,16,384]{2,1,0:T(8,128)}, f32[4,16,384]{2,1,0:T(8,128)S(1)}, u32[]{:S(2)}) copy-start(f32[4,16,384]{2,1,0:T(8,128)S(1)} %slice.1417) | copy-start | bytes 294916
  42.5 2.3 %copy-start.4 = (f32[32,16,384]{2,1,0:T(8,128)}, f32[32,16,384]{2,1,0:T(8,128)S(1)}, u32[]{:S(2)}) copy-start(f32[32,16,384]{2,1,0:T(8,128)S(1)} %pad_maximum_fusion.1) | copy-start | bytes 2359300
  42.5 5.9 %copy-start.25 = (f32[4,16,384]{2,1,0:T(8,128)S(1)}, f32[4,16,384]{2,1,0:T(8,128)}, u32[]{:S(2)}) copy-start(f32[4,16,384]{2,1,0:T(8,128)} %copy-done.24) | copy-start | bytes 294916
  44.8 0.9 copy-start.3
  48.4 1.4 copy-start.39
  49.8 26.2 %copy-start.6 = (f32[32,16,384]{2,1,0:T(8,128)}, f32[32,16,384]{2,1,0:T(8,128)S(1)}, u32[]{:S(2)}) copy-start(f32[32,16,384]{2,1,0:T(8,128)S(1)} %fusion.46) | copy-start | bytes 2359300
  55.4 3.2 %copy-start.11 = (f32[512,384]{1,0:T(8,128)}, f32[512,384]{1,0:T(8,128)S(1)}, u32[]{:S(2)}) copy-start(f32[512,384]{1,0:T(8,128)S(1)} %fusion.2) | copy-start | bytes 2359300
  55.4 1.4 copy-start.5
  62.5 1.6 %copy-start.10 = (f32[512,384]{1,0:T(8,128)}, f32[512,384]{1,0:T(8,128)S(1)}, u32[]{:S(2)}) copy-start(f32[512,384]{1,0:T(8,128)S(1)} %fusion) | copy-start | bytes 2359300
  62.5 1.0 copy-start.15
  62.5 1.2 copy-start.28
  62.5 1.3 copy-start.30
  62.5 1.6 %copy-start.13 = (f32[4,16,384]{2,1,0:T(8,128)S(1)}, f32[4,16,384]{2,1,0:T(8,128)}, u32[]{:S(2)}) copy-start(f32[4,16,384]{2,1,0:T(8,128)} %copy-done.12) | copy-start | bytes 294916
  62.6 1.6 %copy-start.27 = (f32[8,16,384]{2,1,0:T(8,128)S(1)}, f32[8,16,384]{2,1,0:T(8,128)}, u32[]{:S(2)}) copy-start(f32[8,16,384]{2,1,0:T(8,128)} %get-tuple-element.45) | copy-start | bytes 589828
  62.6 1.6 %copy-start.29 = (f32[4,16,384]{2,1,0:T(8,128)S(1)}, f32[4,16,384]{2,1,0:T(8,128)}, u32[]{:S(2)}) copy-start(f32[4,16,384]{2,1,0:T(8,128)} %get-tuple-element.59) | copy-start | bytes 294916
  62.6 1.9 %copy-start.26 = (f32[1,32,16,384]{3,2,1,0:T(8,128)S(1)}, f32[1,32,16,384]{3,2,1,0:T(8,128)}, u32[]{:S(2)}) copy-start(f32[1,32,16,384]{3,2,1,0:T(8,128)} %param.20) | copy-start | bytes 2359300
  64.1 7.1 %copy-start.8 = (f32[24,16,384]{2,1,0:T(8,128)S(1)}, f32[24,16,384]{2,1,0:T(8,128)}, u32[]{:S(2)}) copy-start(f32[24,16,384]{2,1,0:T(8,128)} %fusion.121) | copy-start | bytes 1769476
  64.1 7.1 %slice-start.1 = ((f32[512,384]{1,0:T(8,128)}), f32[384,384]{1,0:T(8,128)S(1)}, s32[]{:S(2)}) async-start(f32[512,384]{1,0:T(8,128)} %copy-done.11), calls=%async_computation.3 | async-start | bytes 1179648 | tf_op jit(solution)/shard_map/slice | solution.py:193
  64.5 11.2 %collective-permute-start.3 = (f32[4,16,384]{2,1,0:T(8,128)S(1)}, f32[4,16,384]{2,1,0:T(8,128)S(1)}, u32[]{:S(2)}, u32[]{:S(2)}) collective-permute-start(f32[4,16,384]{2,1,0:T(8,128)S(1)} %get-tuple-element.39), channel_id=1, source_target_pairs={{1,0},{2,1},{3,2},{4,3},{5,4},{6,5},{7,6},{8,7},{9,8},{10,9},{11,1... | collective-permute-start | bytes 294920 | tf_op jit(solution)/shard_map/ppermute | solution.py:43
  66.4 9.6 %collective-permute-start.2 = (f32[4,16,384]{2,1,0:T(8,128)S(1)}, f32[4,16,384]{2,1,0:T(8,128)S(1)}, u32[]{:S(2)}, u32[]{:S(2)}) collective-permute-start(f32[4,16,384]{2,1,0:T(8,128)S(1)} %get-tuple-element.40), channel_id=1, source_target_pairs={{0,1},{1,2},{2,3},{3,4},{4,5},{5,6},{6,7},{7,8},{8,9},{9,10},{10,1... | collective-permute-start | bytes 294920 | tf_op jit(solution)/shard_map/ppermute | solution.py:42
  71.2 1.1 copy-start.7
  71.2 1.3 slice-start
  117.2 5.3 %copy-start.9 = (f32[24,16,384]{2,1,0:T(8,128)S(1)}, f32[24,16,384]{2,1,0:T(8,128)}, u32[]{:S(2)}) copy-start(f32[24,16,384]{2,1,0:T(8,128)} %get-tuple-element.36) | copy-start | bytes 1769476
  117.2 33.2 %all-to-all-start.1 = ((f32[32,1,16,384]{3,2,1,0:T(8,128)}), f32[32,1,16,384]{3,2,1,0:T(8,128)S(1)}, u32[]{:S(2)}, u32[]{:S(2)}) async-start(f32[32,1,16,384]{3,2,1,0:T(8,128)} %broadcast_in_dim.16), calls=%async_computation.1 | async-start | bytes 1572864 | tf_op jit(solution)/shard_map/all_to_all | solution.py:121

commit v6 on v4

--- a/solution.py
+++ b/solution.py
@@ -80,13 +80,13 @@
 
 def sample(field, rows, cols):
     width_x, width_y, width_z = field.shape
-    picked = jnp.dot(rows, field.reshape(width_x * width_y, width_z), precision=lax.Precision.HIGHEST)
+    picked = jnp.dot(rows, field.reshape(width_x * width_y, width_z), precision=lax.Precision.HIGH)
     return jnp.sum(picked * cols, axis=1)
 
 
 def receiver_grid(shape, rows, cols, values):
     placed = lax.dot_general(
-        rows * values[:, None], cols, (((0,), (0,)), ((), ())), precision=lax.Precision.HIGHEST
+        rows * values[:, None], cols, (((0,), (0,)), ((), ())), precision=lax.Precision.HIGH
     )
     return placed.reshape(shape)
 

time: 132 us -> 126 us (0.955)
  the two profiles are of different devices: /device:TPU:10 before, /device:TPU:1 now
where the time goes in v6:
time: 126 us
  blocking collectives  70 us (56%)
  starting transfers between devices  17.2 us (14%)
  other arithmetic  14.5 us (12%)
  local copies, waits for them, and re-layouts  9.33 us (7%)
  matrix products  8.07 us (6%)
  between operations  6.83 us (5%)
    all_to_all x1, blocking collectives, shot_sum(): mine = jnp.sum(lax.all_to_all(pieces, 'shot', 0, 0, tiled=False), axis=0)  35.5 us
    all_to_all x1, blocking collectives, shot_sum(): return lax.all_to_all(spread, 'shot', 0, 0, tiled=False).reshape(term.shape)  34.5 us
    ppermute x1, starting transfers between devices, wide_halo(): highs = lax.ppermute(heads, 'dom', backward)  8.92 us
    dot_general x2, matrix products, receiver_grid(): lax.dot_general(rows * values[:, None], cols, (((0,), (0,)), ((), ())), p...  5.37 us
    add x3, other arithmetic, advance(): 2.0 * current[R:-R] - before + coef * (laplace_core(current) + sources)  4.92 us
    add x2, other arithmetic, laplace_core(): total + weight * (padded[:, R:R + width_y, R + offset:R + offset + width_...  4.69 us
    reshape x1, other arithmetic, shot_sum(): pieces = term.reshape((count, term.shape[0] // count) + term.shape[1:])  3.9 us
    ppermute x1, starting transfers between devices, with_halo(): lax.ppermute(lax.slice_in_dim(block, block.shape[dim] - width, None, axis...  3.88 us
  transfers between devices with their start and end apart: 4, of which 0 were waited for; matrix products, arithmetic and copies ran while one was open for 3% of the time, Pallas kernels for 0%

profile of v6, /device:TPU:1, one launch (start us, length us, event | category | flops | bytes accessed | tf_op | source)
XLA Modules:
  0.0 125.9 jit_solution(10468332529259761819)
XLA Ops:
  0.6 1.0 fusion.175
  1.6 1.1 slice_bitcast_fusion.1
  2.6 1.1 slice_bitcast_fusion.4
  3.7 0.0 copy-start.14
  3.7 0.0 copy-start.15
  3.7 0.0 copy-start.13
  3.8 0.0 copy-start.11
  3.8 0.0 copy-start.12
  3.8 0.0 copy-start.10
  3.8 0.0 copy-start
  3.8 8.9 %collective-permute-start.1 = (f32[20,16,384]{2,1,0:T(8,128)S(1)}, f32[20,16,384]{2,1,0:T(8,128)S(1)}, u32[]{:S(2)}, u32[]{:S(2)}) collective-permute-start(f32[20,16,384]{2,1,0:T(8,128)S(1)} %pad_maximum_fusion.6), channel_id=1, source_target_pairs={{1,0},{2,1},{3,2},{4,3},{5,4},{6,5},{7,6},{8,7},{9,8},{10,9},{11,1... | collective-permute-start | bytes 1474568 | tf_op jit(solution)/shard_map/ppermute | solution.py:32
  12.8 1.9 %collective-permute-start = (f32[20,16,384]{2,1,0:T(8,128)S(1)}, f32[20,16,384]{2,1,0:T(8,128)S(1)}, u32[]{:S(2)}, u32[]{:S(2)}) collective-permute-start(f32[20,16,384]{2,1,0:T(8,128)S(1)} %pad_maximum_fusion.5), channel_id=1, source_target_pairs={{0,1},{1,2},{2,3},{3,4},{4,5},{5,6},{6,7},{7,8},{8,9},{9,10},{10,1... | collective-permute-start | bytes 1474568 | tf_op jit(solution)/shard_map/ppermute | solution.py:31
  16.7 0.7 and_reduce_fusion
  17.5 0.7 fusion.179
  20.7 0.0 copy-start.9
  20.7 0.1 pad_maximum_fusion
  20.8 0.7 copy-done.9
  21.5 0.1 slice.569
  21.5 2.8 %fusion.26 = f32[40,16,384]{2,1,0:T(8,128)S(1)} fusion(f32[40,16,384]{2,1,0:T(8,128)S(1)} %slice.569, f32[48,16,384]{2,1,0:T(8,128)S(1)} %pad_maximum_fusion, f32[8,16,384]{2,1,0:T(8,128)S(1)} %slice.568, f32[32,16,384]{2,1,0:T(8,128)S(1)} %bitcast.54, f32[8,16,384]{2,1,0:T(8,128)S(1)} %slice.567), kind=kLoop, calls=%fused_computation.107 | loop fusion | flops 9584640 | bytes 9043968 | tf_op jit(solution)/shard_map/add | solution.py:56
  24.3 0.6 add.403
  25.6 0.1 add.406
  25.8 1.3 %fusion.177 = (f32[4,16,384]{2,1,0:T(8,128)S(1)}, f32[4,16,384]{2,1,0:T(8,128)S(1)}, f32[4,16,384]{2,1,0:T(8,128)S(1)}) fusion(f32[20,16,384]{2,1,0:T(8,128)} %copy-done.9), kind=kLoop, calls=%fused_computation.297 | loop fusion | bytes 589824 | tf_op jit(solution)/shard_map/slice | solution.py:35
  27.1 1.9 %fusion.45 = f32[40,16,384]{2,1,0:T(8,128)S(1)} fusion(f32[4,16,384]{2,1,0:T(8,128)S(1)} %get-tuple-element.41, f32[32,16,384]{2,1,0:T(8,128)} %bitcast.55, f32[4,16,384]{2,1,0:T(8,128)S(1)} %get-tuple-element.44, f32[40,16,384]{2,1,0:T(8,128)} %copy-done.4, f32[4,16,384]{2,1,0:T(8,128)S(1)} %get-tuple-element.40, f32[32,16,384]{2,1,0:T(8,128)} %param.17, ...), kind=kLoop, calls=%fused_computation.130 | loop fusion | flops 1966080 | bytes 4915200 | tf_op jit(solution)/shard_map/add | solution.py:133
  29.0 0.1 slice.580
  29.1 0.0 copy-start.5
  29.1 0.0 copy-start.1
  29.1 1.9 %fusion.113 = f32[32,16,384]{2,1,0:T(8,128)S(1)} fusion(f32[32,16,384]{2,1,0:T(8,128)S(1)} %slice.580, f32[40,16,384]{2,1,0:T(8,128)S(1)} %fusion.45), kind=kLoop, calls=%fused_computation.212 | loop fusion | flops 7274496 | bytes 7864320 | tf_op jit(solution)/shard_map/add | solution.py:56
  31.0 0.6 add.432
  32.3 0.1 add.435
  32.4 0.0 copy-start.6
  32.5 0.0 copy-start.16
  32.5 0.2 multiply_add_fusion
  32.7 0.0 copy-start.7
  32.7 0.9 copy-done.6
  33.6 1.4 %select_reduce_fusion = f32[1024]{0:T(1024)S(1)} fusion(f32[512,384]{1,0:T(8,128)S(1)} %bitcast.58, s32[1024]{0:T(1024)S(1)} %bitcast.66, s32[1024]{0:T(1024)S(1)} %bitcast.70), kind=kOutput, calls=%fused_computation.71 | convolution fusion | flops 1209662464 | bytes 798720 | tf_op jit(solution)/shard_map/dot_general | solution.py:83
  35.0 1.3 %select_reduce_fusion.1 = f32[1024]{0:T(1024)S(1)} fusion(f32[512,384]{1,0:T(8,128)S(1)} %bitcast.59, s32[1024]{0:T(1024)S(1)} %bitcast.67, s32[1024]{0:T(1024)S(1)} %bitcast.71), kind=kOutput, calls=%fused_computation.72 | convolution fusion | flops 1209662464 | bytes 798720 | tf_op jit(solution)/shard_map/dot_general | solution.py:83
  36.3 0.0 copy-start.3
  36.3 2.7 %fusion.2 = f32[512,384]{1,0:T(8,128)S(1)} fusion(f32[1024]{0:T(1024)S(1)} %sub.65, s32[1024]{0:T(1024)S(1)} %bitcast.68, s32[1024]{0:T(1024)S(1)} %bitcast.72), kind=kOutput, calls=%fused_computation.66 | convolution fusion | flops 1209401344 | bytes 798720 | tf_op jit(solution)/shard_map/dot_general | solution.py:88
  39.1 2.8 %fusion.85 = f32[32,16,384]{2,1,0:T(8,128)S(1)} fusion(f32[32,16,384]{2,1,0:T(8,128)S(1)} %copy-done.1, f32[32,16,384]{2,1,0:T(8,128)S(1)} %bitcast.61, f32[32,16,384]{2,1,0:T(8,128)S(1)} %bitcast.56, f32[4,16,384]{2,1,0:T(8,128)S(1)} %get-tuple-element.42, f32[4,16,384]{2,1,0:T(8,128)S(1)} %get-tuple-element.39, f32[1,32,16,384]{3,2,1,0:T(8,128)S(1)} %copy-done.8), kind=kLoop, calls=%fused_computation.184 | loop fusion | flops 9830400 | bytes 4128768 | tf_op jit(solution)/shard_map/add | solution.py:133
  41.9 2.4 %collective-permute-start.2 = (f32[4,16,384]{2,1,0:T(8,128)S(1)}, f32[4,16,384]{2,1,0:T(8,128)S(1)}, u32[]{:S(2)}, u32[]{:S(2)}) collective-permute-start(f32[4,16,384]{2,1,0:T(8,128)S(1)} %get-tuple-element.29), channel_id=1, source_target_pairs={{1,0},{2,1},{3,2},{4,3},{5,4},{6,5},{7,6},{8,7},{9,8},{10,9},{11,1... | collective-permute-start | bytes 294920 | tf_op jit(solution)/shard_map/ppermute | solution.py:20
  44.3 3.9 %collective-permute-start.3 = (f32[4,16,384]{2,1,0:T(8,128)S(1)}, f32[4,16,384]{2,1,0:T(8,128)S(1)}, u32[]{:S(2)}, u32[]{:S(2)}) collective-permute-start(f32[4,16,384]{2,1,0:T(8,128)S(1)} %get-tuple-element.30), channel_id=1, source_target_pairs={{0,1},{1,2},{2,3},{3,4},{4,5},{5,6},{6,7},{7,8},{8,9},{9,10},{10,1... | collective-permute-start | bytes 294920 | tf_op jit(solution)/shard_map/ppermute | solution.py:17
  48.2 2.7 %fusion = f32[512,384]{1,0:T(8,128)S(1)} fusion(f32[1024]{0:T(1024)S(1)} %sub.67, s32[1024]{0:T(1024)S(1)} %bitcast.69, s32[1024]{0:T(1024)S(1)} %bitcast.73), kind=kOutput, calls=%fused_computation.64 | convolution fusion | flops 1209401344 | bytes 798720 | tf_op jit(solution)/shard_map/dot_general | solution.py:88
  51.0 3.9 %add_bitcast_fusion = (f32[32,1,16,384]{3,2,1,0:T(8,128)S(1)}, f32[32,16,384]{2,1,0:T(8,128)}) fusion(f32[32,16,384]{2,1,0:T(8,128)S(1)} %fusion.85, f32[32,16,384]{2,1,0:T(8,128)S(1)} %multiply_add_fusion, f32[1,32,16,384]{3,2,1,0:T(8,128)S(1)} %copy-done.2, f32[1,32,16,384]{3,2,1,0:T(8,128)S(1)} %copy-done, f32[40,16,384]{2,1,0:T(8,128)S(1)} %fusion.45, ...), kind=kLoop, calls=%fused_computation.277 | loop fusion | flops 11599872 | bytes 8060928 | tf_op jit(solution)/shard_map/reshape | solution.py:96
  54.9 35.5 %all_to_all.10 = f32[32,1,16,384]{3,2,1,0:T(8,128)S(1)} all-to-all(f32[32,1,16,384]{3,2,1,0:T(8,128)S(1)} %get-tuple-element.27), channel_id=1, replica_groups=mesh['shot'=32,'dom'=16] {'shot'}, dimensions={0} | all-to-all | bytes 1572864 | tf_op jit(solution)/shard_map/all_to_all | solution.py:97
  90.4 0.1 reduce_sum.29
  90.4 0.1 broadcast_in_dim.13
  90.5 34.5 %all_to_all.11 = f32[32,1,16,384]{3,2,1,0:T(8,128)S(1)} all-to-all(f32[32,1,16,384]{3,2,1,0:T(8,128)S(1)} %broadcast_in_dim.13), channel_id=1, replica_groups=mesh['shot'=32,'dom'=16] {'shot'}, dimensions={0} | all-to-all | bytes 1572864 | tf_op jit(solution)/shard_map/all_to_all | solution.py:99
  125.0 0.9 copy.26
  (32 shorter events, 0.2 us)
Async XLA Ops:
  3.7 13.0 %copy-start.14 = (s32[3]{0:T(128)S(1)}, s32[3]{0:T(128)}, u32[]{:S(2)}) copy-start(s32[3]{0:T(128)} %constant.103.clone.1) | copy-start | bytes 40
  3.7 13.0 %copy-start.15 = (s32[3]{0:T(128)S(1)}, s32[3]{0:T(128)}, u32[]{:S(2)}) copy-start(s32[3]{0:T(128)} %constant.97.clone.1) | copy-start | bytes 40
  3.7 13.7 %copy-start.13 = (f32[1,2]{1,0:T(1,128)S(1)}, f32[1,2]{1,0:T(1,128)}, u32[]{:S(2)}) copy-start(f32[1,2]{1,0:T(1,128)} %param.25) | copy-start | bytes 28
  3.8 16.8 %copy-start.11 = (s32[1,1024]{1,0:T(1,128)S(1)}, s32[1,1024]{1,0:T(1,128)}, u32[]{:S(2)}) copy-start(s32[1,1024]{1,0:T(1,128)} %param.26) | copy-start | bytes 12292
  3.8 16.8 %copy-start.12 = (s32[1,1024]{1,0:T(1,128)S(1)}, s32[1,1024]{1,0:T(1,128)}, u32[]{:S(2)}) copy-start(s32[1,1024]{1,0:T(1,128)} %param.27) | copy-start | bytes 12292
  3.8 16.8 %copy-start.10 = (f32[1,2,1024]{2,1,0:T(2,128)S(1)}, f32[1,2,1024]{2,1,0:T(2,128)}, u32[]{:S(2)}) copy-start(f32[1,2,1024]{2,1,0:T(2,128)} %param.29) | copy-start | bytes 24580
  3.8 16.9 %copy-start = (f32[1,32,16,384]{3,2,1,0:T(8,128)S(1)}, f32[1,32,16,384]{3,2,1,0:T(8,128)}, u32[]{:S(2)}) copy-start(f32[1,32,16,384]{3,2,1,0:T(8,128)} %param.19) | copy-start | bytes 2359300
  3.8 16.8 %collective-permute-start.1 = (f32[20,16,384]{2,1,0:T(8,128)S(1)}, f32[20,16,384]{2,1,0:T(8,128)S(1)}, u32[]{:S(2)}, u32[]{:S(2)}) collective-permute-start(f32[20,16,384]{2,1,0:T(8,128)S(1)} %pad_maximum_fusion.6), channel_id=1, source_target_pairs={{1,0},{2,1},{3,2},{4,3},{5,4},{6,5},{7,6},{8,7},{9,8},{10,9},{11,1... | collective-permute-start | bytes 1474568 | tf_op jit(solution)/shard_map/ppermute | solution.py:32
  12.8 7.9 %collective-permute-start = (f32[20,16,384]{2,1,0:T(8,128)S(1)}, f32[20,16,384]{2,1,0:T(8,128)S(1)}, u32[]{:S(2)}, u32[]{:S(2)}) collective-permute-start(f32[20,16,384]{2,1,0:T(8,128)S(1)} %pad_maximum_fusion.5), channel_id=1, source_target_pairs={{0,1},{1,2},{2,3},{3,4},{4,5},{5,6},{6,7},{7,8},{8,9},{9,10},{10,1... | collective-permute-start | bytes 1474568 | tf_op jit(solution)/shard_map/ppermute | solution.py:31
  20.7 0.8 copy-start.9
  25.7 1.4 %copy-start.4 = (f32[40,16,384]{2,1,0:T(8,128)}, f32[40,16,384]{2,1,0:T(8,128)S(1)}, u32[]{:S(2)}) copy-start(f32[40,16,384]{2,1,0:T(8,128)S(1)} %add.406) | copy-start | bytes 2949124
  29.1 1.9 %copy-start.5 = (f32[32,16,384]{2,1,0:T(8,128)}, f32[32,16,384]{2,1,0:T(8,128)S(1)}, u32[]{:S(2)}) copy-start(f32[32,16,384]{2,1,0:T(8,128)S(1)} %slice.580) | copy-start | bytes 2359300
  29.1 3.3 %copy-start.1 = (f32[32,16,384]{2,1,0:T(8,128)S(1)}, f32[32,16,384]{2,1,0:T(8,128)}, u32[]{:S(2)}) copy-start(f32[32,16,384]{2,1,0:T(8,128)} %param.17) | copy-start | bytes 2359300
  32.4 1.1 copy-start.6
  32.5 1.1 copy-start.16
  32.7 18.3 %copy-start.7 = (f32[32,16,384]{2,1,0:T(8,128)}, f32[32,16,384]{2,1,0:T(8,128)S(1)}, u32[]{:S(2)}) copy-start(f32[32,16,384]{2,1,0:T(8,128)S(1)} %multiply_add_fusion) | copy-start | bytes 2359300
  36.3 2.7 %copy-start.3 = (f32[1,32,16,384]{3,2,1,0:T(8,128)S(1)}, f32[1,32,16,384]{3,2,1,0:T(8,128)}, u32[]{:S(2)}) copy-start(f32[1,32,16,384]{3,2,1,0:T(8,128)} %param.21) | copy-start | bytes 2359300
  36.3 2.7 %copy-start.8 = (f32[1,32,16,384]{3,2,1,0:T(8,128)S(1)}, f32[1,32,16,384]{3,2,1,0:T(8,128)}, u32[]{:S(2)}) copy-start(f32[1,32,16,384]{3,2,1,0:T(8,128)} %param.20) | copy-start | bytes 2359300
  41.9 9.0 %collective-permute-start.2 = (f32[4,16,384]{2,1,0:T(8,128)S(1)}, f32[4,16,384]{2,1,0:T(8,128)S(1)}, u32[]{:S(2)}, u32[]{:S(2)}) collective-permute-start(f32[4,16,384]{2,1,0:T(8,128)S(1)} %get-tuple-element.29), channel_id=1, source_target_pairs={{1,0},{2,1},{3,2},{4,3},{5,4},{6,5},{7,6},{8,7},{9,8},{10,9},{11,1... | collective-permute-start | bytes 294920 | tf_op jit(solution)/shard_map/ppermute | solution.py:20
  44.3 6.6 %collective-permute-start.3 = (f32[4,16,384]{2,1,0:T(8,128)S(1)}, f32[4,16,384]{2,1,0:T(8,128)S(1)}, u32[]{:S(2)}, u32[]{:S(2)}) collective-permute-start(f32[4,16,384]{2,1,0:T(8,128)S(1)} %get-tuple-element.30), channel_id=1, source_target_pairs={{0,1},{1,2},{2,3},{3,4},{4,5},{5,6},{6,7},{7,8},{8,9},{9,10},{10,1... | collective-permute-start | bytes 294920 | tf_op jit(solution)/shard_map/ppermute | solution.py:17
  48.2 2.7 %copy-start.2 = (f32[1,32,16,384]{3,2,1,0:T(8,128)S(1)}, f32[1,32,16,384]{3,2,1,0:T(8,128)}, u32[]{:S(2)}) copy-start(f32[1,32,16,384]{3,2,1,0:T(8,128)} %param.18) | copy-start | bytes 2359300

commit v7 on v6

--- a/solution.py
+++ b/solution.py
@@ -78,10 +78,14 @@
     return rows, cols
 
 
-def sample(field, rows, cols):
-    width_x, width_y, width_z = field.shape
-    picked = jnp.dot(rows, field.reshape(width_x * width_y, width_z), precision=lax.Precision.HIGH)
-    return jnp.sum(picked * cols, axis=1)
+def sample(fields, rows, cols):
+    width_x, width_y, width_z = fields[0].shape
+    flat = jnp.concatenate([f.reshape(width_x * width_y, width_z) for f in fields], axis=1)
+    picked = jnp.dot(rows, flat, precision=lax.Precision.HIGH)
+    return [
+        jnp.sum(picked[:, k * width_z : (k + 1) * width_z] * cols, axis=1)
+        for k in range(len(fields))
+    ]
 
 
 def receiver_grid(shape, rows, cols, values):
@@ -143,8 +147,9 @@
     recent_own = recent_x[2 * R : -2 * R]
     fwd_three = advance(fwd_two_x, recent_own, coefficient, source_grid(0, 1))
     rows, cols = selectors(shape, rxc, ryc, rzc, base)
-    resid_two = sample(fwd_two, rows, cols) - observed[0, 0]
-    resid_three = sample(fwd_three, rows, cols) - observed[0, 1]
+    at_two, at_three = sample((fwd_two, fwd_three), rows, cols)
+    resid_two = at_two - observed[0, 0]
+    resid_three = at_three - observed[0, 1]
     adj_two = advance(adj_now_x, later, coefficient, receiver_grid(shape, rows, cols, resid_three))
     adj_one = advance(
         with_halo(adj_two, (("dom", 0),), R), adj_now, coefficient,

time: 126 us -> 134 us (1.063)
  blocking collectives: 70 us -> 75.2 us
  other arithmetic: 14.5 us -> 16 us
    all_to_all x1, blocking collectives: 35.5 us -> 39.5 us  [shot_sum(): mine = jnp.sum(lax.all_to_all(pieces, 'shot', 0, 0, tiled=False), axis=0)]
    ppermute x1, starting transfers between devices: 8.92 us -> 5.51 us  [wide_halo(): highs = lax.ppermute(heads, 'dom', backward)]
    ppermute x1, starting transfers between devices: 1.92 us -> 4.73 us  [wide_halo(): lows = lax.ppermute(tails, 'dom', forward)]
    dot_general x2 -> x1, matrix products: 2.71 us -> 2.1 us  [sample(): picked = jnp.dot(rows, flat, precision=lax.Precision.HIGH)]
  transfers between devices with their start and end apart: 4 -> 4, of which waited for: 0 -> 1; matrix products, arithmetic and copies ran while one was open for 3% -> 3% of each run, Pallas kernels for 0% -> 0%
where the time goes in v7:
time: 134 us; the launch traced here: 133 us
  blocking collectives  75.2 us (56%)
  other arithmetic  16 us (12%)
  starting transfers between devices  16 us (12%)
  local copies, waits for them, and re-layouts  10.6 us (8%)
  matrix products  7.46 us (6%)
  between operations  6.78 us (5%)
    all_to_all x1, blocking collectives, shot_sum(): mine = jnp.sum(lax.all_to_all(pieces, 'shot', 0, 0, tiled=False), axis=0)  39.5 us
    all_to_all x1, blocking collectives, shot_sum(): return lax.all_to_all(spread, 'shot', 0, 0, tiled=False).reshape(term.shape)  35.7 us
    add x3, other arithmetic, advance(): 2.0 * current[R:-R] - before + coef * (laplace_core(current) + sources)  6.05 us
    ppermute x1, starting transfers between devices, wide_halo(): highs = lax.ppermute(heads, 'dom', backward)  5.51 us
    dot_general x2, matrix products, receiver_grid(): lax.dot_general(rows * values[:, None], cols, (((0,), (0,)), ((), ())), p...  5.37 us
    ppermute x1, starting transfers between devices, wide_halo(): lows = lax.ppermute(tails, 'dom', forward)  4.73 us
    add x2, other arithmetic, laplace_core(): total + weight * (padded[:, R:R + width_y, R + offset:R + offset + width_...  4.72 us
    reshape x1, other arithmetic, shot_sum(): pieces = term.reshape((count, term.shape[0] // count) + term.shape[1:])  3.9 us
  transfers between devices with their start and end apart: 4, of which 1 were waited for; matrix products, arithmetic and copies ran while one was open for 3% of the time, Pallas kernels for 0%

profile of v7, /device:TPU:1, one launch (start us, length us, event | category | flops | bytes accessed | tf_op | source)
XLA Modules:
  0.0 133.1 jit_solution(16416496866569536411)
XLA Ops:
  0.6 1.1 slice_bitcast_fusion.1
  1.7 0.0 copy-start.14
  1.7 0.0 copy-start.15
  1.7 0.0 copy-start.13
  1.7 0.0 copy-start.11
  1.7 0.0 copy-start.12
  1.7 0.0 copy-start.9
  1.8 1.0 fusion.179
  2.7 1.1 slice_bitcast_fusion.4
  3.8 0.0 copy-start
  3.9 4.7 %collective-permute-start = (f32[20,16,384]{2,1,0:T(8,128)S(1)}, f32[20,16,384]{2,1,0:T(8,128)S(1)}, u32[]{:S(2)}, u32[]{:S(2)}) collective-permute-start(f32[20,16,384]{2,1,0:T(8,128)S(1)} %pad_maximum_fusion.5), channel_id=1, source_target_pairs={{0,1},{1,2},{2,3},{3,4},{4,5},{5,6},{6,7},{7,8},{8,9},{9,10},{10,1... | collective-permute-start | bytes 1474568 | tf_op jit(solution)/shard_map/ppermute | solution.py:31
  8.6 5.5 %collective-permute-start.1 = (f32[20,16,384]{2,1,0:T(8,128)S(1)}, f32[20,16,384]{2,1,0:T(8,128)S(1)}, u32[]{:S(2)}, u32[]{:S(2)}) collective-permute-start(f32[20,16,384]{2,1,0:T(8,128)S(1)} %pad_maximum_fusion.6), channel_id=1, source_target_pairs={{1,0},{2,1},{3,2},{4,3},{5,4},{6,5},{7,6},{8,7},{9,8},{10,9},{11,1... | collective-permute-start | bytes 1474568 | tf_op jit(solution)/shard_map/ppermute | solution.py:32
  16.1 0.7 and_reduce_fusion
  16.9 0.7 fusion.183
  20.1 1.1 collective-permute-done.1
  21.2 0.1 pad_maximum_fusion
  21.3 0.7 copy-done.8
  21.9 0.1 slice.577
  22.0 2.8 %fusion.29 = f32[40,16,384]{2,1,0:T(8,128)S(1)} fusion(f32[40,16,384]{2,1,0:T(8,128)S(1)} %slice.577, f32[48,16,384]{2,1,0:T(8,128)S(1)} %pad_maximum_fusion, f32[8,16,384]{2,1,0:T(8,128)S(1)} %slice.576, f32[32,16,384]{2,1,0:T(8,128)S(1)} %bitcast.52, f32[8,16,384]{2,1,0:T(8,128)S(1)} %slice.575), kind=kLoop, calls=%fused_computation.110 | loop fusion | flops 9584640 | bytes 9043968 | tf_op jit(solution)/shard_map/add | solution.py:56
  24.8 0.6 add.403
  26.0 0.1 add.406
  26.2 1.3 %fusion.180 = (f32[4,16,384]{2,1,0:T(8,128)S(1)}, f32[4,16,384]{2,1,0:T(8,128)S(1)}, f32[4,16,384]{2,1,0:T(8,128)S(1)}) fusion(f32[20,16,384]{2,1,0:T(8,128)} %copy-done.8), kind=kLoop, calls=%fused_computation.300 | loop fusion | bytes 589824 | tf_op jit(solution)/shard_map/slice | solution.py:35
  27.6 1.9 %fusion.48 = f32[40,16,384]{2,1,0:T(8,128)S(1)} fusion(f32[4,16,384]{2,1,0:T(8,128)S(1)} %get-tuple-element.43, f32[32,16,384]{2,1,0:T(8,128)} %bitcast.56, f32[4,16,384]{2,1,0:T(8,128)S(1)} %get-tuple-element.46, f32[40,16,384]{2,1,0:T(8,128)} %copy-done.5, f32[4,16,384]{2,1,0:T(8,128)S(1)} %get-tuple-element.42, f32[32,16,384]{2,1,0:T(8,128)} %param.17, ...), kind=kLoop, calls=%fused_computation.133 | loop fusion | flops 1966080 | bytes 4915200 | tf_op jit(solution)/shard_map/add | solution.py:137
  29.5 0.1 slice.588
  29.6 0.0 copy-start.1
  29.6 1.9 %fusion.116 = f32[32,16,384]{2,1,0:T(8,128)S(1)} fusion(f32[32,16,384]{2,1,0:T(8,128)S(1)} %slice.588, f32[40,16,384]{2,1,0:T(8,128)S(1)} %fusion.48), kind=kLoop, calls=%fused_computation.215 | loop fusion | flops 7274496 | bytes 7864320 | tf_op jit(solution)/shard_map/add | solution.py:56
  31.5 0.0 copy-start.6
  31.5 0.9 copy-done.6
  32.4 0.6 add.432
  33.7 1.4 %add.435 = f32[32,16,384]{2,1,0:T(8,128)} dynamic-update-slice(f32[32,16,384]{2,1,0:T(8,128)} %copy-done.6, f32[1,1,1]{2,1,0:T(1,128)S(6)} %scatter-add.9, s32[]{:T(128)} %bitcast.17, s32[]{:T(128)} %bitcast.10, s32[]{:T(128)} %bitcast.11) | dynamic-update-slice | bytes 12 | tf_op jit(solution)/shard_map/add | solution.py:137
  35.0 1.3 multiply_add_fusion
  36.4 0.0 copy-start.2
  36.4 0.0 copy-start.10
  36.4 2.1 %fusion.4 = f32[1024,768]{0,1:T(8,128)S(1)} fusion(f32[512,384]{1,0:T(8,128)S(1)} %bitcast.54, f32[512,384]{1,0:T(8,128)S(1)} %bitcast.53, s32[1024]{0:T(1024)S(1)} %bitcast.64), kind=kOutput, calls=%fused_computation.69 | convolution fusion | flops 2416836608 | bytes 4722688 | tf_op jit(solution)/shard_map/dot_general | solution.py:84
  38.5 0.4 fusion.6
  38.9 0.0 copy-start.4
  38.9 2.7 %fusion.2 = f32[512,384]{1,0:T(8,128)S(1)} fusion(f32[1024]{0:T(1024)S(1)} %sub.65, s32[1024]{0:T(1024)S(1)} %bitcast.65, s32[1024]{0:T(1024)S(1)} %bitcast.68), kind=kOutput, calls=%fused_computation.66 | convolution fusion | flops 1209401344 | bytes 798720 | tf_op jit(solution)/shard_map/dot_general | solution.py:92
  41.6 2.8 %fusion.88 = f32[32,16,384]{2,1,0:T(8,128)S(1)} fusion(f32[32,16,384]{2,1,0:T(8,128)S(1)} %copy-done.1, f32[32,16,384]{2,1,0:T(8,128)S(1)} %bitcast.59, f32[32,16,384]{2,1,0:T(8,128)S(1)} %bitcast.57, f32[4,16,384]{2,1,0:T(8,128)S(1)} %get-tuple-element.44, f32[4,16,384]{2,1,0:T(8,128)S(1)} %get-tuple-element.41, f32[1,32,16,384]{3,2,1,0:T(8,128)S(1)} %copy-done.7), kind=kLoop, calls=%fused_computation.187 | loop fusion | flops 9830400 | bytes 4128768 | tf_op jit(solution)/shard_map/add | solution.py:137
  44.5 1.9 %collective-permute-start.2 = (f32[4,16,384]{2,1,0:T(8,128)S(1)}, f32[4,16,384]{2,1,0:T(8,128)S(1)}, u32[]{:S(2)}, u32[]{:S(2)}) collective-permute-start(f32[4,16,384]{2,1,0:T(8,128)S(1)} %get-tuple-element.31), channel_id=1, source_target_pairs={{1,0},{2,1},{3,2},{4,3},{5,4},{6,5},{7,6},{8,7},{9,8},{10,9},{11,1... | collective-permute-start | bytes 294920 | tf_op jit(solution)/shard_map/ppermute | solution.py:20
  46.4 3.8 %collective-permute-start.3 = (f32[4,16,384]{2,1,0:T(8,128)S(1)}, f32[4,16,384]{2,1,0:T(8,128)S(1)}, u32[]{:S(2)}, u32[]{:S(2)}) collective-permute-start(f32[4,16,384]{2,1,0:T(8,128)S(1)} %get-tuple-element.32), channel_id=1, source_target_pairs={{0,1},{1,2},{2,3},{3,4},{4,5},{5,6},{6,7},{7,8},{8,9},{9,10},{10,1... | collective-permute-start | bytes 294920 | tf_op jit(solution)/shard_map/ppermute | solution.py:17
  50.2 0.0 copy-start.3
  50.2 2.7 %fusion = f32[512,384]{1,0:T(8,128)S(1)} fusion(f32[1024]{0:T(1024)S(1)} %sub.67, s32[1024]{0:T(1024)S(1)} %bitcast.66, s32[1024]{0:T(1024)S(1)} %bitcast.69), kind=kOutput, calls=%fused_computation.64 | convolution fusion | flops 1209401344 | bytes 798720 | tf_op jit(solution)/shard_map/dot_general | solution.py:92
  53.0 3.9 %add_bitcast_fusion = (f32[32,1,16,384]{3,2,1,0:T(8,128)S(1)}, f32[32,16,384]{2,1,0:T(8,128)}) fusion(f32[32,16,384]{2,1,0:T(8,128)S(1)} %fusion.88, f32[32,16,384]{2,1,0:T(8,128)S(1)} %multiply_add_fusion, f32[1,32,16,384]{3,2,1,0:T(8,128)S(1)} %copy-done.3, f32[1,32,16,384]{3,2,1,0:T(8,128)S(1)} %copy-done, f32[40,16,384]{2,1,0:T(8,128)S(1)} %fusion.48, ...), kind=kLoop, calls=%fused_computation.280 | loop fusion | flops 11599872 | bytes 8060928 | tf_op jit(solution)/shard_map/reshape | solution.py:100
  56.9 39.5 %all_to_all.10 = f32[32,1,16,384]{3,2,1,0:T(8,128)S(1)} all-to-all(f32[32,1,16,384]{3,2,1,0:T(8,128)S(1)} %get-tuple-element.29), channel_id=1, replica_groups=mesh['shot'=32,'dom'=16] {'shot'}, dimensions={0} | all-to-all | bytes 1572864 | tf_op jit(solution)/shard_map/all_to_all | solution.py:101
  96.3 0.1 reduce_sum.29
  96.4 0.1 broadcast_in_dim.13
  96.5 35.7 %all_to_all.11 = f32[32,1,16,384]{3,2,1,0:T(8,128)S(1)} all-to-all(f32[32,1,16,384]{3,2,1,0:T(8,128)S(1)} %broadcast_in_dim.13), channel_id=1, replica_groups=mesh['shot'=32,'dom'=16] {'shot'}, dimensions={0} | all-to-all | bytes 1572864 | tf_op jit(solution)/shard_map/all_to_all | solution.py:103
  132.2 0.9 copy.22
  (30 shorter events, 0.2 us)
Async XLA Ops:
  1.7 14.4 %copy-start.14 = (s32[3]{0:T(128)S(1)}, s32[3]{0:T(128)}, u32[]{:S(2)}) copy-start(s32[3]{0:T(128)} %constant.103.clone.1) | copy-start | bytes 40
  1.7 14.4 %copy-start.15 = (s32[3]{0:T(128)S(1)}, s32[3]{0:T(128)}, u32[]{:S(2)}) copy-start(s32[3]{0:T(128)} %constant.97.clone.1) | copy-start | bytes 40
  1.7 15.2 %copy-start.13 = (f32[1,2]{1,0:T(1,128)S(1)}, f32[1,2]{1,0:T(1,128)}, u32[]{:S(2)}) copy-start(f32[1,2]{1,0:T(1,128)} %param.25) | copy-start | bytes 28
  1.7 18.3 %copy-start.11 = (s32[1,1024]{1,0:T(1,128)S(1)}, s32[1,1024]{1,0:T(1,128)}, u32[]{:S(2)}) copy-start(s32[1,1024]{1,0:T(1,128)} %param.26) | copy-start | bytes 12292
  1.7 18.3 %copy-start.12 = (s32[1,1024]{1,0:T(1,128)S(1)}, s32[1,1024]{1,0:T(1,128)}, u32[]{:S(2)}) copy-start(s32[1,1024]{1,0:T(1,128)} %param.27) | copy-start | bytes 12292
  1.7 18.3 %copy-start.9 = (f32[1,2,1024]{2,1,0:T(2,128)S(1)}, f32[1,2,1024]{2,1,0:T(2,128)}, u32[]{:S(2)}) copy-start(f32[1,2,1024]{2,1,0:T(2,128)} %param.29) | copy-start | bytes 24580
  3.8 17.4 %copy-start = (f32[1,32,16,384]{3,2,1,0:T(8,128)S(1)}, f32[1,32,16,384]{3,2,1,0:T(8,128)}, u32[]{:S(2)}) copy-start(f32[1,32,16,384]{3,2,1,0:T(8,128)} %param.19) | copy-start | bytes 2359300
  3.9 16.2 %collective-permute-start = (f32[20,16,384]{2,1,0:T(8,128)S(1)}, f32[20,16,384]{2,1,0:T(8,128)S(1)}, u32[]{:S(2)}, u32[]{:S(2)}) collective-permute-start(f32[20,16,384]{2,1,0:T(8,128)S(1)} %pad_maximum_fusion.5), channel_id=1, source_target_pairs={{0,1},{1,2},{2,3},{3,4},{4,5},{5,6},{6,7},{7,8},{8,9},{9,10},{10,1... | collective-permute-start | bytes 1474568 | tf_op jit(solution)/shard_map/ppermute | solution.py:31
  8.6 12.5 %collective-permute-start.1 = (f32[20,16,384]{2,1,0:T(8,128)S(1)}, f32[20,16,384]{2,1,0:T(8,128)S(1)}, u32[]{:S(2)}, u32[]{:S(2)}) collective-permute-start(f32[20,16,384]{2,1,0:T(8,128)S(1)} %pad_maximum_fusion.6), channel_id=1, source_target_pairs={{1,0},{2,1},{3,2},{4,3},{5,4},{6,5},{7,6},{8,7},{9,8},{10,9},{11,1... | collective-permute-start | bytes 1474568 | tf_op jit(solution)/shard_map/ppermute | solution.py:32
  21.2 0.8 copy-start.8
  26.2 1.4 %copy-start.5 = (f32[40,16,384]{2,1,0:T(8,128)}, f32[40,16,384]{2,1,0:T(8,128)S(1)}, u32[]{:S(2)}) copy-start(f32[40,16,384]{2,1,0:T(8,128)S(1)} %add.406) | copy-start | bytes 2949124
  29.6 5.5 %copy-start.1 = (f32[32,16,384]{2,1,0:T(8,128)S(1)}, f32[32,16,384]{2,1,0:T(8,128)}, u32[]{:S(2)}) copy-start(f32[32,16,384]{2,1,0:T(8,128)} %param.17) | copy-start | bytes 2359300
  31.5 0.9 copy-start.6
  36.4 16.6 %copy-start.2 = (f32[32,16,384]{2,1,0:T(8,128)}, f32[32,16,384]{2,1,0:T(8,128)S(1)}, u32[]{:S(2)}) copy-start(f32[32,16,384]{2,1,0:T(8,128)S(1)} %multiply_add_fusion) | copy-start | bytes 2359300
  36.4 2.1 %copy-start.10 = (s32[1,1024]{1,0:T(1,128)S(1)}, s32[1,1024]{1,0:T(1,128)}, u32[]{:S(2)}) copy-start(s32[1,1024]{1,0:T(1,128)} %param.28) | copy-start | bytes 12292
  38.9 2.7 %copy-start.4 = (f32[1,32,16,384]{3,2,1,0:T(8,128)S(1)}, f32[1,32,16,384]{3,2,1,0:T(8,128)}, u32[]{:S(2)}) copy-start(f32[1,32,16,384]{3,2,1,0:T(8,128)} %param.21) | copy-start | bytes 2359300
  38.9 2.7 %copy-start.7 = (f32[1,32,16,384]{3,2,1,0:T(8,128)S(1)}, f32[1,32,16,384]{3,2,1,0:T(8,128)}, u32[]{:S(2)}) copy-start(f32[1,32,16,384]{3,2,1,0:T(8,128)} %param.20) | copy-start | bytes 2359300
  44.5 8.5 %collective-permute-start.2 = (f32[4,16,384]{2,1,0:T(8,128)S(1)}, f32[4,16,384]{2,1,0:T(8,128)S(1)}, u32[]{:S(2)}, u32[]{:S(2)}) collective-permute-start(f32[4,16,384]{2,1,0:T(8,128)S(1)} %get-tuple-element.31), channel_id=1, source_target_pairs={{1,0},{2,1},{3,2},{4,3},{5,4},{6,5},{7,6},{8,7},{9,8},{10,9},{11,1... | collective-permute-start | bytes 294920 | tf_op jit(solution)/shard_map/ppermute | solution.py:20
  46.4 6.6 %collective-permute-start.3 = (f32[4,16,384]{2,1,0:T(8,128)S(1)}, f32[4,16,384]{2,1,0:T(8,128)S(1)}, u32[]{:S(2)}, u32[]{:S(2)}) collective-permute-start(f32[4,16,384]{2,1,0:T(8,128)S(1)} %get-tuple-element.32), channel_id=1, source_target_pairs={{0,1},{1,2},{2,3},{3,4},{4,5},{5,6},{6,7},{7,8},{8,9},{9,10},{10,1... | collective-permute-start | bytes 294920 | tf_op jit(solution)/shard_map/ppermute | solution.py:17
  50.2 2.7 %copy-start.3 = (f32[1,32,16,384]{3,2,1,0:T(8,128)S(1)}, f32[1,32,16,384]{3,2,1,0:T(8,128)}, u32[]{:S(2)}) copy-start(f32[1,32,16,384]{3,2,1,0:T(8,128)} %param.18) | copy-start | bytes 2359300

commit v8 on v6

--- a/solution.py
+++ b/solution.py
@@ -43,21 +43,26 @@
     width_y = center.shape[1]
     width_z = center.shape[2]
     total = 3.0 * stencil_weights[0] * center
-    padded = jnp.pad(center, ((0, 0), (R, R), (R, R)))
+    padded = jnp.pad(center, ((0, 0), (R, R), (0, 0)))
     for offset in range(1, R + 1):
         weight = stencil_weights[offset]
         total = total + weight * (
             extended[R + offset : R + offset + count] + extended[R - offset : R - offset + count]
         )
         total = total + weight * (
-            padded[:, R + offset : R + offset + width_y, R : R + width_z]
-            + padded[:, R - offset : R - offset + width_y, R : R + width_z]
+            padded[:, R + offset : R + offset + width_y]
+            + padded[:, R - offset : R - offset + width_y]
         )
-        total = total + weight * (
-            padded[:, R : R + width_y, R + offset : R + offset + width_z]
-            + padded[:, R : R + width_y, R - offset : R - offset + width_z]
-        )
-    return total
+    apart = lax.broadcasted_iota(jnp.int32, (width_z, width_z), 0) - lax.broadcasted_iota(
+        jnp.int32, (width_z, width_z), 1
+    )
+    band = jnp.zeros((width_z, width_z), jnp.float32)
+    for offset in range(1, R + 1):
+        band = jnp.where(jnp.abs(apart) == offset, stencil_weights[offset], band)
+    along_z = jnp.dot(
+        center.reshape(count * width_y, width_z), band, precision=lax.Precision.HIGHEST
+    )
+    return total + along_z.reshape(center.shape)
 
 
 def point_grid(shape, xcells, ycells, zcells, values, start):

time: 126 us -> 130 us (1.032)
  matrix products: 8.07 us -> 18.2 us
  other arithmetic: 14.5 us -> 5.82 us
  local copies, waits for them, and re-layouts: 9.33 us -> 11.3 us
    dot_general x0 -> x4, matrix products: none -> 10.1 us  [laplace_core(): jnp.dot(center.reshape(count * width_y, width_z), band, precision=lax.Pre...]
    add x2 -> x0, other arithmetic: 4.69 us -> none  [laplace_core(): total + weight * (padded[:, R:R + width_y, R + offset:R + offset + width_...]
    reshape x1, other arithmetic: 3.9 us -> 0.44 us  [shot_sum(): pieces = term.reshape((count, term.shape[0] // count) + term.shape[1:])]
    ppermute x1, starting transfers between devices: 3.88 us -> 2.56 us  [with_halo(): lax.ppermute(lax.slice_in_dim(block, block.shape[dim] - width, None, axis...]
  transfers between devices with their start and end apart: 4 -> 4, of which waited for: 0 -> 0; matrix products, arithmetic and copies ran while one was open for 3% -> 5% of each run, Pallas kernels for 0% -> 0%
where the time goes in v8:
time: 130 us; the launch traced here: 129 us
  blocking collectives  70.4 us (54%)
  matrix products  18.2 us (14%)
  starting transfers between devices  16.5 us (13%)
  local copies, waits for them, and re-layouts  11.3 us (9%)
  between operations  6.88 us (5%)
  other arithmetic  5.82 us (4%)
    all_to_all x1, blocking collectives, shot_sum(): mine = jnp.sum(lax.all_to_all(pieces, 'shot', 0, 0, tiled=False), axis=0)  35.4 us
    all_to_all x1, blocking collectives, shot_sum(): return lax.all_to_all(spread, 'shot', 0, 0, tiled=False).reshape(term.shape)  35 us
    dot_general x4, matrix products, laplace_core(): jnp.dot(center.reshape(count * width_y, width_z), band, precision=lax.Pre...  10.1 us
    ppermute x1, starting transfers between devices, wide_halo(): highs = lax.ppermute(heads, 'dom', backward)  8.79 us
    dot_general x2, matrix products, receiver_grid(): lax.dot_general(rows * values[:, None], cols, (((0,), (0,)), ((), ())), p...  5.37 us
    add x3, other arithmetic, advance(): 2.0 * current[R:-R] - before + coef * (laplace_core(current) + sources)  4.35 us
    ppermute x1, starting transfers between devices, with_halo(): lax.ppermute(lax.slice_in_dim(block, 0, width, axis=dim), axis, backward)  3.22 us
    slice x3, local copies, waits for them, and re-layouts, wide_halo(): f[f.shape[0] - w:]  3.05 us
  transfers between devices with their start and end apart: 4, of which 0 were waited for; matrix products, arithmetic and copies ran while one was open for 5% of the time, Pallas kernels for 0%

profile of v8, /device:TPU:1, one launch (start us, length us, event | category | flops | bytes accessed | tf_op | source)
XLA Modules:
  0.0 129.1 jit_solution(14476422518594446865)
XLA Ops:
  0.6 0.0 copy-start.5
  0.6 1.0 fusion.170
  1.7 1.1 slice_bitcast_fusion.1
  2.7 1.0 slice_bitcast_fusion.4
  3.8 8.8 %collective-permute-start.1 = (f32[20,16,384]{2,1,0:T(8,128)S(1)}, f32[20,16,384]{2,1,0:T(8,128)S(1)}, u32[]{:S(2)}, u32[]{:S(2)}) collective-permute-start(f32[20,16,384]{2,1,0:T(8,128)S(1)} %pad_maximum_fusion.6), channel_id=1, source_target_pairs={{1,0},{2,1},{3,2},{4,3},{5,4},{6,5},{7,6},{8,7},{9,8},{10,9},{11,1... | collective-permute-start | bytes 1474568 | tf_op jit(solution)/shard_map/ppermute | solution.py:32
  12.6 1.9 %collective-permute-start = (f32[20,16,384]{2,1,0:T(8,128)S(1)}, f32[20,16,384]{2,1,0:T(8,128)}, u32[]{:S(2)}, u32[]{:S(2)}) collective-permute-start(f32[20,16,384]{2,1,0:T(8,128)S(1)} %pad_maximum_fusion.5), channel_id=1, source_target_pairs={{0,1},{1,2},{2,3},{3,4},{4,5},{5,6},{6,7},{7,8},{8,9},{9,10},{10,1... | collective-permute-start | bytes 1474568 | tf_op jit(solution)/shard_map/ppermute | solution.py:31
  15.8 0.0 copy-start.16
  15.8 0.0 copy-start.17
  15.9 0.0 copy-start.15
  16.5 1.8 %convolution_bitcast_fusion = f32[512,384]{0,1:T(8,128)S(1)} fusion(f32[512,384]{1,0:T(8,128)S(1)} %bitcast.76), kind=kOutput, calls=%fused_computation.55 | convolution fusion | flops 907444224 | bytes 1572864 | tf_op jit(solution)/shard_map/dot_general | solution.py:62
  18.3 0.0 copy-start.13
  18.3 0.0 copy-start.14
  18.4 0.8 and_reduce_fusion
  19.2 0.6 fusion.174
  19.8 1.1 copy.19
  23.5 0.9 slice.439
  24.4 0.1 pad_maximum_fusion
  24.5 0.1 slice.441
  24.6 3.1 %convolution_add_fusion = f32[40,16,384]{2,1,0:T(8,128)S(1)} fusion(f32[48,16,384]{2,1,0:T(8,128)S(1)} %pad_maximum_fusion, f32[40,16,384]{2,1,0:T(8,128)S(1)} %slice.441, f32[8,16,384]{2,1,0:T(8,128)S(1)} %slice.440, f32[32,16,384]{2,1,0:T(8,128)S(1)} %bitcast.70, f32[8,16,384]{2,1,0:T(8,128)S(1)} %slice.439), kind=kOutput, calls=%fused_computation.54 | convolution fusion | flops 1140817920 | bytes 10223616 | tf_op jit(solution)/shard_map/dot_general | solution.py:62
  27.7 0.6 add.312
  29.0 0.1 add.315
  29.2 1.3 %fusion.172 = (f32[4,16,384]{2,1,0:T(8,128)S(1)}, f32[4,16,384]{2,1,0:T(8,128)S(1)}, f32[4,16,384]{2,1,0:T(8,128)S(1)}) fusion(f32[20,16,384]{2,1,0:T(8,128)} %collective-permute-done), kind=kLoop, calls=%fused_computation.267 | loop fusion | bytes 589824 | tf_op jit(solution)/shard_map/slice | solution.py:35
  30.5 1.9 %fusion.36 = f32[40,16,384]{2,1,0:T(8,128)S(1)} fusion(f32[4,16,384]{2,1,0:T(8,128)S(1)} %get-tuple-element.39, f32[32,16,384]{2,1,0:T(8,128)} %bitcast.71, f32[4,16,384]{2,1,0:T(8,128)S(1)} %get-tuple-element.42, f32[40,16,384]{2,1,0:T(8,128)} %copy-done.7, f32[4,16,384]{2,1,0:T(8,128)S(1)} %get-tuple-element.38, f32[32,16,384]{2,1,0:T(8,128)} %param.17, ...), kind=kLoop, calls=%fused_computation.93 | loop fusion | flops 1966080 | bytes 4915200 | tf_op jit(solution)/shard_map/add | solution.py:138
  32.4 0.1 slice.452
  32.5 0.0 copy-start.9
  32.5 2.5 %convolution_add_fusion.1 = f32[32,16,384]{2,1,0:T(8,128)S(1)} fusion(f32[40,16,384]{2,1,0:T(8,128)S(1)} %fusion.36, f32[32,16,384]{2,1,0:T(8,128)S(1)} %slice.452), kind=kOutput, calls=%fused_computation.56 | convolution fusion | flops 912556032 | bytes 8847360 | tf_op jit(solution)/shard_map/dot_general | solution.py:62
  35.1 0.6 add.334
  36.3 0.3 add.337
  36.6 0.0 copy-start.10
  36.7 0.2 multiply_add_fusion
  36.9 0.9 copy-done.10
  37.8 1.4 %select_reduce_fusion = f32[1024]{0:T(1024)S(1)} fusion(f32[512,384]{1,0:T(8,128)S(1)} %bitcast.79, s32[1024]{0:T(1024)S(1)} %bitcast.83, s32[1024]{0:T(1024)S(1)} %bitcast.87), kind=kOutput, calls=%fused_computation.39 | convolution fusion | flops 1209662464 | bytes 798720 | tf_op jit(solution)/shard_map/dot_general | solution.py:88
  39.2 1.4 %select_reduce_fusion.1 = f32[1024]{0:T(1024)S(1)} fusion(f32[512,384]{1,0:T(8,128)S(1)} %bitcast.74, s32[1024]{0:T(1024)S(1)} %bitcast.84, s32[1024]{0:T(1024)S(1)} %bitcast.88), kind=kOutput, calls=%fused_computation.40 | convolution fusion | flops 1209662464 | bytes 798720 | tf_op jit(solution)/shard_map/dot_general | solution.py:88
  40.6 0.0 copy-start.8
  40.6 2.7 %fusion.2 = f32[512,384]{1,0:T(8,128)S(1)} fusion(f32[1024]{0:T(1024)S(1)} %sub.78, s32[1024]{0:T(1024)S(1)} %bitcast.85, s32[1024]{0:T(1024)S(1)} %bitcast.89), kind=kOutput, calls=%fused_computation.10 | convolution fusion | flops 1209401344 | bytes 798720 | tf_op jit(solution)/shard_map/dot_general | solution.py:93
  43.3 2.2 %fusion.68 = f32[32,16,384]{2,1,0:T(8,128)S(1)} fusion(f32[32,16,384]{2,1,0:T(8,128)S(1)} %copy-done.1, f32[32,16,384]{2,1,0:T(8,128)S(1)} %bitcast.78, f32[32,16,384]{2,1,0:T(8,128)S(1)} %bitcast.72, f32[32,16,384]{2,1,0:T(8,128)S(1)} %bitcast.77, f32[4,16,384]{2,1,0:T(8,128)S(1)} %get-tuple-element.40, f32[4,16,384]{2,1,0:T(8,128)S(1)} %get-tuple-element.37, ...), kind=kLoop, calls=%fused_computation.139 | loop fusion | flops 7667712 | bytes 4915200 | tf_op jit(solution)/shard_map/add | solution.py:138
  45.5 3.2 %collective-permute-start.2 = (f32[4,16,384]{2,1,0:T(8,128)S(1)}, f32[4,16,384]{2,1,0:T(8,128)S(1)}, u32[]{:S(2)}, u32[]{:S(2)}) collective-permute-start(f32[4,16,384]{2,1,0:T(8,128)S(1)} %get-tuple-element.27), channel_id=1, source_target_pairs={{1,0},{2,1},{3,2},{4,3},{5,4},{6,5},{7,6},{8,7},{9,8},{10,9},{11,1... | collective-permute-start | bytes 294920 | tf_op jit(solution)/shard_map/ppermute | solution.py:20
  48.8 2.6 %collective-permute-start.3 = (f32[4,16,384]{2,1,0:T(8,128)S(1)}, f32[4,16,384]{2,1,0:T(8,128)S(1)}, u32[]{:S(2)}, u32[]{:S(2)}) collective-permute-start(f32[4,16,384]{2,1,0:T(8,128)S(1)} %get-tuple-element.28), channel_id=1, source_target_pairs={{0,1},{1,2},{2,3},{3,4},{4,5},{5,6},{6,7},{7,8},{8,9},{9,10},{10,1... | collective-permute-start | bytes 294920 | tf_op jit(solution)/shard_map/ppermute | solution.py:17
  51.4 2.7 %fusion = f32[512,384]{1,0:T(8,128)S(1)} fusion(f32[1024]{0:T(1024)S(1)} %sub.80, s32[1024]{0:T(1024)S(1)} %bitcast.86, s32[1024]{0:T(1024)S(1)} %bitcast.90), kind=kOutput, calls=%fused_computation.8 | convolution fusion | flops 1209401344 | bytes 798720 | tf_op jit(solution)/shard_map/dot_general | solution.py:93
  54.1 0.0 copy-start.2
  54.1 2.7 %fusion.8 = f32[32,16,384]{2,1,0:T(8,128)S(1)} fusion(f32[32,16,384]{2,1,0:T(8,128)S(1)} %copy-done.1, f32[32,16,384]{2,1,0:T(8,128)S(1)} %bitcast.91, f32[32,16,384]{2,1,0:T(8,128)S(1)} %fusion.68, f32[4,16,384]{2,1,0:T(8,128)S(1)} %collective-permute-done.3, f32[4,16,384]{2,1,0:T(8,128)S(1)} %collective-permute-done.2, f32[1,32,16,384]{3,2,1,0:T(8,128)S(1)} %copy-done.6), kind=kOutput, calls=%fused_computation.60 | convolution fusion | flops 915111936 | bytes 4915200 | tf_op jit(solution)/shard_map/dot_general | solution.py:62
  56.8 0.4 add_bitcast_fusion
  57.2 0.4 copy-done.11
  57.7 35.4 %all_to_all.10 = f32[32,1,16,384]{3,2,1,0:T(8,128)S(1)} all-to-all(f32[32,1,16,384]{3,2,1,0:T(8,128)S(1)} %add_bitcast_fusion), channel_id=1, replica_groups=mesh['shot'=32,'dom'=16] {'shot'}, dimensions={0} | all-to-all | bytes 1572864 | tf_op jit(solution)/shard_map/all_to_all | solution.py:102
  93.1 0.1 reduce_sum.29
  93.1 0.1 broadcast_in_dim.59
  93.2 35.0 %all_to_all.11 = f32[32,1,16,384]{3,2,1,0:T(8,128)S(1)} all-to-all(f32[32,1,16,384]{3,2,1,0:T(8,128)S(1)} %broadcast_in_dim.59), channel_id=1, replica_groups=mesh['shot'=32,'dom'=16] {'shot'}, dimensions={0} | all-to-all | bytes 1572864 | tf_op jit(solution)/shard_map/all_to_all | solution.py:104
  128.2 0.9 copy.31
  (39 shorter events, 0.2 us)
Async XLA Ops:
  0.6 2.1 %copy-start.5 = (f32[1,32,16,384]{3,2,1,0:T(8,128)S(1)}, f32[1,32,16,384]{3,2,1,0:T(8,128)}, u32[]{:S(2)}) copy-start(f32[1,32,16,384]{3,2,1,0:T(8,128)} %param.21) | copy-start | bytes 2359300
  3.8 19.7 %collective-permute-start.1 = (f32[20,16,384]{2,1,0:T(8,128)S(1)}, f32[20,16,384]{2,1,0:T(8,128)S(1)}, u32[]{:S(2)}, u32[]{:S(2)}) collective-permute-start(f32[20,16,384]{2,1,0:T(8,128)S(1)} %pad_maximum_fusion.6), channel_id=1, source_target_pairs={{1,0},{2,1},{3,2},{4,3},{5,4},{6,5},{7,6},{8,7},{9,8},{10,9},{11,1... | collective-permute-start | bytes 1474568 | tf_op jit(solution)/shard_map/ppermute | solution.py:32
  12.6 10.9 %collective-permute-start = (f32[20,16,384]{2,1,0:T(8,128)S(1)}, f32[20,16,384]{2,1,0:T(8,128)}, u32[]{:S(2)}, u32[]{:S(2)}) collective-permute-start(f32[20,16,384]{2,1,0:T(8,128)S(1)} %pad_maximum_fusion.5), channel_id=1, source_target_pairs={{0,1},{1,2},{2,3},{3,4},{4,5},{5,6},{6,7},{7,8},{8,9},{9,10},{10,1... | collective-permute-start | bytes 1474568 | tf_op jit(solution)/shard_map/ppermute | solution.py:31
  15.8 2.6 %copy-start.16 = (s32[3]{0:T(128)S(1)}, s32[3]{0:T(128)}, u32[]{:S(2)}) copy-start(s32[3]{0:T(128)} %constant.116.clone.1) | copy-start | bytes 40
  15.8 2.6 %copy-start.17 = (s32[3]{0:T(128)S(1)}, s32[3]{0:T(128)}, u32[]{:S(2)}) copy-start(s32[3]{0:T(128)} %constant.110.clone.1) | copy-start | bytes 40
  15.9 3.3 %copy-start.15 = (f32[1,2]{1,0:T(1,128)S(1)}, f32[1,2]{1,0:T(1,128)}, u32[]{:S(2)}) copy-start(f32[1,2]{1,0:T(1,128)} %param.25) | copy-start | bytes 28
  18.3 5.0 %copy-start.13 = (s32[1,1024]{1,0:T(1,128)S(1)}, s32[1,1024]{1,0:T(1,128)}, u32[]{:S(2)}) copy-start(s32[1,1024]{1,0:T(1,128)} %param.26) | copy-start | bytes 12292
  18.3 5.0 %copy-start.14 = (s32[1,1024]{1,0:T(1,128)S(1)}, s32[1,1024]{1,0:T(1,128)}, u32[]{:S(2)}) copy-start(s32[1,1024]{1,0:T(1,128)} %param.27) | copy-start | bytes 12292
  18.3 5.1 %copy-start.12 = (f32[1,2,1024]{2,1,0:T(2,128)S(1)}, f32[1,2,1024]{2,1,0:T(2,128)}, u32[]{:S(2)}) copy-start(f32[1,2,1024]{2,1,0:T(2,128)} %param.29) | copy-start | bytes 24580
  19.8 4.6 %copy-start = (f32[1,32,16,384]{3,2,1,0:T(8,128)S(1)}, f32[1,32,16,384]{3,2,1,0:T(8,128)}, u32[]{:S(2)}) copy-start(f32[1,32,16,384]{3,2,1,0:T(8,128)} %param.19) | copy-start | bytes 2359300
  29.1 1.4 %copy-start.7 = (f32[40,16,384]{2,1,0:T(8,128)}, f32[40,16,384]{2,1,0:T(8,128)S(1)}, u32[]{:S(2)}) copy-start(f32[40,16,384]{2,1,0:T(8,128)S(1)} %add.315) | copy-start | bytes 2949124
  32.5 2.5 %copy-start.9 = (f32[32,16,384]{2,1,0:T(8,128)}, f32[32,16,384]{2,1,0:T(8,128)S(1)}, u32[]{:S(2)}) copy-start(f32[32,16,384]{2,1,0:T(8,128)S(1)} %slice.452) | copy-start | bytes 2359300
  32.5 4.1 %copy-start.1 = (f32[32,16,384]{2,1,0:T(8,128)S(1)}, f32[32,16,384]{2,1,0:T(8,128)}, u32[]{:S(2)}) copy-start(f32[32,16,384]{2,1,0:T(8,128)} %param.17) | copy-start | bytes 2359300
  36.6 1.1 copy-start.10
  36.7 1.1 copy-start.18
  36.9 19.9 %copy-start.4 = (f32[32,16,384]{2,1,0:T(8,128)}, f32[32,16,384]{2,1,0:T(8,128)S(1)}, u32[]{:S(2)}) copy-start(f32[32,16,384]{2,1,0:T(8,128)S(1)} %multiply_add_fusion) | copy-start | bytes 2359300
  40.5 2.7 %copy-start.3 = (f32[512,384]{1,0:T(8,128)S(1)}, f32[512,384]{1,0:T(8,128)}, u32[]{:S(2)}) copy-start(f32[512,384]{1,0:T(8,128)} %copy.19) | copy-start | bytes 2359300
  40.5 2.7 %copy-start.6 = (f32[1,32,16,384]{3,2,1,0:T(8,128)S(1)}, f32[1,32,16,384]{3,2,1,0:T(8,128)}, u32[]{:S(2)}) copy-start(f32[1,32,16,384]{3,2,1,0:T(8,128)} %param.21) | copy-start | bytes 2359300
  40.6 2.7 %copy-start.8 = (f32[1,32,16,384]{3,2,1,0:T(8,128)S(1)}, f32[1,32,16,384]{3,2,1,0:T(8,128)}, u32[]{:S(2)}) copy-start(f32[1,32,16,384]{3,2,1,0:T(8,128)} %param.20) | copy-start | bytes 2359300
  45.5 8.5 %collective-permute-start.2 = (f32[4,16,384]{2,1,0:T(8,128)S(1)}, f32[4,16,384]{2,1,0:T(8,128)S(1)}, u32[]{:S(2)}, u32[]{:S(2)}) collective-permute-start(f32[4,16,384]{2,1,0:T(8,128)S(1)} %get-tuple-element.27), channel_id=1, source_target_pairs={{1,0},{2,1},{3,2},{4,3},{5,4},{6,5},{7,6},{8,7},{9,8},{10,9},{11,1... | collective-permute-start | bytes 294920 | tf_op jit(solution)/shard_map/ppermute | solution.py:20
  48.8 5.3 %collective-permute-start.3 = (f32[4,16,384]{2,1,0:T(8,128)S(1)}, f32[4,16,384]{2,1,0:T(8,128)S(1)}, u32[]{:S(2)}, u32[]{:S(2)}) collective-permute-start(f32[4,16,384]{2,1,0:T(8,128)S(1)} %get-tuple-element.28), channel_id=1, source_target_pairs={{0,1},{1,2},{2,3},{3,4},{4,5},{5,6},{6,7},{7,8},{8,9},{9,10},{10,1... | collective-permute-start | bytes 294920 | tf_op jit(solution)/shard_map/ppermute | solution.py:17
  54.1 2.7 %copy-start.2 = (f32[1,32,16,384]{3,2,1,0:T(8,128)S(1)}, f32[1,32,16,384]{3,2,1,0:T(8,128)}, u32[]{:S(2)}) copy-start(f32[1,32,16,384]{3,2,1,0:T(8,128)} %param.18) | copy-start | bytes 2359300
  56.8 0.9 copy-start.11

commit v9 on v8

--- a/solution.py
+++ b/solution.py
@@ -38,6 +38,29 @@
 
 
 def laplace_core(extended):
+    count = extended.shape[0] - 2 * R
+    center = extended[R : R + count]
+    width_y = center.shape[1]
+    width_z = center.shape[2]
+    total = 3.0 * stencil_weights[0] * center
+    padded = jnp.pad(center, ((0, 0), (R, R), (R, R)))
+    for offset in range(1, R + 1):
+        weight = stencil_weights[offset]
+        total = total + weight * (
+            extended[R + offset : R + offset + count] + extended[R - offset : R - offset + count]
+        )
+        total = total + weight * (
+            padded[:, R + offset : R + offset + width_y, R : R + width_z]
+            + padded[:, R - offset : R - offset + width_y, R : R + width_z]
+        )
+        total = total + weight * (
+            padded[:, R : R + width_y, R + offset : R + offset + width_z]
+            + padded[:, R : R + width_y, R - offset : R - offset + width_z]
+        )
+    return total
+
+
+def laplace_banded(extended):
     count = extended.shape[0] - 2 * R
     center = extended[R : R + count]
     width_y = center.shape[1]
@@ -134,8 +157,8 @@
     fields = (recent, older, coefficient, adj_now)
     recent_x, older_x, coef_x, adj_now_x = wide_halo(fields, widths)
 
-    def advance(current, before, coef, sources):
-        return 2.0 * current[R:-R] - before + coef * (laplace_core(current) + sources)
+    def advance(current, before, coef, sources, laplace=laplace_core):
+        return 2.0 * current[R:-R] - before + coef * (laplace(current) + sources)
 
     def source_grid(margin, step):
         return point_grid(
@@ -150,10 +173,12 @@
     rows, cols = selectors(shape, rxc, ryc, rzc, base)
     resid_two = sample(fwd_two, rows, cols) - observed[0, 0]
     resid_three = sample(fwd_three, rows, cols) - observed[0, 1]
-    adj_two = advance(adj_now_x, later, coefficient, receiver_grid(shape, rows, cols, resid_three))
+    adj_two = advance(
+        adj_now_x, later, coefficient, receiver_grid(shape, rows, cols, resid_three), laplace_banded
+    )
     adj_one = advance(
         with_halo(adj_two, (("dom", 0),), R), adj_now, coefficient,
-        receiver_grid(shape, rows, cols, resid_two),
+        receiver_grid(shape, rows, cols, resid_two), laplace_banded,
     )
     late_term = adj_two * (fwd_three - 2.0 * fwd_two + recent_own)
     early_term = adj_one * (fwd_two - 2.0 * recent_own + older)

time: 130 us -> 129 us (level)
  matrix products: 18.2 us -> 12.6 us
  other arithmetic: 5.82 us -> 10.5 us
    dot_general x4 -> x2, matrix products: 10.1 us -> 4.46 us  [laplace_banded(): jnp.dot(center.reshape(count * width_y, width_z), band, precision=lax.Pre...]
    add x3 -> x5, other arithmetic: 4.35 us -> 9.03 us  [the longest x2 4.69 us: laplace_core(): total + weight * (padded[:, R:R + width_y, R + offset:R + offset + width_...]
  transfers between devices with their start and end apart: 4 -> 4, of which waited for: 0 -> 0; matrix products, arithmetic and copies ran while one was open for 5% -> 6% of each run, Pallas kernels for 0% -> 0%
where the time goes in v9:
time: 129 us; the launch traced here: 128 us
  blocking collectives  70.5 us (55%)
  starting transfers between devices  16.5 us (13%)
  matrix products  12.6 us (10%)
  local copies, waits for them, and re-layouts  11.3 us (9%)
  other arithmetic  10.5 us (8%)
  between operations  6.89 us (5%)
    all_to_all x1, blocking collectives, shot_sum(): mine = jnp.sum(lax.all_to_all(pieces, 'shot', 0, 0, tiled=False), axis=0)  35.4 us
    all_to_all x1, blocking collectives, shot_sum(): return lax.all_to_all(spread, 'shot', 0, 0, tiled=False).reshape(term.shape)  35.1 us
    ppermute x1, starting transfers between devices, wide_halo(): highs = lax.ppermute(heads, 'dom', backward)  8.79 us
    dot_general x2, matrix products, receiver_grid(): lax.dot_general(rows * values[:, None], cols, (((0,), (0,)), ((), ())), p...  5.37 us
    add x2, other arithmetic, laplace_core(): total + weight * (padded[:, R:R + width_y, R + offset:R + offset + width_...  4.69 us
    dot_general x2, matrix products, laplace_banded(): jnp.dot(center.reshape(count * width_y, width_z), band, precision=lax.Pre...  4.46 us
    add x3, other arithmetic, advance(): return 2.0 * current[R:-R] - before + coef * (laplace(current) + sources)  4.35 us
    ppermute x1, starting transfers between devices, with_halo(): lax.ppermute(lax.slice_in_dim(block, 0, width, axis=dim), axis, backward)  3.21 us
  transfers between devices with their start and end apart: 4, of which 0 were waited for; matrix products, arithmetic and copies ran while one was open for 6% of the time, Pallas kernels for 0%

profile of v9, /device:TPU:1, one launch (start us, length us, event | category | flops | bytes accessed | tf_op | source)
XLA Modules:
  0.0 128.2 jit_solution(2234330070838469376)
XLA Ops:
  0.6 0.0 copy-start.8
  0.6 1.0 fusion.192
  1.7 1.1 slice_bitcast_fusion.1
  2.7 1.0 slice_bitcast_fusion.4
  3.8 8.8 %collective-permute-start.1 = (f32[20,16,384]{2,1,0:T(8,128)S(1)}, f32[20,16,384]{2,1,0:T(8,128)S(1)}, u32[]{:S(2)}, u32[]{:S(2)}) collective-permute-start(f32[20,16,384]{2,1,0:T(8,128)S(1)} %pad_maximum_fusion.6), channel_id=1, source_target_pairs={{1,0},{2,1},{3,2},{4,3},{5,4},{6,5},{7,6},{8,7},{9,8},{10,9},{11,1... | collective-permute-start | bytes 1474568 | tf_op jit(solution)/shard_map/ppermute | solution.py:32
  12.6 1.9 %collective-permute-start = (f32[20,16,384]{2,1,0:T(8,128)S(1)}, f32[20,16,384]{2,1,0:T(8,128)}, u32[]{:S(2)}, u32[]{:S(2)}) collective-permute-start(f32[20,16,384]{2,1,0:T(8,128)S(1)} %pad_maximum_fusion.5), channel_id=1, source_target_pairs={{0,1},{1,2},{2,3},{3,4},{4,5},{5,6},{6,7},{7,8},{8,9},{9,10},{10,1... | collective-permute-start | bytes 1474568 | tf_op jit(solution)/shard_map/ppermute | solution.py:31
  15.8 0.0 copy-start.16
  15.8 0.0 copy-start.17
  15.9 0.0 copy-start.15
  16.5 1.8 %convolution_bitcast_fusion = f32[512,384]{0,1:T(8,128)S(1)} fusion(f32[512,384]{1,0:T(8,128)S(1)} %bitcast.71), kind=kOutput, calls=%fused_computation.70 | convolution fusion | flops 907444224 | bytes 1572864 | tf_op jit(solution)/shard_map/dot_general | solution.py:85
  18.3 0.0 copy-start.13
  18.4 0.8 and_reduce_fusion
  19.2 0.6 fusion.196
  19.8 1.1 copy.18
  23.5 0.9 slice.503
  24.4 0.1 pad_maximum_fusion
  24.5 0.1 slice.505
  24.6 2.8 %fusion.29 = f32[40,16,384]{2,1,0:T(8,128)S(1)} fusion(f32[40,16,384]{2,1,0:T(8,128)S(1)} %slice.505, f32[48,16,384]{2,1,0:T(8,128)S(1)} %pad_maximum_fusion, f32[8,16,384]{2,1,0:T(8,128)S(1)} %slice.504, f32[32,16,384]{2,1,0:T(8,128)S(1)} %bitcast.64, f32[8,16,384]{2,1,0:T(8,128)S(1)} %slice.503), kind=kLoop, calls=%fused_computation.96 | loop fusion | flops 9584640 | bytes 9043968 | tf_op jit(solution)/shard_map/add | solution.py:56
  27.4 0.6 add.361
  28.6 0.1 add.364
  28.8 1.3 %fusion.194 = (f32[4,16,384]{2,1,0:T(8,128)S(1)}, f32[4,16,384]{2,1,0:T(8,128)S(1)}, f32[4,16,384]{2,1,0:T(8,128)S(1)}) fusion(f32[20,16,384]{2,1,0:T(8,128)} %collective-permute-done), kind=kLoop, calls=%fused_computation.303 | loop fusion | bytes 589824 | tf_op jit(solution)/shard_map/slice | solution.py:35
  30.2 1.9 %fusion.48 = f32[40,16,384]{2,1,0:T(8,128)S(1)} fusion(f32[4,16,384]{2,1,0:T(8,128)S(1)} %get-tuple-element.39, f32[32,16,384]{2,1,0:T(8,128)} %bitcast.65, f32[4,16,384]{2,1,0:T(8,128)S(1)} %get-tuple-element.42, f32[40,16,384]{2,1,0:T(8,128)} %copy-done.3, f32[4,16,384]{2,1,0:T(8,128)S(1)} %get-tuple-element.38, f32[32,16,384]{2,1,0:T(8,128)} %param.17, ...), kind=kLoop, calls=%fused_computation.119 | loop fusion | flops 1966080 | bytes 4915200 | tf_op jit(solution)/shard_map/add | solution.py:161
  32.1 0.1 slice.516
  32.2 0.0 copy-start.1
  32.2 1.9 %fusion.122 = f32[32,16,384]{2,1,0:T(8,128)S(1)} fusion(f32[32,16,384]{2,1,0:T(8,128)S(1)} %slice.516, f32[40,16,384]{2,1,0:T(8,128)S(1)} %fusion.48), kind=kLoop, calls=%fused_computation.207 | loop fusion | flops 7274496 | bytes 7864320 | tf_op jit(solution)/shard_map/add | solution.py:56
  34.1 0.6 add.390
  35.4 0.3 add.393
  35.7 0.0 copy-start.18
  35.7 0.2 multiply_add_fusion
  35.9 0.0 copy-start.5
  35.9 0.9 copy-done.7
  36.8 1.4 %select_reduce_fusion = f32[1024]{0:T(1024)S(1)} fusion(f32[512,384]{1,0:T(8,128)S(1)} %bitcast.70, s32[1024]{0:T(1024)S(1)} %bitcast.77, s32[1024]{0:T(1024)S(1)} %bitcast.81), kind=kOutput, calls=%fused_computation.55 | convolution fusion | flops 1209662464 | bytes 798720 | tf_op jit(solution)/shard_map/dot_general | solution.py:111
  38.2 1.4 %select_reduce_fusion.1 = f32[1024]{0:T(1024)S(1)} fusion(f32[512,384]{1,0:T(8,128)S(1)} %bitcast.68, s32[1024]{0:T(1024)S(1)} %bitcast.78, s32[1024]{0:T(1024)S(1)} %bitcast.82), kind=kOutput, calls=%fused_computation.56 | convolution fusion | flops 1209662464 | bytes 798720 | tf_op jit(solution)/shard_map/dot_general | solution.py:111
  39.6 0.0 copy-start.9
  39.6 0.0 copy-start.10
  39.6 2.7 %fusion.2 = f32[512,384]{1,0:T(8,128)S(1)} fusion(f32[1024]{0:T(1024)S(1)} %sub.72, s32[1024]{0:T(1024)S(1)} %bitcast.79, s32[1024]{0:T(1024)S(1)} %bitcast.83), kind=kOutput, calls=%fused_computation.34 | convolution fusion | flops 1209401344 | bytes 798720 | tf_op jit(solution)/shard_map/dot_general | solution.py:116
  42.3 2.2 %fusion.80 = f32[32,16,384]{2,1,0:T(8,128)S(1)} fusion(f32[32,16,384]{2,1,0:T(8,128)S(1)} %copy-done.1, f32[32,16,384]{2,1,0:T(8,128)S(1)} %bitcast.73, f32[32,16,384]{2,1,0:T(8,128)S(1)} %bitcast.66, f32[32,16,384]{2,1,0:T(8,128)S(1)} %bitcast.72, f32[4,16,384]{2,1,0:T(8,128)S(1)} %get-tuple-element.40, f32[4,16,384]{2,1,0:T(8,128)S(1)} %get-tuple-element.37, ...), kind=kLoop, calls=%fused_computation.165 | loop fusion | flops 7667712 | bytes 4915200 | tf_op jit(solution)/shard_map/add | solution.py:161
  44.6 3.2 %collective-permute-start.2 = (f32[4,16,384]{2,1,0:T(8,128)S(1)}, f32[4,16,384]{2,1,0:T(8,128)S(1)}, u32[]{:S(2)}, u32[]{:S(2)}) collective-permute-start(f32[4,16,384]{2,1,0:T(8,128)S(1)} %get-tuple-element.27), channel_id=1, source_target_pairs={{1,0},{2,1},{3,2},{4,3},{5,4},{6,5},{7,6},{8,7},{9,8},{10,9},{11,1... | collective-permute-start | bytes 294920 | tf_op jit(solution)/shard_map/ppermute | solution.py:20
  47.8 2.6 %collective-permute-start.3 = (f32[4,16,384]{2,1,0:T(8,128)S(1)}, f32[4,16,384]{2,1,0:T(8,128)S(1)}, u32[]{:S(2)}, u32[]{:S(2)}) collective-permute-start(f32[4,16,384]{2,1,0:T(8,128)S(1)} %get-tuple-element.28), channel_id=1, source_target_pairs={{0,1},{1,2},{2,3},{3,4},{4,5},{5,6},{6,7},{7,8},{8,9},{9,10},{10,1... | collective-permute-start | bytes 294920 | tf_op jit(solution)/shard_map/ppermute | solution.py:17
  50.4 2.7 %fusion = f32[512,384]{1,0:T(8,128)S(1)} fusion(f32[1024]{0:T(1024)S(1)} %sub.74, s32[1024]{0:T(1024)S(1)} %bitcast.80, s32[1024]{0:T(1024)S(1)} %bitcast.84), kind=kOutput, calls=%fused_computation.32 | convolution fusion | flops 1209401344 | bytes 798720 | tf_op jit(solution)/shard_map/dot_general | solution.py:116
  53.1 2.7 %fusion.8 = f32[32,16,384]{2,1,0:T(8,128)S(1)} fusion(f32[32,16,384]{2,1,0:T(8,128)S(1)} %copy-done.1, f32[32,16,384]{2,1,0:T(8,128)S(1)} %bitcast.85, f32[32,16,384]{2,1,0:T(8,128)S(1)} %fusion.80, f32[4,16,384]{2,1,0:T(8,128)S(1)} %collective-permute-done.3, f32[4,16,384]{2,1,0:T(8,128)S(1)} %collective-permute-done.2, f32[1,32,16,384]{3,2,1,0:T(8,128)S(1)} %copy-done.9), kind=kOutput, calls=%fused_computation.74 | convolution fusion | flops 915111936 | bytes 4915200 | tf_op jit(solution)/shard_map/dot_general | solution.py:85
  55.8 0.4 add_bitcast_fusion
  56.3 0.4 copy-done.11
  56.7 35.4 %all_to_all.10 = f32[32,1,16,384]{3,2,1,0:T(8,128)S(1)} all-to-all(f32[32,1,16,384]{3,2,1,0:T(8,128)S(1)} %add_bitcast_fusion), channel_id=1, replica_groups=mesh['shot'=32,'dom'=16] {'shot'}, dimensions={0} | all-to-all | bytes 1572864 | tf_op jit(solution)/shard_map/all_to_all | solution.py:125
  92.1 0.1 reduce_sum.29
  92.2 0.1 broadcast_in_dim.51
  92.2 35.1 %all_to_all.11 = f32[32,1,16,384]{3,2,1,0:T(8,128)S(1)} all-to-all(f32[32,1,16,384]{3,2,1,0:T(8,128)S(1)} %broadcast_in_dim.51), channel_id=1, replica_groups=mesh['shot'=32,'dom'=16] {'shot'}, dimensions={0} | all-to-all | bytes 1572864 | tf_op jit(solution)/shard_map/all_to_all | solution.py:127
  127.4 0.9 copy.26
  (39 shorter events, 0.2 us)
Async XLA Ops:
  0.6 2.1 %copy-start.8 = (f32[1,32,16,384]{3,2,1,0:T(8,128)S(1)}, f32[1,32,16,384]{3,2,1,0:T(8,128)}, u32[]{:S(2)}) copy-start(f32[1,32,16,384]{3,2,1,0:T(8,128)} %param.21) | copy-start | bytes 2359300
  3.8 19.7 %collective-permute-start.1 = (f32[20,16,384]{2,1,0:T(8,128)S(1)}, f32[20,16,384]{2,1,0:T(8,128)S(1)}, u32[]{:S(2)}, u32[]{:S(2)}) collective-permute-start(f32[20,16,384]{2,1,0:T(8,128)S(1)} %pad_maximum_fusion.6), channel_id=1, source_target_pairs={{1,0},{2,1},{3,2},{4,3},{5,4},{6,5},{7,6},{8,7},{9,8},{10,9},{11,1... | collective-permute-start | bytes 1474568 | tf_op jit(solution)/shard_map/ppermute | solution.py:32
  12.6 10.9 %collective-permute-start = (f32[20,16,384]{2,1,0:T(8,128)S(1)}, f32[20,16,384]{2,1,0:T(8,128)}, u32[]{:S(2)}, u32[]{:S(2)}) collective-permute-start(f32[20,16,384]{2,1,0:T(8,128)S(1)} %pad_maximum_fusion.5), channel_id=1, source_target_pairs={{0,1},{1,2},{2,3},{3,4},{4,5},{5,6},{6,7},{7,8},{8,9},{9,10},{10,1... | collective-permute-start | bytes 1474568 | tf_op jit(solution)/shard_map/ppermute | solution.py:31
  15.8 2.6 %copy-start.16 = (s32[3]{0:T(128)S(1)}, s32[3]{0:T(128)}, u32[]{:S(2)}) copy-start(s32[3]{0:T(128)} %constant.112.clone.1) | copy-start | bytes 40
  15.8 2.6 %copy-start.17 = (s32[3]{0:T(128)S(1)}, s32[3]{0:T(128)}, u32[]{:S(2)}) copy-start(s32[3]{0:T(128)} %constant.106.clone.1) | copy-start | bytes 40
  15.9 3.3 %copy-start.15 = (f32[1,2]{1,0:T(1,128)S(1)}, f32[1,2]{1,0:T(1,128)}, u32[]{:S(2)}) copy-start(f32[1,2]{1,0:T(1,128)} %param.25) | copy-start | bytes 28
  18.3 5.0 %copy-start.13 = (s32[1,1024]{1,0:T(1,128)S(1)}, s32[1,1024]{1,0:T(1,128)}, u32[]{:S(2)}) copy-start(s32[1,1024]{1,0:T(1,128)} %param.26) | copy-start | bytes 12292
  18.3 5.0 %copy-start.14 = (s32[1,1024]{1,0:T(1,128)S(1)}, s32[1,1024]{1,0:T(1,128)}, u32[]{:S(2)}) copy-start(s32[1,1024]{1,0:T(1,128)} %param.27) | copy-start | bytes 12292
  18.3 5.1 %copy-start.12 = (f32[1,2,1024]{2,1,0:T(2,128)S(1)}, f32[1,2,1024]{2,1,0:T(2,128)}, u32[]{:S(2)}) copy-start(f32[1,2,1024]{2,1,0:T(2,128)} %param.29) | copy-start | bytes 24580
  19.8 4.6 %copy-start = (f32[1,32,16,384]{3,2,1,0:T(8,128)S(1)}, f32[1,32,16,384]{3,2,1,0:T(8,128)}, u32[]{:S(2)}) copy-start(f32[1,32,16,384]{3,2,1,0:T(8,128)} %param.19) | copy-start | bytes 2359300
  28.8 1.4 %copy-start.3 = (f32[40,16,384]{2,1,0:T(8,128)}, f32[40,16,384]{2,1,0:T(8,128)S(1)}, u32[]{:S(2)}) copy-start(f32[40,16,384]{2,1,0:T(8,128)S(1)} %add.364) | copy-start | bytes 2949124
  32.2 1.9 %copy-start.6 = (f32[32,16,384]{2,1,0:T(8,128)}, f32[32,16,384]{2,1,0:T(8,128)S(1)}, u32[]{:S(2)}) copy-start(f32[32,16,384]{2,1,0:T(8,128)S(1)} %slice.516) | copy-start | bytes 2359300
  32.2 3.5 %copy-start.1 = (f32[32,16,384]{2,1,0:T(8,128)S(1)}, f32[32,16,384]{2,1,0:T(8,128)}, u32[]{:S(2)}) copy-start(f32[32,16,384]{2,1,0:T(8,128)} %param.17) | copy-start | bytes 2359300
  35.7 1.1 copy-start.7
  35.7 1.1 copy-start.18
  35.9 19.9 %copy-start.5 = (f32[32,16,384]{2,1,0:T(8,128)}, f32[32,16,384]{2,1,0:T(8,128)S(1)}, u32[]{:S(2)}) copy-start(f32[32,16,384]{2,1,0:T(8,128)S(1)} %multiply_add_fusion) | copy-start | bytes 2359300
  39.6 2.7 %copy-start.4 = (f32[512,384]{1,0:T(8,128)S(1)}, f32[512,384]{1,0:T(8,128)}, u32[]{:S(2)}) copy-start(f32[512,384]{1,0:T(8,128)} %copy.18) | copy-start | bytes 2359300
  39.6 2.7 %copy-start.9 = (f32[1,32,16,384]{3,2,1,0:T(8,128)S(1)}, f32[1,32,16,384]{3,2,1,0:T(8,128)}, u32[]{:S(2)}) copy-start(f32[1,32,16,384]{3,2,1,0:T(8,128)} %param.21) | copy-start | bytes 2359300
  39.6 2.7 %copy-start.10 = (f32[1,32,16,384]{3,2,1,0:T(8,128)S(1)}, f32[1,32,16,384]{3,2,1,0:T(8,128)}, u32[]{:S(2)}) copy-start(f32[1,32,16,384]{3,2,1,0:T(8,128)} %param.20) | copy-start | bytes 2359300
  44.6 8.5 %collective-permute-start.2 = (f32[4,16,384]{2,1,0:T(8,128)S(1)}, f32[4,16,384]{2,1,0:T(8,128)S(1)}, u32[]{:S(2)}, u32[]{:S(2)}) collective-permute-start(f32[4,16,384]{2,1,0:T(8,128)S(1)} %get-tuple-element.27), channel_id=1, source_target_pairs={{1,0},{2,1},{3,2},{4,3},{5,4},{6,5},{7,6},{8,7},{9,8},{10,9},{11,1... | collective-permute-start | bytes 294920 | tf_op jit(solution)/shard_map/ppermute | solution.py:20
  47.8 5.3 %collective-permute-start.3 = (f32[4,16,384]{2,1,0:T(8,128)S(1)}, f32[4,16,384]{2,1,0:T(8,128)S(1)}, u32[]{:S(2)}, u32[]{:S(2)}) collective-permute-start(f32[4,16,384]{2,1,0:T(8,128)S(1)} %get-tuple-element.28), channel_id=1, source_target_pairs={{0,1},{1,2},{2,3},{3,4},{4,5},{5,6},{6,7},{7,8},{8,9},{9,10},{10,1... | collective-permute-start | bytes 294920 | tf_op jit(solution)/shard_map/ppermute | solution.py:17
  53.1 2.7 %copy-start.2 = (f32[1,32,16,384]{3,2,1,0:T(8,128)S(1)}, f32[1,32,16,384]{3,2,1,0:T(8,128)}, u32[]{:S(2)}) copy-start(f32[1,32,16,384]{3,2,1,0:T(8,128)} %param.18) | copy-start | bytes 2359300
  55.8 0.9 copy-start.11

commit v10 on v6

--- a/solution.py
+++ b/solution.py
@@ -85,8 +85,13 @@
 
 
 def receiver_grid(shape, rows, cols, values):
+    high = values.astype(jnp.bfloat16)
+    rest = (values - high.astype(jnp.float32)).astype(jnp.bfloat16)
+    picks = rows.astype(jnp.bfloat16)
+    lhs = jnp.concatenate([picks * high[:, None], picks * rest[:, None]])
+    rhs = jnp.concatenate([cols, cols]).astype(jnp.bfloat16)
     placed = lax.dot_general(
-        rows * values[:, None], cols, (((0,), (0,)), ((), ())), precision=lax.Precision.HIGH
+        lhs, rhs, (((0,), (0,)), ((), ())), preferred_element_type=jnp.float32
     )
     return placed.reshape(shape)
 

time: 126 us -> 127 us (level); the launches traced: 126 us -> 124 us
  matrix products: 8.07 us -> 5.3 us
  other arithmetic: 14.5 us -> 16.5 us
    dot_general x2, matrix products: 5.37 us -> 2.59 us  [receiver_grid(): lax.dot_general(lhs, rhs, (((0,), (0,)), ((), ())), preferred_element_typ...]
    unnamed x35 -> x37, local copies, waits for them, and re-layouts: 2.53 us -> 2.59 us
  transfers between devices with their start and end apart: 4 -> 4, of which waited for: 0 -> 1; matrix products, arithmetic and copies ran while one was open for 3% -> 3% of each run, Pallas kernels for 0% -> 0%
where the time goes in v10:
time: 127 us; the launch traced here: 124 us
  blocking collectives  69.4 us (55%)
  starting transfers between devices  16.6 us (13%)
  other arithmetic  16.5 us (13%)
  local copies, waits for them, and re-layouts  9.38 us (7%)
  between operations  6.8 us (5%)
  matrix products  5.3 us (4%)
    all_to_all x1, blocking collectives, shot_sum(): mine = jnp.sum(lax.all_to_all(pieces, 'shot', 0, 0, tiled=False), axis=0)  35.3 us
    all_to_all x1, blocking collectives, shot_sum(): return lax.all_to_all(spread, 'shot', 0, 0, tiled=False).reshape(term.shape)  34.1 us
    ppermute x1, starting transfers between devices, wide_halo(): highs = lax.ppermute(heads, 'dom', backward)  8.92 us
    add x3, other arithmetic, advance(): 2.0 * current[R:-R] - before + coef * (laplace_core(current) + sources)  4.89 us
    add x2, other arithmetic, laplace_core(): total + weight * (padded[:, R:R + width_y, R + offset:R + offset + width_...  4.69 us
    reshape x1, other arithmetic, shot_sum(): pieces = term.reshape((count, term.shape[0] // count) + term.shape[1:])  3.87 us
    ppermute x1, starting transfers between devices, with_halo(): lax.ppermute(lax.slice_in_dim(block, block.shape[dim] - width, None, axis...  3.3 us
    slice x3, local copies, waits for them, and re-layouts, wide_halo(): f[f.shape[0] - w:]  3.08 us
  transfers between devices with their start and end apart: 4, of which 1 were waited for; matrix products, arithmetic and copies ran while one was open for 3% of the time, Pallas kernels for 0%

profile of v10, /device:TPU:1, one launch (start us, length us, event | category | flops | bytes accessed | tf_op | source)
XLA Modules:
  0.0 124.1 jit_solution(10876519041291740992)
XLA Ops:
  0.6 1.0 fusion.177
  1.6 1.1 slice_bitcast_fusion.1
  2.6 1.1 slice_bitcast_fusion.4
  3.7 0.0 copy-start.13
  3.7 0.0 copy-start.14
  3.7 0.0 copy-start.16
  3.8 0.0 copy-start.17
  3.8 0.0 copy-start.15
  3.8 0.0 copy-start.12
  3.9 8.9 %collective-permute-start.1 = (f32[20,16,384]{2,1,0:T(8,128)S(1)}, f32[20,16,384]{2,1,0:T(8,128)S(1)}, u32[]{:S(2)}, u32[]{:S(2)}) collective-permute-start(f32[20,16,384]{2,1,0:T(8,128)S(1)} %pad_maximum_fusion.6), channel_id=1, source_target_pairs={{1,0},{2,1},{3,2},{4,3},{5,4},{6,5},{7,6},{8,7},{9,8},{10,9},{11,1... | collective-permute-start | bytes 1474568 | tf_op jit(solution)/shard_map/ppermute | solution.py:32
  12.8 1.9 %collective-permute-start = (f32[20,16,384]{2,1,0:T(8,128)S(1)}, f32[20,16,384]{2,1,0:T(8,128)S(1)}, u32[]{:S(2)}, u32[]{:S(2)}) collective-permute-start(f32[20,16,384]{2,1,0:T(8,128)S(1)} %pad_maximum_fusion.5), channel_id=1, source_target_pairs={{0,1},{1,2},{2,3},{3,4},{4,5},{5,6},{6,7},{7,8},{8,9},{9,10},{10,1... | collective-permute-start | bytes 1474568 | tf_op jit(solution)/shard_map/ppermute | solution.py:31
  16.8 0.8 and_reduce_fusion
  17.5 0.6 fusion.181
  20.7 1.0 iota_compare_fusion.3
  21.7 0.0 copy-start.9
  21.8 0.1 pad_maximum_fusion
  21.8 0.7 copy-done.9
  22.5 0.1 slice.569
  22.6 2.8 %fusion.28 = f32[40,16,384]{2,1,0:T(8,128)S(1)} fusion(f32[40,16,384]{2,1,0:T(8,128)S(1)} %slice.569, f32[48,16,384]{2,1,0:T(8,128)S(1)} %pad_maximum_fusion, f32[8,16,384]{2,1,0:T(8,128)S(1)} %slice.568, f32[32,16,384]{2,1,0:T(8,128)S(1)} %bitcast.54, f32[8,16,384]{2,1,0:T(8,128)S(1)} %slice.567), kind=kLoop, calls=%fused_computation.111 | loop fusion | flops 9584640 | bytes 9043968 | tf_op jit(solution)/shard_map/add | solution.py:56
  25.4 0.6 add.403
  26.5 0.1 add.406
  26.7 1.3 %fusion.179 = (f32[4,16,384]{2,1,0:T(8,128)S(1)}, f32[4,16,384]{2,1,0:T(8,128)S(1)}, f32[4,16,384]{2,1,0:T(8,128)S(1)}) fusion(f32[20,16,384]{2,1,0:T(8,128)} %copy-done.9), kind=kLoop, calls=%fused_computation.305 | loop fusion | bytes 589824 | tf_op jit(solution)/shard_map/slice | solution.py:35
  28.1 1.9 %fusion.47 = f32[40,16,384]{2,1,0:T(8,128)S(1)} fusion(f32[4,16,384]{2,1,0:T(8,128)S(1)} %get-tuple-element.41, f32[32,16,384]{2,1,0:T(8,128)} %bitcast.55, f32[4,16,384]{2,1,0:T(8,128)S(1)} %get-tuple-element.44, f32[40,16,384]{2,1,0:T(8,128)} %copy-done.4, f32[4,16,384]{2,1,0:T(8,128)S(1)} %get-tuple-element.40, f32[32,16,384]{2,1,0:T(8,128)} %param.17, ...), kind=kLoop, calls=%fused_computation.134 | loop fusion | flops 1966080 | bytes 4915200 | tf_op jit(solution)/shard_map/add | solution.py:138
  30.0 0.1 slice.580
  30.1 1.9 %fusion.115 = f32[32,16,384]{2,1,0:T(8,128)S(1)} fusion(f32[32,16,384]{2,1,0:T(8,128)S(1)} %slice.580, f32[40,16,384]{2,1,0:T(8,128)S(1)} %fusion.47), kind=kLoop, calls=%fused_computation.216 | loop fusion | flops 7274496 | bytes 7864320 | tf_op jit(solution)/shard_map/add | solution.py:56
  32.0 0.6 add.432
  33.2 0.1 add.435
  33.4 0.0 copy-start.6
  33.4 0.2 multiply_add_fusion
  33.6 0.0 copy-start.7
  33.6 0.9 copy-done.6
  34.5 1.4 %select_reduce_fusion = f32[1024]{0:T(1024)S(1)} fusion(f32[512,384]{1,0:T(8,128)S(1)} %bitcast.58, s32[1024]{0:T(1024)S(1)} %bitcast.64, s32[1024]{0:T(1024)S(1)} %bitcast.70), kind=kOutput, calls=%fused_computation.81 | convolution fusion | flops 1209662464 | bytes 798720 | tf_op jit(solution)/shard_map/dot_general | solution.py:83
  35.9 1.3 %select_reduce_fusion.1 = f32[1024]{0:T(1024)S(1)} fusion(f32[512,384]{1,0:T(8,128)S(1)} %bitcast.59, s32[1024]{0:T(1024)S(1)} %bitcast.65, s32[1024]{0:T(1024)S(1)} %bitcast.71), kind=kOutput, calls=%fused_computation.82 | convolution fusion | flops 1209662464 | bytes 798720 | tf_op jit(solution)/shard_map/dot_general | solution.py:83
  37.3 0.0 copy-start.10
  37.3 1.1 fusion.11
  38.5 1.3 %fusion = f32[512,384]{1,0:T(8,128)S(1)} fusion(bf16[1024,512]{1,0:T(8,128)(2,1)S(1)} %get-tuple-element.53, bf16[1024,512]{1,0:T(8,128)(2,1)S(1)} %get-tuple-element.54, pred[1024,384]{0,1:T(32,128)(4,1)S(1)} %copy-done.10), kind=kOutput, calls=%fused_computation.65 | convolution fusion | flops 811859968 | bytes 3276800 | tf_op jit(solution)/shard_map/dot_general | solution.py:93
  39.8 0.0 copy-done.8
  39.8 2.8 %fusion.87 = f32[32,16,384]{2,1,0:T(8,128)S(1)} fusion(f32[32,16,384]{2,1,0:T(8,128)S(1)} %copy-done.1, f32[32,16,384]{2,1,0:T(8,128)S(1)} %bitcast.61, f32[32,16,384]{2,1,0:T(8,128)S(1)} %bitcast.56, f32[4,16,384]{2,1,0:T(8,128)S(1)} %get-tuple-element.42, f32[4,16,384]{2,1,0:T(8,128)S(1)} %get-tuple-element.39, f32[1,32,16,384]{3,2,1,0:T(8,128)S(1)} %copy-done.8), kind=kLoop, calls=%fused_computation.188 | loop fusion | flops 9830400 | bytes 4128768 | tf_op jit(solution)/shard_map/add | solution.py:138
  42.6 2.4 %collective-permute-start.2 = (f32[4,16,384]{2,1,0:T(8,128)S(1)}, f32[4,16,384]{2,1,0:T(8,128)S(1)}, u32[]{:S(2)}, u32[]{:S(2)}) collective-permute-start(f32[4,16,384]{2,1,0:T(8,128)S(1)} %get-tuple-element.29), channel_id=1, source_target_pairs={{1,0},{2,1},{3,2},{4,3},{5,4},{6,5},{7,6},{8,7},{9,8},{10,9},{11,1... | collective-permute-start | bytes 294920 | tf_op jit(solution)/shard_map/ppermute | solution.py:20
  45.1 3.3 %collective-permute-start.3 = (f32[4,16,384]{2,1,0:T(8,128)S(1)}, f32[4,16,384]{2,1,0:T(8,128)S(1)}, u32[]{:S(2)}, u32[]{:S(2)}) collective-permute-start(f32[4,16,384]{2,1,0:T(8,128)S(1)} %get-tuple-element.30), channel_id=1, source_target_pairs={{0,1},{1,2},{2,3},{3,4},{4,5},{5,6},{6,7},{7,8},{8,9},{9,10},{10,1... | collective-permute-start | bytes 294920 | tf_op jit(solution)/shard_map/ppermute | solution.py:17
  48.4 1.3 %fusion.4 = f32[512,384]{1,0:T(8,128)S(1)} fusion(bf16[1024,512]{1,0:T(8,128)(2,1)S(1)} %get-tuple-element.52, bf16[1024,512]{1,0:T(8,128)(2,1)S(1)} %get-tuple-element.51, pred[1024,384]{0,1:T(32,128)(4,1)S(1)} %copy-done.10), kind=kOutput, calls=%fused_computation.69 | convolution fusion | flops 811859968 | bytes 3276800 | tf_op jit(solution)/shard_map/dot_general | solution.py:93
  49.7 0.1 collective-permute-done.3
  49.8 3.9 %add_bitcast_fusion = (f32[32,1,16,384]{3,2,1,0:T(8,128)S(1)}, f32[32,16,384]{2,1,0:T(8,128)}) fusion(f32[32,16,384]{2,1,0:T(8,128)S(1)} %fusion.87, f32[32,16,384]{2,1,0:T(8,128)S(1)} %multiply_add_fusion, f32[1,32,16,384]{3,2,1,0:T(8,128)S(1)} %copy-done.2, f32[1,32,16,384]{3,2,1,0:T(8,128)S(1)} %copy-done, f32[40,16,384]{2,1,0:T(8,128)S(1)} %fusion.47, ...), kind=kLoop, calls=%fused_computation.281 | loop fusion | flops 11599872 | bytes 8060928 | tf_op jit(solution)/shard_map/reshape | solution.py:101
  53.7 35.3 %all_to_all.10 = f32[32,1,16,384]{3,2,1,0:T(8,128)S(1)} all-to-all(f32[32,1,16,384]{3,2,1,0:T(8,128)S(1)} %get-tuple-element.27), channel_id=1, replica_groups=mesh['shot'=32,'dom'=16] {'shot'}, dimensions={0} | all-to-all | bytes 1572864 | tf_op jit(solution)/shard_map/all_to_all | solution.py:102
  89.0 0.1 reduce_sum.29
  89.1 0.1 broadcast_in_dim.13
  89.2 34.1 %all_to_all.11 = f32[32,1,16,384]{3,2,1,0:T(8,128)S(1)} all-to-all(f32[32,1,16,384]{3,2,1,0:T(8,128)S(1)} %broadcast_in_dim.13), channel_id=1, replica_groups=mesh['shot'=32,'dom'=16] {'shot'}, dimensions={0} | all-to-all | bytes 1572864 | tf_op jit(solution)/shard_map/all_to_all | solution.py:104
  123.2 0.9 copy.25
  (36 shorter events, 0.2 us)
Async XLA Ops:
  3.7 13.0 %copy-start.13 = (s32[1,1024]{1,0:T(1,128)S(1)}, s32[1,1024]{1,0:T(1,128)}, u32[]{:S(2)}) copy-start(s32[1,1024]{1,0:T(1,128)} %param.26) | copy-start | bytes 12292
  3.7 13.0 %copy-start.14 = (s32[1,1024]{1,0:T(1,128)S(1)}, s32[1,1024]{1,0:T(1,128)}, u32[]{:S(2)}) copy-start(s32[1,1024]{1,0:T(1,128)} %param.27) | copy-start | bytes 12292
  3.7 13.0 %copy-start.16 = (s32[3]{0:T(128)S(1)}, s32[3]{0:T(128)}, u32[]{:S(2)}) copy-start(s32[3]{0:T(128)} %constant.101.clone.1) | copy-start | bytes 40
  3.8 13.0 %copy-start.17 = (s32[3]{0:T(128)S(1)}, s32[3]{0:T(128)}, u32[]{:S(2)}) copy-start(s32[3]{0:T(128)} %constant.95.clone.1) | copy-start | bytes 40
  3.8 13.8 %copy-start.15 = (f32[1,2]{1,0:T(1,128)S(1)}, f32[1,2]{1,0:T(1,128)}, u32[]{:S(2)}) copy-start(f32[1,2]{1,0:T(1,128)} %param.25) | copy-start | bytes 28
  3.8 16.9 %copy-start.11 = (f32[1,2,1024]{2,1,0:T(2,128)S(1)}, f32[1,2,1024]{2,1,0:T(2,128)}, u32[]{:S(2)}) copy-start(f32[1,2,1024]{2,1,0:T(2,128)} %param.29) | copy-start | bytes 24580
  3.8 16.9 %copy-start.12 = (s32[1,1024]{1,0:T(1,128)S(1)}, s32[1,1024]{1,0:T(1,128)}, u32[]{:S(2)}) copy-start(s32[1,1024]{1,0:T(1,128)} %param.28) | copy-start | bytes 12292
  3.8 17.9 %copy-start = (f32[1,32,16,384]{3,2,1,0:T(8,128)S(1)}, f32[1,32,16,384]{3,2,1,0:T(8,128)}, u32[]{:S(2)}) copy-start(f32[1,32,16,384]{3,2,1,0:T(8,128)} %param.19) | copy-start | bytes 2359300
  3.9 17.8 %collective-permute-start.1 = (f32[20,16,384]{2,1,0:T(8,128)S(1)}, f32[20,16,384]{2,1,0:T(8,128)S(1)}, u32[]{:S(2)}, u32[]{:S(2)}) collective-permute-start(f32[20,16,384]{2,1,0:T(8,128)S(1)} %pad_maximum_fusion.6), channel_id=1, source_target_pairs={{1,0},{2,1},{3,2},{4,3},{5,4},{6,5},{7,6},{8,7},{9,8},{10,9},{11,1... | collective-permute-start | bytes 1474568 | tf_op jit(solution)/shard_map/ppermute | solution.py:32
  12.8 8.9 %collective-permute-start = (f32[20,16,384]{2,1,0:T(8,128)S(1)}, f32[20,16,384]{2,1,0:T(8,128)S(1)}, u32[]{:S(2)}, u32[]{:S(2)}) collective-permute-start(f32[20,16,384]{2,1,0:T(8,128)S(1)} %pad_maximum_fusion.5), channel_id=1, source_target_pairs={{0,1},{1,2},{2,3},{3,4},{4,5},{5,6},{6,7},{7,8},{8,9},{9,10},{10,1... | collective-permute-start | bytes 1474568 | tf_op jit(solution)/shard_map/ppermute | solution.py:31
  21.7 0.8 copy-start.9
  26.7 1.4 %copy-start.4 = (f32[40,16,384]{2,1,0:T(8,128)}, f32[40,16,384]{2,1,0:T(8,128)S(1)}, u32[]{:S(2)}) copy-start(f32[40,16,384]{2,1,0:T(8,128)S(1)} %add.406) | copy-start | bytes 2949124
  30.1 1.9 %copy-start.5 = (f32[32,16,384]{2,1,0:T(8,128)}, f32[32,16,384]{2,1,0:T(8,128)S(1)}, u32[]{:S(2)}) copy-start(f32[32,16,384]{2,1,0:T(8,128)S(1)} %slice.580) | copy-start | bytes 2359300
  30.1 3.3 %copy-start.1 = (f32[32,16,384]{2,1,0:T(8,128)S(1)}, f32[32,16,384]{2,1,0:T(8,128)}, u32[]{:S(2)}) copy-start(f32[32,16,384]{2,1,0:T(8,128)} %param.17) | copy-start | bytes 2359300
  33.4 1.1 copy-start.6
  33.6 16.2 %copy-start.7 = (f32[32,16,384]{2,1,0:T(8,128)}, f32[32,16,384]{2,1,0:T(8,128)S(1)}, u32[]{:S(2)}) copy-start(f32[32,16,384]{2,1,0:T(8,128)S(1)} %multiply_add_fusion) | copy-start | bytes 2359300
  37.3 1.2 copy-start.10
  38.5 1.3 %copy-start.3 = (f32[1,32,16,384]{3,2,1,0:T(8,128)S(1)}, f32[1,32,16,384]{3,2,1,0:T(8,128)}, u32[]{:S(2)}) copy-start(f32[1,32,16,384]{3,2,1,0:T(8,128)} %param.21) | copy-start | bytes 2359300
  38.5 1.4 %copy-start.8 = (f32[1,32,16,384]{3,2,1,0:T(8,128)S(1)}, f32[1,32,16,384]{3,2,1,0:T(8,128)}, u32[]{:S(2)}) copy-start(f32[1,32,16,384]{3,2,1,0:T(8,128)} %param.20) | copy-start | bytes 2359300
  42.6 7.1 %collective-permute-start.2 = (f32[4,16,384]{2,1,0:T(8,128)S(1)}, f32[4,16,384]{2,1,0:T(8,128)S(1)}, u32[]{:S(2)}, u32[]{:S(2)}) collective-permute-start(f32[4,16,384]{2,1,0:T(8,128)S(1)} %get-tuple-element.29), channel_id=1, source_target_pairs={{1,0},{2,1},{3,2},{4,3},{5,4},{6,5},{7,6},{8,7},{9,8},{10,9},{11,1... | collective-permute-start | bytes 294920 | tf_op jit(solution)/shard_map/ppermute | solution.py:20
  45.1 4.7 %collective-permute-start.3 = (f32[4,16,384]{2,1,0:T(8,128)S(1)}, f32[4,16,384]{2,1,0:T(8,128)S(1)}, u32[]{:S(2)}, u32[]{:S(2)}) collective-permute-start(f32[4,16,384]{2,1,0:T(8,128)S(1)} %get-tuple-element.30), channel_id=1, source_target_pairs={{0,1},{1,2},{2,3},{3,4},{4,5},{5,6},{6,7},{7,8},{8,9},{9,10},{10,1... | collective-permute-start | bytes 294920 | tf_op jit(solution)/shard_map/ppermute | solution.py:17
  48.4 1.4 %copy-start.2 = (f32[1,32,16,384]{3,2,1,0:T(8,128)S(1)}, f32[1,32,16,384]{3,2,1,0:T(8,128)}, u32[]{:S(2)}) copy-start(f32[1,32,16,384]{3,2,1,0:T(8,128)} %param.18) | copy-start | bytes 2359300

commit v11 on v6

--- a/solution.py
+++ b/solution.py
@@ -80,8 +80,11 @@
 
 def sample(field, rows, cols):
     width_x, width_y, width_z = field.shape
-    picked = jnp.dot(rows, field.reshape(width_x * width_y, width_z), precision=lax.Precision.HIGH)
-    return jnp.sum(picked * cols, axis=1)
+    along = lax.dot_general(
+        field.reshape(width_x * width_y, width_z), cols, (((1,), (1,)), ((), ())),
+        precision=lax.Precision.HIGH,
+    )
+    return jnp.sum(along * rows.T, axis=0)
 
 
 def receiver_grid(shape, rows, cols, values):

time: 126 us -> 126 us (level)
  matrix products: 8.07 us -> 6.61 us
    dot_general x2, matrix products: 5.37 us -> 3.68 us  [receiver_grid(): lax.dot_general(rows * values[:, None], cols, (((0,), (0,)), ((), ())), p...]
where the time goes in v11:
time: 126 us; the launch traced here: 125 us
  blocking collectives  70.4 us (56%)
  starting transfers between devices  17.1 us (14%)
  other arithmetic  14.5 us (12%)
  local copies, waits for them, and re-layouts  9.33 us (7%)
  between operations  6.84 us (5%)
  matrix products  6.61 us (5%)
    all_to_all x1, blocking collectives, shot_sum(): mine = jnp.sum(lax.all_to_all(pieces, 'shot', 0, 0, tiled=False), axis=0)  35.5 us
    all_to_all x1, blocking collectives, shot_sum(): return lax.all_to_all(spread, 'shot', 0, 0, tiled=False).reshape(term.shape)  34.9 us
    ppermute x1, starting transfers between devices, wide_halo(): highs = lax.ppermute(heads, 'dom', backward)  8.92 us
    add x3, other arithmetic, advance(): 2.0 * current[R:-R] - before + coef * (laplace_core(current) + sources)  4.92 us
    add x2, other arithmetic, laplace_core(): total + weight * (padded[:, R:R + width_y, R + offset:R + offset + width_...  4.69 us
    reshape x1, other arithmetic, shot_sum(): pieces = term.reshape((count, term.shape[0] // count) + term.shape[1:])  3.9 us
    ppermute x1, starting transfers between devices, with_halo(): lax.ppermute(lax.slice_in_dim(block, block.shape[dim] - width, None, axis...  3.86 us
    dot_general x2, matrix products, receiver_grid(): lax.dot_general(rows * values[:, None], cols, (((0,), (0,)), ((), ())), p...  3.68 us
  transfers between devices with their start and end apart: 4, of which 0 were waited for; matrix products, arithmetic and copies ran while one was open for 3% of the time, Pallas kernels for 0%

profile of v11, /device:TPU:1, one launch (start us, length us, event | category | flops | bytes accessed | tf_op | source)
XLA Modules:
  0.0 124.8 jit_solution(7110576053234873372)
XLA Ops:
  0.6 1.0 fusion.173
  1.6 1.1 slice_bitcast_fusion.1
  2.6 1.1 slice_bitcast_fusion.4
  3.7 0.0 copy-start.14
  3.7 0.0 copy-start.15
  3.7 0.0 copy-start.13
  3.8 0.0 copy-start.11
  3.8 0.0 copy-start.12
  3.8 0.0 copy-start.10
  3.8 0.0 copy-start
  3.8 8.9 %collective-permute-start.1 = (f32[20,16,384]{2,1,0:T(8,128)S(1)}, f32[20,16,384]{2,1,0:T(8,128)S(1)}, u32[]{:S(2)}, u32[]{:S(2)}) collective-permute-start(f32[20,16,384]{2,1,0:T(8,128)S(1)} %pad_maximum_fusion.6), channel_id=1, source_target_pairs={{1,0},{2,1},{3,2},{4,3},{5,4},{6,5},{7,6},{8,7},{9,8},{10,9},{11,1... | collective-permute-start | bytes 1474568 | tf_op jit(solution)/shard_map/ppermute | solution.py:32
  12.8 1.9 %collective-permute-start = (f32[20,16,384]{2,1,0:T(8,128)S(1)}, f32[20,16,384]{2,1,0:T(8,128)S(1)}, u32[]{:S(2)}, u32[]{:S(2)}) collective-permute-start(f32[20,16,384]{2,1,0:T(8,128)S(1)} %pad_maximum_fusion.5), channel_id=1, source_target_pairs={{0,1},{1,2},{2,3},{3,4},{4,5},{5,6},{6,7},{7,8},{8,9},{9,10},{10,1... | collective-permute-start | bytes 1474568 | tf_op jit(solution)/shard_map/ppermute | solution.py:31
  16.7 0.7 and_reduce_fusion
  17.5 0.7 fusion.177
  20.7 0.0 copy-start.9
  20.7 0.1 pad_maximum_fusion
  20.8 0.7 copy-done.9
  21.5 0.1 slice.569
  21.5 2.8 %fusion.22 = f32[40,16,384]{2,1,0:T(8,128)S(1)} fusion(f32[40,16,384]{2,1,0:T(8,128)S(1)} %slice.569, f32[48,16,384]{2,1,0:T(8,128)S(1)} %pad_maximum_fusion, f32[8,16,384]{2,1,0:T(8,128)S(1)} %slice.568, f32[32,16,384]{2,1,0:T(8,128)S(1)} %bitcast.54, f32[8,16,384]{2,1,0:T(8,128)S(1)} %slice.567), kind=kLoop, calls=%fused_computation.104 | loop fusion | flops 9584640 | bytes 9043968 | tf_op jit(solution)/shard_map/add | solution.py:56
  24.3 0.6 add.403
  25.6 0.1 add.406
  25.8 1.3 %fusion.175 = (f32[4,16,384]{2,1,0:T(8,128)S(1)}, f32[4,16,384]{2,1,0:T(8,128)S(1)}, f32[4,16,384]{2,1,0:T(8,128)S(1)}) fusion(f32[20,16,384]{2,1,0:T(8,128)} %copy-done.9), kind=kLoop, calls=%fused_computation.296 | loop fusion | bytes 589824 | tf_op jit(solution)/shard_map/slice | solution.py:35
  27.1 1.9 %fusion.41 = f32[40,16,384]{2,1,0:T(8,128)S(1)} fusion(f32[4,16,384]{2,1,0:T(8,128)S(1)} %get-tuple-element.41, f32[32,16,384]{2,1,0:T(8,128)} %bitcast.55, f32[4,16,384]{2,1,0:T(8,128)S(1)} %get-tuple-element.44, f32[40,16,384]{2,1,0:T(8,128)} %copy-done.4, f32[4,16,384]{2,1,0:T(8,128)S(1)} %get-tuple-element.40, f32[32,16,384]{2,1,0:T(8,128)} %param.17, ...), kind=kLoop, calls=%fused_computation.127 | loop fusion | flops 1966080 | bytes 4915200 | tf_op jit(solution)/shard_map/add | solution.py:136
  29.0 0.1 slice.580
  29.1 0.0 copy-start.5
  29.1 0.0 copy-start.1
  29.1 1.9 %fusion.109 = f32[32,16,384]{2,1,0:T(8,128)S(1)} fusion(f32[32,16,384]{2,1,0:T(8,128)S(1)} %slice.580, f32[40,16,384]{2,1,0:T(8,128)S(1)} %fusion.41), kind=kLoop, calls=%fused_computation.209 | loop fusion | flops 7274496 | bytes 7864320 | tf_op jit(solution)/shard_map/add | solution.py:56
  31.0 0.6 add.432
  32.3 0.1 add.435
  32.4 0.0 copy-start.6
  32.5 0.2 multiply_add_fusion
  32.7 0.0 copy-start.7
  32.7 0.9 copy-done.6
  33.6 1.5 %select_reduce_fusion = f32[1024]{0:T(1024)S(1)} fusion(f32[512,384]{1,0:T(8,128)S(1)} %bitcast.58, s32[1024]{0:T(1024)S(1)} %bitcast.66, s32[1024]{0:T(1024)S(1)} %bitcast.70), kind=kOutput, calls=%fused_computation.66 | convolution fusion | flops 1209924608 | bytes 798720 | tf_op jit(solution)/shard_map/dot_general | solution.py:83
  35.1 1.5 %select_reduce_fusion.1 = f32[1024]{0:T(1024)S(1)} fusion(f32[512,384]{1,0:T(8,128)S(1)} %bitcast.59, s32[1024]{0:T(1024)S(1)} %bitcast.67, s32[1024]{0:T(1024)S(1)} %bitcast.71), kind=kOutput, calls=%fused_computation.69 | convolution fusion | flops 1209924608 | bytes 798720 | tf_op jit(solution)/shard_map/dot_general | solution.py:83
  36.5 0.0 copy-start.3
  36.6 1.8 %fusion.2 = f32[512,384]{1,0:T(8,128)S(1)} fusion(f32[1024]{0:T(1024)S(1)} %sub.65, s32[1024]{0:T(1024)S(1)} %bitcast.68, s32[1024]{0:T(1024)S(1)} %bitcast.72), kind=kOutput, calls=%fused_computation.67 | convolution fusion | flops 1209401344 | bytes 798720 | tf_op jit(solution)/shard_map/dot_general | solution.py:91
  38.4 2.8 %fusion.81 = f32[32,16,384]{2,1,0:T(8,128)S(1)} fusion(f32[32,16,384]{2,1,0:T(8,128)S(1)} %copy-done.1, f32[32,16,384]{2,1,0:T(8,128)S(1)} %bitcast.61, f32[32,16,384]{2,1,0:T(8,128)S(1)} %bitcast.56, f32[4,16,384]{2,1,0:T(8,128)S(1)} %get-tuple-element.42, f32[4,16,384]{2,1,0:T(8,128)S(1)} %get-tuple-element.39, f32[1,32,16,384]{3,2,1,0:T(8,128)S(1)} %copy-done.8), kind=kLoop, calls=%fused_computation.181 | loop fusion | flops 9830400 | bytes 4128768 | tf_op jit(solution)/shard_map/add | solution.py:136
  41.3 2.4 %collective-permute-start.2 = (f32[4,16,384]{2,1,0:T(8,128)S(1)}, f32[4,16,384]{2,1,0:T(8,128)S(1)}, u32[]{:S(2)}, u32[]{:S(2)}) collective-permute-start(f32[4,16,384]{2,1,0:T(8,128)S(1)} %get-tuple-element.29), channel_id=1, source_target_pairs={{1,0},{2,1},{3,2},{4,3},{5,4},{6,5},{7,6},{8,7},{9,8},{10,9},{11,1... | collective-permute-start | bytes 294920 | tf_op jit(solution)/shard_map/ppermute | solution.py:20
  43.7 3.9 %collective-permute-start.3 = (f32[4,16,384]{2,1,0:T(8,128)S(1)}, f32[4,16,384]{2,1,0:T(8,128)S(1)}, u32[]{:S(2)}, u32[]{:S(2)}) collective-permute-start(f32[4,16,384]{2,1,0:T(8,128)S(1)} %get-tuple-element.30), channel_id=1, source_target_pairs={{0,1},{1,2},{2,3},{3,4},{4,5},{5,6},{6,7},{7,8},{8,9},{9,10},{10,1... | collective-permute-start | bytes 294920 | tf_op jit(solution)/shard_map/ppermute | solution.py:17
  47.6 0.0 copy-start.2
  47.6 1.8 %fusion = f32[512,384]{1,0:T(8,128)S(1)} fusion(f32[1024]{0:T(1024)S(1)} %sub.67, s32[1024]{0:T(1024)S(1)} %bitcast.69, s32[1024]{0:T(1024)S(1)} %bitcast.73), kind=kOutput, calls=%fused_computation.64 | convolution fusion | flops 1209401344 | bytes 798720 | tf_op jit(solution)/shard_map/dot_general | solution.py:91
  49.5 3.9 %add_bitcast_fusion = (f32[32,1,16,384]{3,2,1,0:T(8,128)S(1)}, f32[32,16,384]{2,1,0:T(8,128)}) fusion(f32[32,16,384]{2,1,0:T(8,128)S(1)} %fusion.81, f32[32,16,384]{2,1,0:T(8,128)S(1)} %multiply_add_fusion, f32[1,32,16,384]{3,2,1,0:T(8,128)S(1)} %copy-done.2, f32[1,32,16,384]{3,2,1,0:T(8,128)S(1)} %copy-done, f32[40,16,384]{2,1,0:T(8,128)S(1)} %fusion.41, ...), kind=kLoop, calls=%fused_computation.274 | loop fusion | flops 11599872 | bytes 8060928 | tf_op jit(solution)/shard_map/reshape | solution.py:99
  53.4 35.5 %all_to_all.10 = f32[32,1,16,384]{3,2,1,0:T(8,128)S(1)} all-to-all(f32[32,1,16,384]{3,2,1,0:T(8,128)S(1)} %get-tuple-element.27), channel_id=1, replica_groups=mesh['shot'=32,'dom'=16] {'shot'}, dimensions={0} | all-to-all | bytes 1572864 | tf_op jit(solution)/shard_map/all_to_all | solution.py:100
  88.9 0.1 reduce_sum.29
  89.0 0.1 broadcast_in_dim.13
  89.0 34.9 %all_to_all.11 = f32[32,1,16,384]{3,2,1,0:T(8,128)S(1)} all-to-all(f32[32,1,16,384]{3,2,1,0:T(8,128)S(1)} %broadcast_in_dim.13), channel_id=1, replica_groups=mesh['shot'=32,'dom'=16] {'shot'}, dimensions={0} | all-to-all | bytes 1572864 | tf_op jit(solution)/shard_map/all_to_all | solution.py:102
  123.9 0.9 copy.22
  (32 shorter events, 0.2 us)
Async XLA Ops:
  3.7 13.0 %copy-start.14 = (s32[3]{0:T(128)S(1)}, s32[3]{0:T(128)}, u32[]{:S(2)}) copy-start(s32[3]{0:T(128)} %constant.103.clone.1) | copy-start | bytes 40
  3.7 13.0 %copy-start.15 = (s32[3]{0:T(128)S(1)}, s32[3]{0:T(128)}, u32[]{:S(2)}) copy-start(s32[3]{0:T(128)} %constant.97.clone.1) | copy-start | bytes 40
  3.7 13.7 %copy-start.13 = (f32[1,2]{1,0:T(1,128)S(1)}, f32[1,2]{1,0:T(1,128)}, u32[]{:S(2)}) copy-start(f32[1,2]{1,0:T(1,128)} %param.25) | copy-start | bytes 28
  3.8 16.8 %copy-start.11 = (s32[1,1024]{1,0:T(1,128)S(1)}, s32[1,1024]{1,0:T(1,128)}, u32[]{:S(2)}) copy-start(s32[1,1024]{1,0:T(1,128)} %param.26) | copy-start | bytes 12292
  3.8 16.8 %copy-start.12 = (s32[1,1024]{1,0:T(1,128)S(1)}, s32[1,1024]{1,0:T(1,128)}, u32[]{:S(2)}) copy-start(s32[1,1024]{1,0:T(1,128)} %param.27) | copy-start | bytes 12292
  3.8 16.8 %copy-start.10 = (f32[1,2,1024]{2,1,0:T(2,128)S(1)}, f32[1,2,1024]{2,1,0:T(2,128)}, u32[]{:S(2)}) copy-start(f32[1,2,1024]{2,1,0:T(2,128)} %param.29) | copy-start | bytes 24580
  3.8 16.9 %copy-start = (f32[1,32,16,384]{3,2,1,0:T(8,128)S(1)}, f32[1,32,16,384]{3,2,1,0:T(8,128)}, u32[]{:S(2)}) copy-start(f32[1,32,16,384]{3,2,1,0:T(8,128)} %param.19) | copy-start | bytes 2359300
  3.8 16.8 %collective-permute-start.1 = (f32[20,16,384]{2,1,0:T(8,128)S(1)}, f32[20,16,384]{2,1,0:T(8,128)S(1)}, u32[]{:S(2)}, u32[]{:S(2)}) collective-permute-start(f32[20,16,384]{2,1,0:T(8,128)S(1)} %pad_maximum_fusion.6), channel_id=1, source_target_pairs={{1,0},{2,1},{3,2},{4,3},{5,4},{6,5},{7,6},{8,7},{9,8},{10,9},{11,1... | collective-permute-start | bytes 1474568 | tf_op jit(solution)/shard_map/ppermute | solution.py:32
  12.8 7.9 %collective-permute-start = (f32[20,16,384]{2,1,0:T(8,128)S(1)}, f32[20,16,384]{2,1,0:T(8,128)S(1)}, u32[]{:S(2)}, u32[]{:S(2)}) collective-permute-start(f32[20,16,384]{2,1,0:T(8,128)S(1)} %pad_maximum_fusion.5), channel_id=1, source_target_pairs={{0,1},{1,2},{2,3},{3,4},{4,5},{5,6},{6,7},{7,8},{8,9},{9,10},{10,1... | collective-permute-start | bytes 1474568 | tf_op jit(solution)/shard_map/ppermute | solution.py:31
  20.7 0.8 copy-start.9
  25.7 1.4 %copy-start.4 = (f32[40,16,384]{2,1,0:T(8,128)}, f32[40,16,384]{2,1,0:T(8,128)S(1)}, u32[]{:S(2)}) copy-start(f32[40,16,384]{2,1,0:T(8,128)S(1)} %add.406) | copy-start | bytes 2949124
  29.1 1.9 %copy-start.5 = (f32[32,16,384]{2,1,0:T(8,128)}, f32[32,16,384]{2,1,0:T(8,128)S(1)}, u32[]{:S(2)}) copy-start(f32[32,16,384]{2,1,0:T(8,128)S(1)} %slice.580) | copy-start | bytes 2359300
  29.1 3.3 %copy-start.1 = (f32[32,16,384]{2,1,0:T(8,128)S(1)}, f32[32,16,384]{2,1,0:T(8,128)}, u32[]{:S(2)}) copy-start(f32[32,16,384]{2,1,0:T(8,128)} %param.17) | copy-start | bytes 2359300
  32.4 1.1 copy-start.6
  32.5 1.1 copy-start.16
  32.7 16.8 %copy-start.7 = (f32[32,16,384]{2,1,0:T(8,128)}, f32[32,16,384]{2,1,0:T(8,128)S(1)}, u32[]{:S(2)}) copy-start(f32[32,16,384]{2,1,0:T(8,128)S(1)} %multiply_add_fusion) | copy-start | bytes 2359300
  36.5 1.9 %copy-start.3 = (f32[1,32,16,384]{3,2,1,0:T(8,128)S(1)}, f32[1,32,16,384]{3,2,1,0:T(8,128)}, u32[]{:S(2)}) copy-start(f32[1,32,16,384]{3,2,1,0:T(8,128)} %param.21) | copy-start | bytes 2359300
  36.5 1.9 %copy-start.8 = (f32[1,32,16,384]{3,2,1,0:T(8,128)S(1)}, f32[1,32,16,384]{3,2,1,0:T(8,128)}, u32[]{:S(2)}) copy-start(f32[1,32,16,384]{3,2,1,0:T(8,128)} %param.20) | copy-start | bytes 2359300
  41.3 8.2 %collective-permute-start.2 = (f32[4,16,384]{2,1,0:T(8,128)S(1)}, f32[4,16,384]{2,1,0:T(8,128)S(1)}, u32[]{:S(2)}, u32[]{:S(2)}) collective-permute-start(f32[4,16,384]{2,1,0:T(8,128)S(1)} %get-tuple-element.29), channel_id=1, source_target_pairs={{1,0},{2,1},{3,2},{4,3},{5,4},{6,5},{7,6},{8,7},{9,8},{10,9},{11,1... | collective-permute-start | bytes 294920 | tf_op jit(solution)/shard_map/ppermute | solution.py:20
  43.7 5.8 %collective-permute-start.3 = (f32[4,16,384]{2,1,0:T(8,128)S(1)}, f32[4,16,384]{2,1,0:T(8,128)S(1)}, u32[]{:S(2)}, u32[]{:S(2)}) collective-permute-start(f32[4,16,384]{2,1,0:T(8,128)S(1)} %get-tuple-element.30), channel_id=1, source_target_pairs={{0,1},{1,2},{2,3},{3,4},{4,5},{5,6},{6,7},{7,8},{8,9},{9,10},{10,1... | collective-permute-start | bytes 294920 | tf_op jit(solution)/shard_map/ppermute | solution.py:17
  47.6 1.9 %copy-start.2 = (f32[1,32,16,384]{3,2,1,0:T(8,128)S(1)}, f32[1,32,16,384]{3,2,1,0:T(8,128)}, u32[]{:S(2)}) copy-start(f32[1,32,16,384]{3,2,1,0:T(8,128)} %param.18) | copy-start | bytes 2359300

commit v12 on v11

--- a/solution.py
+++ b/solution.py
@@ -73,7 +73,7 @@
     inside = (xcells >= start) & (xcells < start + width_x)
     row = jnp.where(inside, (xcells - start) * width_y + ycells, -1)
     count = xcells.shape[0]
-    rows = (row[:, None] == lax.broadcasted_iota(jnp.int32, (count, width_x * width_y), 1)).astype(jnp.float32)
+    rows = (row[None, :] == lax.broadcasted_iota(jnp.int32, (width_x * width_y, count), 0)).astype(jnp.float32)
     cols = (zcells[:, None] == lax.broadcasted_iota(jnp.int32, (count, width_z), 1)).astype(jnp.float32)
     return rows, cols
 
@@ -84,12 +84,12 @@
         field.reshape(width_x * width_y, width_z), cols, (((1,), (1,)), ((), ())),
         precision=lax.Precision.HIGH,
     )
-    return jnp.sum(along * rows.T, axis=0)
+    return jnp.sum(along * rows, axis=0)
 
 
 def receiver_grid(shape, rows, cols, values):
     placed = lax.dot_general(
-        rows * values[:, None], cols, (((0,), (0,)), ((), ())), precision=lax.Precision.HIGH
+        rows * values[None, :], cols, (((1,), (0,)), ((), ())), precision=lax.Precision.HIGH
     )
     return placed.reshape(shape)
 

time: 126 us -> 126 us (level)
  transfers between devices with their start and end apart: 4 -> 4, of which waited for: 0 -> 0; matrix products, arithmetic and copies ran while one was open for 3% -> 2% of each run, Pallas kernels for 0% -> 0%
where the time goes in v12:
time: 126 us; the launch traced here: 125 us
  blocking collectives  71.4 us (57%)
  starting transfers between devices  17.1 us (14%)
  other arithmetic  14.5 us (12%)
  local copies, waits for them, and re-layouts  9.33 us (7%)
  between operations  6.84 us (5%)
  matrix products  5.78 us (5%)
    all_to_all x1, blocking collectives, shot_sum(): return lax.all_to_all(spread, 'shot', 0, 0, tiled=False).reshape(term.shape)  35.8 us
    all_to_all x1, blocking collectives, shot_sum(): mine = jnp.sum(lax.all_to_all(pieces, 'shot', 0, 0, tiled=False), axis=0)  35.5 us
    ppermute x1, starting transfers between devices, wide_halo(): highs = lax.ppermute(heads, 'dom', backward)  8.92 us
    add x3, other arithmetic, advance(): 2.0 * current[R:-R] - before + coef * (laplace_core(current) + sources)  4.92 us
    add x2, other arithmetic, laplace_core(): total + weight * (padded[:, R:R + width_y, R + offset:R + offset + width_...  4.69 us
    reshape x1, other arithmetic, shot_sum(): pieces = term.reshape((count, term.shape[0] // count) + term.shape[1:])  3.9 us
    ppermute x1, starting transfers between devices, with_halo(): lax.ppermute(lax.slice_in_dim(block, block.shape[dim] - width, None, axis...  3.86 us
    slice x3, local copies, waits for them, and re-layouts, wide_halo(): f[f.shape[0] - w:]  3.08 us
  transfers between devices with their start and end apart: 4, of which 0 were waited for; matrix products, arithmetic and copies ran while one was open for 2% of the time, Pallas kernels for 0%

profile of v12, /device:TPU:1, one launch (start us, length us, event | category | flops | bytes accessed | tf_op | source)
XLA Modules:
  0.0 124.9 jit_solution(7855534555873062462)
XLA Ops:
  0.6 1.0 fusion.173
  1.6 1.1 slice_bitcast_fusion.1
  2.6 1.1 slice_bitcast_fusion.4
  3.7 0.0 copy-start.14
  3.7 0.0 copy-start.15
  3.7 0.0 copy-start.13
  3.8 0.0 copy-start.11
  3.8 0.0 copy-start.12
  3.8 0.0 copy-start.10
  3.8 0.0 copy-start
  3.8 8.9 %collective-permute-start.1 = (f32[20,16,384]{2,1,0:T(8,128)S(1)}, f32[20,16,384]{2,1,0:T(8,128)S(1)}, u32[]{:S(2)}, u32[]{:S(2)}) collective-permute-start(f32[20,16,384]{2,1,0:T(8,128)S(1)} %pad_maximum_fusion.6), channel_id=1, source_target_pairs={{1,0},{2,1},{3,2},{4,3},{5,4},{6,5},{7,6},{8,7},{9,8},{10,9},{11,1... | collective-permute-start | bytes 1474568 | tf_op jit(solution)/shard_map/ppermute | solution.py:32
  12.8 1.9 %collective-permute-start = (f32[20,16,384]{2,1,0:T(8,128)S(1)}, f32[20,16,384]{2,1,0:T(8,128)S(1)}, u32[]{:S(2)}, u32[]{:S(2)}) collective-permute-start(f32[20,16,384]{2,1,0:T(8,128)S(1)} %pad_maximum_fusion.5), channel_id=1, source_target_pairs={{0,1},{1,2},{2,3},{3,4},{4,5},{5,6},{6,7},{7,8},{8,9},{9,10},{10,1... | collective-permute-start | bytes 1474568 | tf_op jit(solution)/shard_map/ppermute | solution.py:31
  16.7 0.7 and_reduce_fusion
  17.5 0.7 fusion.177
  20.7 0.0 copy-start.9
  20.7 0.1 pad_maximum_fusion
  20.8 0.7 copy-done.9
  21.5 0.1 slice.569
  21.5 2.8 %fusion.22 = f32[40,16,384]{2,1,0:T(8,128)S(1)} fusion(f32[40,16,384]{2,1,0:T(8,128)S(1)} %slice.569, f32[48,16,384]{2,1,0:T(8,128)S(1)} %pad_maximum_fusion, f32[8,16,384]{2,1,0:T(8,128)S(1)} %slice.568, f32[32,16,384]{2,1,0:T(8,128)S(1)} %bitcast.54, f32[8,16,384]{2,1,0:T(8,128)S(1)} %slice.567), kind=kLoop, calls=%fused_computation.103 | loop fusion | flops 9584640 | bytes 9043968 | tf_op jit(solution)/shard_map/add | solution.py:56
  24.3 0.6 add.399
  25.6 0.1 add.402
  25.8 1.3 %fusion.175 = (f32[4,16,384]{2,1,0:T(8,128)S(1)}, f32[4,16,384]{2,1,0:T(8,128)S(1)}, f32[4,16,384]{2,1,0:T(8,128)S(1)}) fusion(f32[20,16,384]{2,1,0:T(8,128)} %copy-done.9), kind=kLoop, calls=%fused_computation.295 | loop fusion | bytes 589824 | tf_op jit(solution)/shard_map/slice | solution.py:35
  27.1 1.9 %fusion.41 = f32[40,16,384]{2,1,0:T(8,128)S(1)} fusion(f32[4,16,384]{2,1,0:T(8,128)S(1)} %get-tuple-element.41, f32[32,16,384]{2,1,0:T(8,128)} %bitcast.55, f32[4,16,384]{2,1,0:T(8,128)S(1)} %get-tuple-element.44, f32[40,16,384]{2,1,0:T(8,128)} %copy-done.4, f32[4,16,384]{2,1,0:T(8,128)S(1)} %get-tuple-element.40, f32[32,16,384]{2,1,0:T(8,128)} %param.17, ...), kind=kLoop, calls=%fused_computation.126 | loop fusion | flops 1966080 | bytes 4915200 | tf_op jit(solution)/shard_map/add | solution.py:136
  29.0 0.1 slice.580
  29.1 0.0 copy-start.5
  29.1 0.0 copy-start.1
  29.1 1.9 %fusion.109 = f32[32,16,384]{2,1,0:T(8,128)S(1)} fusion(f32[32,16,384]{2,1,0:T(8,128)S(1)} %slice.580, f32[40,16,384]{2,1,0:T(8,128)S(1)} %fusion.41), kind=kLoop, calls=%fused_computation.208 | loop fusion | flops 7274496 | bytes 7864320 | tf_op jit(solution)/shard_map/add | solution.py:56
  31.0 0.6 add.428
  32.3 0.1 add.431
  32.4 0.0 copy-start.6
  32.5 0.2 multiply_add_fusion
  32.7 0.0 copy-start.7
  32.7 0.9 copy-done.6
  33.6 1.5 %select_reduce_fusion = f32[1024]{0:T(1024)S(1)} fusion(f32[512,384]{1,0:T(8,128)S(1)} %bitcast.58, s32[1024]{0:T(1024)S(1)} %bitcast.66, s32[1024]{0:T(1024)S(1)} %bitcast.70), kind=kOutput, calls=%fused_computation.66 | convolution fusion | flops 1209924608 | bytes 798720 | tf_op jit(solution)/shard_map/dot_general | solution.py:83
  35.1 1.5 %select_reduce_fusion.1 = f32[1024]{0:T(1024)S(1)} fusion(f32[512,384]{1,0:T(8,128)S(1)} %bitcast.59, s32[1024]{0:T(1024)S(1)} %bitcast.67, s32[1024]{0:T(1024)S(1)} %bitcast.71), kind=kOutput, calls=%fused_computation.69 | convolution fusion | flops 1209924608 | bytes 798720 | tf_op jit(solution)/shard_map/dot_general | solution.py:83
  36.5 0.0 copy-start.3
  36.5 0.0 copy-start.8
  36.6 1.4 %fusion.2 = f32[512,384]{1,0:T(8,128)S(1)} fusion(f32[1024]{0:T(1024)S(1)} %sub.61, s32[1024]{0:T(1024)S(1)} %bitcast.68, s32[1024]{0:T(1024)S(1)} %bitcast.72), kind=kOutput, calls=%fused_computation.67 | convolution fusion | flops 1209401344 | bytes 798720 | tf_op jit(solution)/shard_map/dot_general | solution.py:91
  38.0 2.8 %fusion.81 = f32[32,16,384]{2,1,0:T(8,128)S(1)} fusion(f32[32,16,384]{2,1,0:T(8,128)S(1)} %copy-done.1, f32[32,16,384]{2,1,0:T(8,128)S(1)} %bitcast.61, f32[32,16,384]{2,1,0:T(8,128)S(1)} %bitcast.56, f32[4,16,384]{2,1,0:T(8,128)S(1)} %get-tuple-element.42, f32[4,16,384]{2,1,0:T(8,128)S(1)} %get-tuple-element.39, f32[1,32,16,384]{3,2,1,0:T(8,128)S(1)} %copy-done.8), kind=kLoop, calls=%fused_computation.180 | loop fusion | flops 9830400 | bytes 4128768 | tf_op jit(solution)/shard_map/add | solution.py:136
  40.9 2.4 %collective-permute-start.2 = (f32[4,16,384]{2,1,0:T(8,128)S(1)}, f32[4,16,384]{2,1,0:T(8,128)S(1)}, u32[]{:S(2)}, u32[]{:S(2)}) collective-permute-start(f32[4,16,384]{2,1,0:T(8,128)S(1)} %get-tuple-element.29), channel_id=1, source_target_pairs={{1,0},{2,1},{3,2},{4,3},{5,4},{6,5},{7,6},{8,7},{9,8},{10,9},{11,1... | collective-permute-start | bytes 294920 | tf_op jit(solution)/shard_map/ppermute | solution.py:20
  43.3 3.9 %collective-permute-start.3 = (f32[4,16,384]{2,1,0:T(8,128)S(1)}, f32[4,16,384]{2,1,0:T(8,128)S(1)}, u32[]{:S(2)}, u32[]{:S(2)}) collective-permute-start(f32[4,16,384]{2,1,0:T(8,128)S(1)} %get-tuple-element.30), channel_id=1, source_target_pairs={{0,1},{1,2},{2,3},{3,4},{4,5},{5,6},{6,7},{7,8},{8,9},{9,10},{10,1... | collective-permute-start | bytes 294920 | tf_op jit(solution)/shard_map/ppermute | solution.py:17
  47.2 1.4 %fusion = f32[512,384]{1,0:T(8,128)S(1)} fusion(f32[1024]{0:T(1024)S(1)} %sub.63, s32[1024]{0:T(1024)S(1)} %bitcast.69, s32[1024]{0:T(1024)S(1)} %bitcast.73), kind=kOutput, calls=%fused_computation.64 | convolution fusion | flops 1209401344 | bytes 798720 | tf_op jit(solution)/shard_map/dot_general | solution.py:91
  48.7 3.9 %add_bitcast_fusion = (f32[32,1,16,384]{3,2,1,0:T(8,128)S(1)}, f32[32,16,384]{2,1,0:T(8,128)}) fusion(f32[32,16,384]{2,1,0:T(8,128)S(1)} %fusion.81, f32[32,16,384]{2,1,0:T(8,128)S(1)} %multiply_add_fusion, f32[1,32,16,384]{3,2,1,0:T(8,128)S(1)} %copy-done.2, f32[1,32,16,384]{3,2,1,0:T(8,128)S(1)} %copy-done, f32[40,16,384]{2,1,0:T(8,128)S(1)} %fusion.41, ...), kind=kLoop, calls=%fused_computation.273 | loop fusion | flops 11599872 | bytes 8060928 | tf_op jit(solution)/shard_map/reshape | solution.py:99
  52.6 35.5 %all_to_all.10 = f32[32,1,16,384]{3,2,1,0:T(8,128)S(1)} all-to-all(f32[32,1,16,384]{3,2,1,0:T(8,128)S(1)} %get-tuple-element.27), channel_id=1, replica_groups=mesh['shot'=32,'dom'=16] {'shot'}, dimensions={0} | all-to-all | bytes 1572864 | tf_op jit(solution)/shard_map/all_to_all | solution.py:100
  88.1 0.1 reduce_sum.29
  88.1 0.1 broadcast_in_dim.13
  88.2 35.8 %all_to_all.11 = f32[32,1,16,384]{3,2,1,0:T(8,128)S(1)} all-to-all(f32[32,1,16,384]{3,2,1,0:T(8,128)S(1)} %broadcast_in_dim.13), channel_id=1, replica_groups=mesh['shot'=32,'dom'=16] {'shot'}, dimensions={0} | all-to-all | bytes 1572864 | tf_op jit(solution)/shard_map/all_to_all | solution.py:102
  124.0 0.9 copy.22
  (32 shorter events, 0.2 us)
Async XLA Ops:
  3.7 13.0 %copy-start.14 = (s32[3]{0:T(128)S(1)}, s32[3]{0:T(128)}, u32[]{:S(2)}) copy-start(s32[3]{0:T(128)} %constant.103.clone.1) | copy-start | bytes 40
  3.7 13.0 %copy-start.15 = (s32[3]{0:T(128)S(1)}, s32[3]{0:T(128)}, u32[]{:S(2)}) copy-start(s32[3]{0:T(128)} %constant.97.clone.1) | copy-start | bytes 40
  3.7 13.7 %copy-start.13 = (f32[1,2]{1,0:T(1,128)S(1)}, f32[1,2]{1,0:T(1,128)}, u32[]{:S(2)}) copy-start(f32[1,2]{1,0:T(1,128)} %param.25) | copy-start | bytes 28
  3.8 16.8 %copy-start.11 = (s32[1,1024]{1,0:T(1,128)S(1)}, s32[1,1024]{1,0:T(1,128)}, u32[]{:S(2)}) copy-start(s32[1,1024]{1,0:T(1,128)} %param.26) | copy-start | bytes 12292
  3.8 16.8 %copy-start.12 = (s32[1,1024]{1,0:T(1,128)S(1)}, s32[1,1024]{1,0:T(1,128)}, u32[]{:S(2)}) copy-start(s32[1,1024]{1,0:T(1,128)} %param.27) | copy-start | bytes 12292
  3.8 16.8 %copy-start.10 = (f32[1,2,1024]{2,1,0:T(2,128)S(1)}, f32[1,2,1024]{2,1,0:T(2,128)}, u32[]{:S(2)}) copy-start(f32[1,2,1024]{2,1,0:T(2,128)} %param.29) | copy-start | bytes 24580
  3.8 16.9 %copy-start = (f32[1,32,16,384]{3,2,1,0:T(8,128)S(1)}, f32[1,32,16,384]{3,2,1,0:T(8,128)}, u32[]{:S(2)}) copy-start(f32[1,32,16,384]{3,2,1,0:T(8,128)} %param.19) | copy-start | bytes 2359300
  3.8 16.8 %collective-permute-start.1 = (f32[20,16,384]{2,1,0:T(8,128)S(1)}, f32[20,16,384]{2,1,0:T(8,128)S(1)}, u32[]{:S(2)}, u32[]{:S(2)}) collective-permute-start(f32[20,16,384]{2,1,0:T(8,128)S(1)} %pad_maximum_fusion.6), channel_id=1, source_target_pairs={{1,0},{2,1},{3,2},{4,3},{5,4},{6,5},{7,6},{8,7},{9,8},{10,9},{11,1... | collective-permute-start | bytes 1474568 | tf_op jit(solution)/shard_map/ppermute | solution.py:32
  12.8 7.9 %collective-permute-start = (f32[20,16,384]{2,1,0:T(8,128)S(1)}, f32[20,16,384]{2,1,0:T(8,128)S(1)}, u32[]{:S(2)}, u32[]{:S(2)}) collective-permute-start(f32[20,16,384]{2,1,0:T(8,128)S(1)} %pad_maximum_fusion.5), channel_id=1, source_target_pairs={{0,1},{1,2},{2,3},{3,4},{4,5},{5,6},{6,7},{7,8},{8,9},{9,10},{10,1... | collective-permute-start | bytes 1474568 | tf_op jit(solution)/shard_map/ppermute | solution.py:31
  20.7 0.8 copy-start.9
  25.7 1.4 %copy-start.4 = (f32[40,16,384]{2,1,0:T(8,128)}, f32[40,16,384]{2,1,0:T(8,128)S(1)}, u32[]{:S(2)}) copy-start(f32[40,16,384]{2,1,0:T(8,128)S(1)} %add.402) | copy-start | bytes 2949124
  29.1 1.9 %copy-start.5 = (f32[32,16,384]{2,1,0:T(8,128)}, f32[32,16,384]{2,1,0:T(8,128)S(1)}, u32[]{:S(2)}) copy-start(f32[32,16,384]{2,1,0:T(8,128)S(1)} %slice.580) | copy-start | bytes 2359300
  29.1 3.3 %copy-start.1 = (f32[32,16,384]{2,1,0:T(8,128)S(1)}, f32[32,16,384]{2,1,0:T(8,128)}, u32[]{:S(2)}) copy-start(f32[32,16,384]{2,1,0:T(8,128)} %param.17) | copy-start | bytes 2359300
  32.4 1.1 copy-start.6
  32.5 1.1 copy-start.16
  32.7 16.0 %copy-start.7 = (f32[32,16,384]{2,1,0:T(8,128)}, f32[32,16,384]{2,1,0:T(8,128)S(1)}, u32[]{:S(2)}) copy-start(f32[32,16,384]{2,1,0:T(8,128)S(1)} %multiply_add_fusion) | copy-start | bytes 2359300
  36.5 1.5 %copy-start.3 = (f32[1,32,16,384]{3,2,1,0:T(8,128)S(1)}, f32[1,32,16,384]{3,2,1,0:T(8,128)}, u32[]{:S(2)}) copy-start(f32[1,32,16,384]{3,2,1,0:T(8,128)} %param.21) | copy-start | bytes 2359300
  36.5 1.5 %copy-start.8 = (f32[1,32,16,384]{3,2,1,0:T(8,128)S(1)}, f32[1,32,16,384]{3,2,1,0:T(8,128)}, u32[]{:S(2)}) copy-start(f32[1,32,16,384]{3,2,1,0:T(8,128)} %param.20) | copy-start | bytes 2359300
  40.9 7.8 %collective-permute-start.2 = (f32[4,16,384]{2,1,0:T(8,128)S(1)}, f32[4,16,384]{2,1,0:T(8,128)S(1)}, u32[]{:S(2)}, u32[]{:S(2)}) collective-permute-start(f32[4,16,384]{2,1,0:T(8,128)S(1)} %get-tuple-element.29), channel_id=1, source_target_pairs={{1,0},{2,1},{3,2},{4,3},{5,4},{6,5},{7,6},{8,7},{9,8},{10,9},{11,1... | collective-permute-start | bytes 294920 | tf_op jit(solution)/shard_map/ppermute | solution.py:20
  43.3 5.3 %collective-permute-start.3 = (f32[4,16,384]{2,1,0:T(8,128)S(1)}, f32[4,16,384]{2,1,0:T(8,128)S(1)}, u32[]{:S(2)}, u32[]{:S(2)}) collective-permute-start(f32[4,16,384]{2,1,0:T(8,128)S(1)} %get-tuple-element.30), channel_id=1, source_target_pairs={{0,1},{1,2},{2,3},{3,4},{4,5},{5,6},{6,7},{7,8},{8,9},{9,10},{10,1... | collective-permute-start | bytes 294920 | tf_op jit(solution)/shard_map/ppermute | solution.py:17
  47.2 1.5 %copy-start.2 = (f32[1,32,16,384]{3,2,1,0:T(8,128)S(1)}, f32[1,32,16,384]{3,2,1,0:T(8,128)}, u32[]{:S(2)}) copy-start(f32[1,32,16,384]{3,2,1,0:T(8,128)} %param.18) | copy-start | bytes 2359300
